TPU v7x, 128 devices: a whole 4x4x4 slice. The times are simulated.
128 devices in a mesh: outer: 16 (over z, x), inner: 8 (over y, core).
Axes of the slice: x: 4, y: 4, z: 4, core: 2. Of those that a mesh axis runs over, the one named last changes fastest.
Arguments:
- features: bfloat16 [4194304, 64], P(('outer', 'inner')), may hold values from -6 to 6
- block_offset: int32 [32768], P(('outer', 'inner')), may hold values from 0 to 7
- parent_entry: int32 [4194304], P(('outer', 'inner')), may hold values from 0 to 8191, as said below
- owner_cell: int32 [128, 8192], P(('outer', 'inner')), may hold values from 0 to 4096, as said below
- w_down: bfloat16 [8, 64, 128], replicated, may hold values from -0.25 to 0.25
- b_down: float32 [128], replicated, may hold values from -3 to 3
- w_up: bfloat16 [8, 128, 64], replicated, may hold values from -0.5 to 0.5
Outputs:
- refined: bfloat16 [4194304, 64], P(('outer', 'inner'))
Inputs may be any that keep to these rules, and one draw needn't show every extreme that they name: `parent_entry`: In each group the first c slots are used (1 <= c <= 512), the rest empty; group 7 and one more group have all 512 slots used on every device. A voxel names a used entry of its own device; all voxels of one brick of 128 name entries of one aligned window of 128 entries (entries k * 128 to k * 128 + 127), lying in one group or among the device's own entries, and every neighbour group is named by some brick of every device. owner_cell[d, e] for e < 4096 is the cell of d's own entry e; for e >= 4096 it is the cell named by that entry of the device at d's position minus the step of group (e - 4096) // 512, or 4096 where that slot is empty. The used entries of one aligned window of 128 entries name cells of one aligned window of 128 cells.
All inputs are finite; a program needn't handle non-finite values.
Results may differ from a plain program's by a relative error of at most 0.017.
Values may be sent and summed in bfloat16 or wider, within the bound.
No kernel may reach another device: no remote copies, remote signals or barrier semaphores. Data moves between devices by JAX's collectives and lax.ppermute only.
A program may use at most 128 MiB of HBM per device.

v0:
```python
import functools

import jax
import jax.numpy as jnp
from jax import lax
from jax.experimental import pallas as pl
from jax.experimental.pallas import tpu as pltpu
from jax.sharding import PartitionSpec as P

BLK = 128
C_DEV = 4096
SELF_CAP = 4096
WIN = 128
BRICKS_PER_STEP = 64
UNROLL = 16
UP_UNROLL = 32
WIN_UNROLL = 16

step_table = ((-1, -1), (-1, 0), (-1, 1), (0, -1), (0, 1), (1, -1), (1, 0), (1, 1))

NT = (((1,), (1,)), ((), ()))
TN = (((0,), (0,)), ((), ()))


def split_parts(data):
    high = data.astype(jnp.bfloat16)
    low = (data - high.astype(jnp.float32)).astype(jnp.bfloat16)
    return high, low


def one_hot_rows(index_row):
    span = lax.broadcasted_iota(jnp.int32, (WIN, index_row.shape[1]), 0)
    return (span == index_row).astype(jnp.bfloat16)


def down_kernel(first_window, count_ref, order_ref, win_ref, off_ref, xt_ref, e_ref, w_ref, *refs):
    outs = refs[:-1]
    acc = refs[-1]
    step = pl.program_id(0)
    per_step = e_ref.shape[0]
    trash = acc.shape[0] // WIN - 1

    @pl.when(step == 0)
    def _():
        acc[...] = jnp.zeros_like(acc)

    neighbours = count_ref[step]
    if first_window == 0:
        start, stop = neighbours, per_step
    else:
        start, stop = 0, neighbours

    def run(first, width, trips):
        def body(u, carry):
            results = []
            for t in range(width):
                position = first + u * width + t
                j = order_ref[step * per_step + jnp.minimum(position, per_step - 1)]
                brick = step * per_step + j
                window = jnp.where(position < stop, win_ref[brick] - first_window, trash)
                offset = off_ref[brick]
                inside = jnp.bitwise_and(e_ref[pl.ds(j, 1), :], WIN - 1)
                pick = one_hot_rows(inside)
                cols = pl.ds(pl.multiple_of(j * BLK, BLK), BLK)
                summed = lax.dot_general(pick, xt_ref[:, cols], NT, preferred_element_type=jnp.float32)
                part = jnp.dot(summed.astype(jnp.bfloat16), w_ref[offset], preferred_element_type=jnp.float32)
                results.append((window, part))
            for window, part in results:
                rows = pl.ds(pl.multiple_of(window * WIN, WIN), WIN)
                acc[rows, :] += part
            return carry

        lax.fori_loop(0, trips, body, 0)

    run(start, UNROLL, (stop - start + UNROLL - 1) // UNROLL)

    @pl.when(step == pl.num_programs(0) - 1)
    def _():
        size = outs[0].shape[0]
        for g, out in enumerate(outs):
            out[...] = acc[g * size : (g + 1) * size, :].astype(out.dtype)


def coarse_kernel(cw_ref, cells_ref, bias_ref, *refs):
    n_groups = len(step_table)
    sources = refs[: 1 + n_groups]
    outs = refs[1 + n_groups : 2 + 2 * n_groups]
    acc, coarse = refs[2 + 2 * n_groups :]
    cell_windows = acc.shape[0] // WIN
    acc[...] = jnp.zeros_like(acc)

    def pick_of(w):
        window = jnp.minimum(cw_ref[w], cell_windows - 1)
        cells = cells_ref[pl.ds(w, 1), :]
        inside = jnp.where(cells < C_DEV, cells - window * WIN, -1)
        rows = pl.ds(pl.multiple_of(window * WIN, WIN), WIN)
        return one_hot_rows(inside), rows

    base = 0
    for src in sources:
        count = src.shape[0] // WIN
        unroll = min(WIN_UNROLL, count)

        def gather_body(u, carry, src=src, base=base, unroll=unroll):
            results = []
            for t in range(unroll):
                j = u * unroll + t
                pick, rows = pick_of(base + j)
                entries = src[pl.ds(pl.multiple_of(j * WIN, WIN), WIN), :]
                results.append((rows, jnp.dot(pick, entries, preferred_element_type=jnp.float32)))
            for rows, value in results:
                acc[rows, :] += value
            return carry

        lax.fori_loop(0, count // unroll, gather_body, 0)
        base += count

    coarse[...] = jnp.maximum(acc[...] + bias_ref[...], 0.0).astype(jnp.bfloat16)

    base = 0
    for out in outs:
        count = out.shape[1] // WIN
        unroll = min(WIN_UNROLL, count)

        def scatter_body(u, carry, out=out, base=base, unroll=unroll):
            for t in range(unroll):
                j = u * unroll + t
                pick, rows = pick_of(base + j)
                chosen = lax.dot_general(coarse[rows, :], pick, TN, preferred_element_type=jnp.float32)
                out[:, pl.ds(pl.multiple_of(j * WIN, WIN), WIN)] = chosen.astype(jnp.bfloat16)
            return carry

        lax.fori_loop(0, count // unroll, scatter_body, 0)
        base += count


def up_kernel(win_ref, off_ref, xt_ref, e_ref, wt_ref, *refs):
    n_groups = len(step_table)
    sources = refs[: 1 + n_groups]
    out_ref = refs[1 + n_groups]
    stack, sems = refs[2 + n_groups :]
    step = pl.program_id(0)
    per_step = e_ref.shape[0]

    @pl.when(step == 0)
    def _():
        copies = []
        start = 0
        for index, src in enumerate(sources):
            size = src.shape[1]
            copy = pltpu.make_async_copy(src, stack.at[:, pl.ds(start, size)], sems.at[index])
            copy.start()
            copies.append(copy)
            start += size
        for copy in copies:
            copy.wait()

    def body(u, carry):
        for t in range(UP_UNROLL):
            j = u * UP_UNROLL + t
            brick = step * per_step + j
            window = win_ref[brick]
            offset = off_ref[brick]
            inside = jnp.bitwise_and(e_ref[pl.ds(j, 1), :], WIN - 1)
            pick = one_hot_rows(inside)
            parents = stack[:, pl.ds(pl.multiple_of(window * WIN, WIN), WIN)]
            rows_t = jnp.dot(parents, pick, preferred_element_type=jnp.float32).astype(jnp.bfloat16)
            lifted = jnp.dot(wt_ref[offset], rows_t, preferred_element_type=jnp.float32)
            cols = pl.ds(pl.multiple_of(j * BLK, BLK), BLK)
            out_ref[:, cols] = (xt_ref[:, cols].astype(jnp.float32) + lifted).astype(out_ref.dtype)
        return carry

    lax.fori_loop(0, per_step // UP_UNROLL, body, 0)


def group_route(g, sign):
    n_outer = lax.axis_size("outer")
    n_inner = lax.axis_size("inner")
    a, b = step_table[g]
    route = []
    for s in range(n_outer * n_inner):
        row, col = divmod(s, n_inner)
        owner = ((row + a) % n_outer) * n_inner + (col + b) % n_inner
        route.append((s, owner) if sign > 0 else (owner, s))
    return route


def local(features, block_offset, parent_entry, owner_cell, w_down, b_down, w_up):
    n_groups = len(step_table)
    fine_rows, in_width = features.shape
    out_width = w_down.shape[2]
    entries = owner_cell.shape[1]
    cap = (entries - SELF_CAP) // n_groups
    blocks = fine_rows // BLK
    steps = blocks // BRICKS_PER_STEP

    xt = features.T
    entry_rows = parent_entry.reshape(blocks, BLK)
    brick_window = entry_rows[:, 0] // WIN
    cells = owner_cell.reshape(entries // WIN, WIN)
    cell_window = jnp.min(cells, axis=1) // WIN
    w_up_t = jnp.swapaxes(w_up, 1, 2)

    part_shapes = [jax.ShapeDtypeStruct((SELF_CAP, out_width), jnp.bfloat16)] + [
        jax.ShapeDtypeStruct((cap, out_width), jnp.bfloat16)
    ] * n_groups
    answer_shapes = [jax.ShapeDtypeStruct((s.shape[1], s.shape[0]), s.dtype) for s in part_shapes]
    whole = lambda shape: pl.BlockSpec(shape, lambda *idx: (0,) * len(shape))

    is_far = (brick_window >= SELF_CAP // WIN).astype(jnp.int32).reshape(steps, BRICKS_PER_STEP)
    far_count = jnp.sum(is_far, axis=1)
    far_rank = jnp.cumsum(is_far, axis=1) - is_far
    own_rank = jnp.cumsum(1 - is_far, axis=1) - (1 - is_far)
    position = jnp.where(is_far == 1, far_rank, far_count[:, None] + own_rank)
    local_ids = jnp.arange(BRICKS_PER_STEP, dtype=jnp.int32)
    order = jnp.sum(
        jnp.where(position[:, None, :] == local_ids[None, :, None], local_ids[None, None, :], 0), axis=2
    )
    order = order.reshape(blocks).astype(jnp.int32)
    counts = far_count.astype(jnp.int32)

    def down_call(first_window, shapes):
        rows = sum(s.shape[0] for s in shapes)
        return pl.pallas_call(
            functools.partial(down_kernel, first_window),
            out_shape=shapes,
            grid_spec=pltpu.PrefetchScalarGridSpec(
                num_scalar_prefetch=4,
                grid=(steps,),
                in_specs=[
                    pl.BlockSpec((in_width, BRICKS_PER_STEP * BLK), lambda i, *_: (0, i)),
                    pl.BlockSpec((BRICKS_PER_STEP, BLK), lambda i, *_: (i, 0)),
                    whole(w_down.shape),
                ],
                out_specs=[whole(s.shape) for s in shapes],
                scratch_shapes=[pltpu.VMEM((rows + WIN, out_width), jnp.float32)],
            ),
            compiler_params=pltpu.CompilerParams(dimension_semantics=("arbitrary",)),
            cost_estimate=pl.CostEstimate(
                flops=2 * fine_rows * in_width * out_width,
                transcendentals=0,
                bytes_accessed=fine_rows * (in_width * 2 + 4) + rows * out_width * 2,
            ),
        )(counts, order, brick_window, block_offset, xt, entry_rows, w_down)

    parts = [None] + list(down_call(SELF_CAP // WIN, part_shapes[1:]))
    parts[0] = down_call(0, part_shapes[:1])[0]

    arrived = [
        lax.ppermute(parts[1 + g], ("outer", "inner"), group_route(g, 1)) for g in range(n_groups)
    ]

    coarse = pl.pallas_call(
        coarse_kernel,
        out_shape=answer_shapes,
        grid_spec=pltpu.PrefetchScalarGridSpec(
            num_scalar_prefetch=1,
            grid=(1,),
            in_specs=[whole(cells.shape), whole((1, out_width))]
            + [whole(s.shape) for s in part_shapes],
            out_specs=[whole(s.shape) for s in answer_shapes],
            scratch_shapes=[
                pltpu.VMEM((C_DEV, out_width), jnp.float32),
                pltpu.VMEM((C_DEV, out_width), jnp.bfloat16),
            ],
        ),
        cost_estimate=pl.CostEstimate(
            flops=4 * entries * WIN * out_width,
            transcendentals=0,
            bytes_accessed=4 * entries * out_width,
        ),
    )
    answers = coarse(cell_window, cells, b_down.reshape(1, out_width), parts[0], *arrived)

    returned = [
        lax.ppermute(answers[1 + g], ("outer", "inner"), group_route(g, -1)) for g in range(n_groups)
    ]

    up = pl.pallas_call(
        up_kernel,
        out_shape=jax.ShapeDtypeStruct((in_width, fine_rows), features.dtype),
        grid_spec=pltpu.PrefetchScalarGridSpec(
            num_scalar_prefetch=2,
            grid=(steps,),
            in_specs=[
                pl.BlockSpec((in_width, BRICKS_PER_STEP * BLK), lambda i, *_: (0, i)),
                pl.BlockSpec((BRICKS_PER_STEP, BLK), lambda i, *_: (i, 0)),
                whole(w_up_t.shape),
            ]
            + [pl.BlockSpec(memory_space=pl.ANY)] * (1 + n_groups),
            out_specs=pl.BlockSpec((in_width, BRICKS_PER_STEP * BLK), lambda i, *_: (0, i)),
            scratch_shapes=[
                pltpu.VMEM((out_width, entries), jnp.bfloat16),
                pltpu.SemaphoreType.DMA((1 + n_groups,)),
            ],
        ),
        compiler_params=pltpu.CompilerParams(dimension_semantics=("arbitrary",)),
        cost_estimate=pl.CostEstimate(
            flops=6 * fine_rows * in_width * out_width,
            transcendentals=0,
            bytes_accessed=fine_rows * (in_width * 4 + 4) + entries * out_width * 2,
        ),
    )
    out_t = up(brick_window, block_offset, xt, entry_rows, w_up_t, answers[0], *returned)
    return out_t.T


def solution(mesh):
    in_specs = (
        P(("outer", "inner"), None),
        P(("outer", "inner")),
        P(("outer", "inner")),
        P(("outer", "inner"), None),
        P(),
        P(),
        P(),
    )
    out_specs = P(("outer", "inner"), None)
    return jax.shard_map(local, mesh=mesh, in_specs=in_specs, out_specs=out_specs, check_vma=False)
```

profile of v0, /device:TPU:24, one launch (start us, length us, event | category | flops | bytes accessed | tf_op | source)
XLA Modules:
  0.0 83.7 jit_solution(188298075943163003)
XLA Ops:
  0.0 1.0 %slice_reduce_fusion = s32[256]{0:T(256)S(1)} fusion(s32[256,128]{1,0:T(8,128)} %bitcast.9), kind=kLoop, calls=%fused_computation | loop fusion | bytes 2048 | tf_op jit(solution)/shard_map/slice | solution.py:199
  1.0 0.6 and_select_fusion.1.win_ref
  1.6 0.1 squeeze.6
  1.7 0.1 convert_reduce_fusion.count_ref
  1.9 0.2 reduce_window_sum.18
  2.1 0.2 reduce_window_sum.17
  2.3 0.1 fusion.2
  2.4 0.1 select_reduce_fusion
  2.6 0.7 reshape.114.order_ref
  3.2 0.0 copy-done.17
  3.2 9.9 %shard_map.74 = (bf16[512,128]{1,0:T(8,128)(2,1)}, bf16[512,128]{1,0:T(8,128)(2,1)}, bf16[512,128]{1,0:T(8,128)(2,1)}, bf16[512,128]{1,0:T(8,128)(2,1)}, bf16[51...) custom-call(s32[4]{0:T(128)} %copy-done.17, ...), custom_call_target="tpu_custom_call" | custom-call | flops 536870912 | bytes 5373952 | tf_op jit(solution)/shard_map/pallas_call | solution.py:224
  13.1 5.9 %collective-permute-start = (bf16[512,128]{1,0:T(8,128)(2,1)}, bf16[512,128]{1,0:T(8,128)(2,1)S(1)}, u32[]{:S(2)}, u32[]{:S(2)}) collective-permute-start(bf16[512,128]{1,0:T(8,128)(2,1)} %get-tuple-element.22), channel_id=1, source_target_pairs={{0,127},{1,120},{2,121},{3,122},{4,123},{5,124},{6,125},{7,126},{8... | collective-permute-start | bytes 393224 | tf_op jit(solution)/shard_map/ppermute | solution.py:250
  19.0 1.5 %collective-permute-start.1 = (bf16[512,128]{1,0:T(8,128)(2,1)}, bf16[512,128]{1,0:T(8,128)(2,1)S(1)}, u32[]{:S(2)}, u32[]{:S(2)}) collective-permute-start(bf16[512,128]{1,0:T(8,128)(2,1)} %get-tuple-element.23), channel_id=1, source_target_pairs={{0,120},{1,121},{2,122},{3,123},{4,124},{5,125},{6,126},{7,127},{8... | collective-permute-start | bytes 393224 | tf_op jit(solution)/shard_map/ppermute | solution.py:250
  20.4 0.0 collective-permute-start.2
  20.4 1.2 %collective-permute-start.3 = (bf16[512,128]{1,0:T(8,128)(2,1)}, bf16[512,128]{1,0:T(8,128)(2,1)S(1)}, u32[]{:S(2)}, u32[]{:S(2)}) collective-permute-start(bf16[512,128]{1,0:T(8,128)(2,1)} %get-tuple-element.25), channel_id=1, source_target_pairs={{0,7},{1,0},{2,1},{3,2},{4,3},{5,4},{6,5},{7,6},{8,15},{9,8},{10,9... | collective-permute-start | bytes 393224 | tf_op jit(solution)/shard_map/ppermute | solution.py:250
  21.6 0.1 collective-permute-start.4
  21.7 0.0 copy-done.8
  21.7 0.1 reduce_min.9
  21.8 1.3 %collective-permute-done.refs_1_ = bf16[512,128]{1,0:T(8,128)(2,1)S(1)} collective-permute-done((bf16[512,128]{1,0:T(8,128)(2,1)}, bf16[512,128]{1,0:T(8,128)(2,1)S(1)}, u32[]{:S(2)}, u32[]{:S(2)}) %collective-permute-start) | collective-permute-done | bytes 131104 | tf_op jit(solution)/shard_map/ppermute | solution.py:250
  23.2 1.9 %collective-permute-start.5 = (bf16[512,128]{1,0:T(8,128)(2,1)}, bf16[512,128]{1,0:T(8,128)(2,1)S(1)}, u32[]{:S(2)}, u32[]{:S(2)}) collective-permute-start(bf16[512,128]{1,0:T(8,128)(2,1)} %get-tuple-element.27), channel_id=1, source_target_pairs={{0,15},{1,8},{2,9},{3,10},{4,11},{5,12},{6,13},{7,14},{8,23},{9,16... | collective-permute-start | bytes 393224 | tf_op jit(solution)/shard_map/ppermute | solution.py:250
  25.0 0.9 %collective-permute-done.1.refs_2_ = bf16[512,128]{1,0:T(8,128)(2,1)S(1)} collective-permute-done((bf16[512,128]{1,0:T(8,128)(2,1)}, bf16[512,128]{1,0:T(8,128)(2,1)S(1)}, u32[]{:S(2)}, u32[]{:S(2)}) %collective-permute-start.1) | collective-permute-done | bytes 131104 | tf_op jit(solution)/shard_map/ppermute | solution.py:250
  26.0 0.0 collective-permute-start.6
  26.0 2.6 %collective-permute-done.2.refs_3_ = bf16[512,128]{1,0:T(8,128)(2,1)S(1)} collective-permute-done((bf16[512,128]{1,0:T(8,128)(2,1)}, bf16[512,128]{1,0:T(8,128)(2,1)S(1)}, u32[]{:S(2)}, u32[]{:S(2)}) %collective-permute-start.2) | collective-permute-done | bytes 131104 | tf_op jit(solution)/shard_map/ppermute | solution.py:250
  28.6 0.4 collective-permute-start.7
  28.9 0.6 and_select_fusion.cw_ref
  29.5 9.2 %shard_map.73.refs_0_ = bf16[4096,128]{1,0:T(8,128)(2,1)} custom-call(s32[4]{0:T(128)} %copy-done.17, s32[256]{0:T(256)} %reshape.114.order_ref, s32[256]{0:T(256)} %and_select_fusion.1.win_ref, s32[256]{0:T(256)} %off_ref.5, bf16[64,32768]{1,0:T(8,128)(2,1)} %bitcast.7, s32[256,128]{1,0:T(8,128)} %bitcast.11, bf16[8,64,128]{2,1,0:T(8,128)(2,1)} %w_ref.3), custom_call_target="tpu_custom_call" | custom-call | flops 536870912 | bytes 5373952 | tf_op jit(solution)/shard_map/pallas_call | solution.py:224
  38.8 0.0 collective-permute-done.3.refs_4_
  38.8 0.0 collective-permute-done.4.refs_5_
  38.8 0.0 copy-start.13
  38.8 0.0 collective-permute-done.5.refs_6_
  38.8 0.0 copy-start.14
  38.8 1.4 %collective-permute-done.6.refs_7_ = bf16[512,128]{1,0:T(8,128)(2,1)S(1)} collective-permute-done((bf16[512,128]{1,0:T(8,128)(2,1)}, bf16[512,128]{1,0:T(8,128)(2,1)S(1)}, u32[]{:S(2)}, u32[]{:S(2)}) %collective-permute-start.6) | collective-permute-done | bytes 131104 | tf_op jit(solution)/shard_map/ppermute | solution.py:250
  40.2 0.5 collective-permute-done.7.refs_8_
  40.7 0.0 copy-done.9
  40.7 0.0 copy-done.10
  40.7 0.0 copy-done.11
  40.7 0.0 copy-done.12
  40.7 0.0 copy-done.13
  40.7 0.0 copy-done.14
  40.7 0.1 copy-done.15
  40.8 0.5 copy-done.16
  41.3 6.0 %shard_map.75 = (bf16[128,4096]{1,0:T(8,128)(2,1)}, bf16[128,512]{1,0:T(8,128)(2,1)}, bf16[128,512]{1,0:T(8,128)(2,1)}, bf16[128,512]{1,0:T(8,128)(2,1)}, bf16[1...) custom-call(s32[64]{0:T(128)} %and_select_fusion.cw_ref, ...), custom_call_target="tpu_custom_call" | custom-call | flops 536870912 | bytes 4194304 | tf_op jit(solution)/shard_map/pallas_call | solution.py:273
  47.3 0.0 collective-permute-start.8
  47.3 2.4 %collective-permute-start.9 = (bf16[128,512]{1,0:T(8,128)(2,1)}, bf16[128,512]{1,0:T(8,128)(2,1)S(1)}, u32[]{:S(2)}, u32[]{:S(2)}) collective-permute-start(bf16[128,512]{1,0:T(8,128)(2,1)} %get-tuple-element.32), channel_id=1, source_target_pairs={{120,0},{121,1},{122,2},{123,3},{124,4},{125,5},{126,6},{127,7},{0... | collective-permute-start | bytes 393224 | tf_op jit(solution)/shard_map/ppermute | solution.py:276
  49.7 0.0 collective-permute-start.10
  49.7 0.1 collective-permute-start.11
  49.9 1.6 %collective-permute-start.12 = (bf16[128,512]{1,0:T(8,128)(2,1)}, bf16[128,512]{1,0:T(8,128)(2,1)S(1)}, u32[]{:S(2)}, u32[]{:S(2)}) collective-permute-start(bf16[128,512]{1,0:T(8,128)(2,1)} %get-tuple-element.35), channel_id=1, source_target_pairs={{1,0},{2,1},{3,2},{4,3},{5,4},{6,5},{7,6},{0,7},{9,8},{10,9},{11,1... | collective-permute-start | bytes 393224 | tf_op jit(solution)/shard_map/ppermute | solution.py:276
  51.5 6.7 %collective-permute-done.8.refs_1_ = bf16[128,512]{1,0:T(8,128)(2,1)S(1)} collective-permute-done((bf16[128,512]{1,0:T(8,128)(2,1)}, bf16[128,512]{1,0:T(8,128)(2,1)S(1)}, u32[]{:S(2)}, u32[]{:S(2)}) %collective-permute-start.8) | collective-permute-done | bytes 131104 | tf_op jit(solution)/shard_map/ppermute | solution.py:276
  58.2 0.4 collective-permute-start.13
  58.6 0.7 collective-permute-done.9.refs_2_
  59.2 2.9 %collective-permute-start.14 = (bf16[128,512]{1,0:T(8,128)(2,1)}, bf16[128,512]{1,0:T(8,128)(2,1)S(1)}, u32[]{:S(2)}, u32[]{:S(2)}) collective-permute-start(bf16[128,512]{1,0:T(8,128)(2,1)} %get-tuple-element.37), channel_id=1, source_target_pairs={{8,0},{9,1},{10,2},{11,3},{12,4},{13,5},{14,6},{15,7},{16,8},{17,9... | collective-permute-start | bytes 393224 | tf_op jit(solution)/shard_map/ppermute | solution.py:276
  62.2 2.2 %collective-permute-done.10.refs_3_ = bf16[128,512]{1,0:T(8,128)(2,1)S(1)} collective-permute-done((bf16[128,512]{1,0:T(8,128)(2,1)}, bf16[128,512]{1,0:T(8,128)(2,1)S(1)}, u32[]{:S(2)}, u32[]{:S(2)}) %collective-permute-start.10) | collective-permute-done | bytes 131104 | tf_op jit(solution)/shard_map/ppermute | solution.py:276
  64.4 0.0 collective-permute-start.15
  64.4 0.0 collective-permute-done.11.refs_4_
  64.4 0.0 copy-start.3
  64.4 0.0 collective-permute-done.12.refs_5_
  64.4 0.0 copy-start.4
  64.4 0.4 collective-permute-done.13.refs_6_
  64.8 1.5 %collective-permute-done.14.refs_7_ = bf16[128,512]{1,0:T(8,128)(2,1)S(1)} collective-permute-done((bf16[128,512]{1,0:T(8,128)(2,1)}, bf16[128,512]{1,0:T(8,128)(2,1)S(1)}, u32[]{:S(2)}, u32[]{:S(2)}) %collective-permute-start.14) | collective-permute-done | bytes 131104 | tf_op jit(solution)/shard_map/ppermute | solution.py:276
  66.3 5.6 %collective-permute-done.15.refs_8_ = bf16[128,512]{1,0:T(8,128)(2,1)S(1)} collective-permute-done((bf16[128,512]{1,0:T(8,128)(2,1)}, bf16[128,512]{1,0:T(8,128)(2,1)S(1)}, u32[]{:S(2)}, u32[]{:S(2)}) %collective-permute-start.15) | collective-permute-done | bytes 131104 | tf_op jit(solution)/shard_map/ppermute | solution.py:276
  71.9 0.0 copy-done
  71.9 0.0 copy-done.1
  71.9 0.6 copy-done.7
  72.5 11.2 %shard_map.76 = bf16[64,32768]{1,0:T(8,128)(2,1)} custom-call(s32[256]{0:T(256)} %and_select_fusion.1.win_ref, s32[256]{0:T(256)} %off_ref.5, bf16[64,32768]{1,0:T(8,128)(2,1)} %bitcast.8, s32[256,128]{1,0:T(8,128)} %bitcast.12, bf16[8,64,128]{2,1,0:T(8,128)(2,1)} %bitcast.13, bf16[128,4096]{1,0:T(8,128)(2,1)} %get-tuple-element.30.refs_0_, ...), custom_call_target="tpu_custom_call" | custom-call | flops 1610612736 | bytes 10616832 | tf_op jit(solution)/shard_map/pallas_call | solution.py:304
  (21 shorter events, 0.1 us)
Async XLA Ops:
  0.0 21.7 %copy-start.8 = (s32[1,8192]{1,0:T(1,128)S(1)}, s32[1,8192]{1,0:T(1,128)}, u32[]{:S(2)}) copy-start(s32[1,8192]{1,0:T(1,128)} %param.10) | copy-start | bytes 98308
  1.8 1.4 %copy-start.17 = (s32[4]{0:T(128)}, s32[4]{0:T(128)S(1)}, u32[]{:S(2)}) copy-start(s32[4]{0:T(128)S(1)} %convert_reduce_fusion.count_ref) | copy-start | bytes 52
  13.1 10.1 %collective-permute-start = (bf16[512,128]{1,0:T(8,128)(2,1)}, bf16[512,128]{1,0:T(8,128)(2,1)S(1)}, u32[]{:S(2)}, u32[]{:S(2)}) collective-permute-start(bf16[512,128]{1,0:T(8,128)(2,1)} %get-tuple-element.22), channel_id=1, source_target_pairs={{0,127},{1,120},{2,121},{3,122},{4,123},{5,124},{6,125},{7,126},{8... | collective-permute-start | bytes 393224 | tf_op jit(solution)/shard_map/ppermute | solution.py:250
  19.0 7.0 %collective-permute-start.1 = (bf16[512,128]{1,0:T(8,128)(2,1)}, bf16[512,128]{1,0:T(8,128)(2,1)S(1)}, u32[]{:S(2)}, u32[]{:S(2)}) collective-permute-start(bf16[512,128]{1,0:T(8,128)(2,1)} %get-tuple-element.23), channel_id=1, source_target_pairs={{0,120},{1,121},{2,122},{3,123},{4,124},{5,125},{6,126},{7,127},{8... | collective-permute-start | bytes 393224 | tf_op jit(solution)/shard_map/ppermute | solution.py:250
  20.4 8.2 %collective-permute-start.2 = (bf16[512,128]{1,0:T(8,128)(2,1)}, bf16[512,128]{1,0:T(8,128)(2,1)S(1)}, u32[]{:S(2)}, u32[]{:S(2)}) collective-permute-start(bf16[512,128]{1,0:T(8,128)(2,1)} %get-tuple-element.24), channel_id=1, source_target_pairs={{0,121},{1,122},{2,123},{3,124},{4,125},{5,126},{6,127},{7,120},{8... | collective-permute-start | bytes 393224 | tf_op jit(solution)/shard_map/ppermute | solution.py:250
  20.4 18.3 %collective-permute-start.3 = (bf16[512,128]{1,0:T(8,128)(2,1)}, bf16[512,128]{1,0:T(8,128)(2,1)S(1)}, u32[]{:S(2)}, u32[]{:S(2)}) collective-permute-start(bf16[512,128]{1,0:T(8,128)(2,1)} %get-tuple-element.25), channel_id=1, source_target_pairs={{0,7},{1,0},{2,1},{3,2},{4,3},{5,4},{6,5},{7,6},{8,15},{9,8},{10,9... | collective-permute-start | bytes 393224 | tf_op jit(solution)/shard_map/ppermute | solution.py:250
  21.6 17.2 %collective-permute-start.4 = (bf16[512,128]{1,0:T(8,128)(2,1)}, bf16[512,128]{1,0:T(8,128)(2,1)S(1)}, u32[]{:S(2)}, u32[]{:S(2)}) collective-permute-start(bf16[512,128]{1,0:T(8,128)(2,1)} %get-tuple-element.26), channel_id=1, source_target_pairs={{0,1},{1,2},{2,3},{3,4},{4,5},{5,6},{6,7},{7,0},{8,9},{9,10},{10,1... | collective-permute-start | bytes 393224 | tf_op jit(solution)/shard_map/ppermute | solution.py:250
  23.2 17.5 %copy-start.9 = (bf16[512,128]{1,0:T(8,128)(2,1)}, bf16[512,128]{1,0:T(8,128)(2,1)S(1)}, u32[]{:S(2)}) copy-start(bf16[512,128]{1,0:T(8,128)(2,1)S(1)} %collective-permute-done.refs_1_) | copy-start | bytes 393220
  23.2 15.6 %collective-permute-start.5 = (bf16[512,128]{1,0:T(8,128)(2,1)}, bf16[512,128]{1,0:T(8,128)(2,1)S(1)}, u32[]{:S(2)}, u32[]{:S(2)}) collective-permute-start(bf16[512,128]{1,0:T(8,128)(2,1)} %get-tuple-element.27), channel_id=1, source_target_pairs={{0,15},{1,8},{2,9},{3,10},{4,11},{5,12},{6,13},{7,14},{8,23},{9,16... | collective-permute-start | bytes 393224 | tf_op jit(solution)/shard_map/ppermute | solution.py:250
  26.0 14.7 %copy-start.10 = (bf16[512,128]{1,0:T(8,128)(2,1)}, bf16[512,128]{1,0:T(8,128)(2,1)S(1)}, u32[]{:S(2)}) copy-start(bf16[512,128]{1,0:T(8,128)(2,1)S(1)} %collective-permute-done.1.refs_2_) | copy-start | bytes 393220
  26.0 14.2 %collective-permute-start.6 = (bf16[512,128]{1,0:T(8,128)(2,1)}, bf16[512,128]{1,0:T(8,128)(2,1)S(1)}, u32[]{:S(2)}, u32[]{:S(2)}) collective-permute-start(bf16[512,128]{1,0:T(8,128)(2,1)} %get-tuple-element.28), channel_id=1, source_target_pairs={{0,8},{1,9},{2,10},{3,11},{4,12},{5,13},{6,14},{7,15},{8,16},{9,17... | collective-permute-start | bytes 393224 | tf_op jit(solution)/shard_map/ppermute | solution.py:250
  28.6 12.1 %copy-start.11 = (bf16[512,128]{1,0:T(8,128)(2,1)}, bf16[512,128]{1,0:T(8,128)(2,1)S(1)}, u32[]{:S(2)}) copy-start(bf16[512,128]{1,0:T(8,128)(2,1)S(1)} %collective-permute-done.2.refs_3_) | copy-start | bytes 393220
  28.6 12.1 %collective-permute-start.7 = (bf16[512,128]{1,0:T(8,128)(2,1)}, bf16[512,128]{1,0:T(8,128)(2,1)S(1)}, u32[]{:S(2)}, u32[]{:S(2)}) collective-permute-start(bf16[512,128]{1,0:T(8,128)(2,1)} %get-tuple-element.29), channel_id=1, source_target_pairs={{0,9},{1,10},{2,11},{3,12},{4,13},{5,14},{6,15},{7,8},{8,17},{9,18... | collective-permute-start | bytes 393224 | tf_op jit(solution)/shard_map/ppermute | solution.py:250
  38.8 1.9 %copy-start.12 = (bf16[512,128]{1,0:T(8,128)(2,1)}, bf16[512,128]{1,0:T(8,128)(2,1)S(1)}, u32[]{:S(2)}) copy-start(bf16[512,128]{1,0:T(8,128)(2,1)S(1)} %collective-permute-done.3.refs_4_) | copy-start | bytes 393220
  38.8 1.9 %copy-start.13 = (bf16[512,128]{1,0:T(8,128)(2,1)}, bf16[512,128]{1,0:T(8,128)(2,1)S(1)}, u32[]{:S(2)}) copy-start(bf16[512,128]{1,0:T(8,128)(2,1)S(1)} %collective-permute-done.4.refs_5_) | copy-start | bytes 393220
  38.8 1.9 %copy-start.14 = (bf16[512,128]{1,0:T(8,128)(2,1)}, bf16[512,128]{1,0:T(8,128)(2,1)S(1)}, u32[]{:S(2)}) copy-start(bf16[512,128]{1,0:T(8,128)(2,1)S(1)} %collective-permute-done.5.refs_6_) | copy-start | bytes 393220
  40.2 0.7 copy-start.15
  40.7 0.6 copy-start.16
  47.3 10.9 %collective-permute-start.8 = (bf16[128,512]{1,0:T(8,128)(2,1)}, bf16[128,512]{1,0:T(8,128)(2,1)S(1)}, u32[]{:S(2)}, u32[]{:S(2)}) collective-permute-start(bf16[128,512]{1,0:T(8,128)(2,1)} %get-tuple-element.31), channel_id=1, source_target_pairs={{127,0},{120,1},{121,2},{122,3},{123,4},{124,5},{125,6},{126,7},{7... | collective-permute-start | bytes 393224 | tf_op jit(solution)/shard_map/ppermute | solution.py:276
  47.3 11.9 %collective-permute-start.9 = (bf16[128,512]{1,0:T(8,128)(2,1)}, bf16[128,512]{1,0:T(8,128)(2,1)S(1)}, u32[]{:S(2)}, u32[]{:S(2)}) collective-permute-start(bf16[128,512]{1,0:T(8,128)(2,1)} %get-tuple-element.32), channel_id=1, source_target_pairs={{120,0},{121,1},{122,2},{123,3},{124,4},{125,5},{126,6},{127,7},{0... | collective-permute-start | bytes 393224 | tf_op jit(solution)/shard_map/ppermute | solution.py:276
  49.7 14.6 %collective-permute-start.10 = (bf16[128,512]{1,0:T(8,128)(2,1)}, bf16[128,512]{1,0:T(8,128)(2,1)S(1)}, u32[]{:S(2)}, u32[]{:S(2)}) collective-permute-start(bf16[128,512]{1,0:T(8,128)(2,1)} %get-tuple-element.33), channel_id=1, source_target_pairs={{121,0},{122,1},{123,2},{124,3},{125,4},{126,5},{127,6},{120,7},{1... | collective-permute-start | bytes 393224 | tf_op jit(solution)/shard_map/ppermute | solution.py:276
  49.7 14.6 %collective-permute-start.11 = (bf16[128,512]{1,0:T(8,128)(2,1)}, bf16[128,512]{1,0:T(8,128)(2,1)S(1)}, u32[]{:S(2)}, u32[]{:S(2)}) collective-permute-start(bf16[128,512]{1,0:T(8,128)(2,1)} %get-tuple-element.34), channel_id=1, source_target_pairs={{7,0},{0,1},{1,2},{2,3},{3,4},{4,5},{5,6},{6,7},{15,8},{8,9},{9,10... | collective-permute-start | bytes 393224 | tf_op jit(solution)/shard_map/ppermute | solution.py:276
  49.9 14.5 %collective-permute-start.12 = (bf16[128,512]{1,0:T(8,128)(2,1)}, bf16[128,512]{1,0:T(8,128)(2,1)S(1)}, u32[]{:S(2)}, u32[]{:S(2)}) collective-permute-start(bf16[128,512]{1,0:T(8,128)(2,1)} %get-tuple-element.35), channel_id=1, source_target_pairs={{1,0},{2,1},{3,2},{4,3},{5,4},{6,5},{7,6},{0,7},{9,8},{10,9},{11,1... | collective-permute-start | bytes 393224 | tf_op jit(solution)/shard_map/ppermute | solution.py:276
  58.2 13.7 %copy-start = (bf16[128,512]{1,0:T(8,128)(2,1)}, bf16[128,512]{1,0:T(8,128)(2,1)S(1)}, u32[]{:S(2)}) copy-start(bf16[128,512]{1,0:T(8,128)(2,1)S(1)} %collective-permute-done.8.refs_1_) | copy-start | bytes 393220
  58.2 6.5 %collective-permute-start.13 = (bf16[128,512]{1,0:T(8,128)(2,1)}, bf16[128,512]{1,0:T(8,128)(2,1)S(1)}, u32[]{:S(2)}, u32[]{:S(2)}) collective-permute-start(bf16[128,512]{1,0:T(8,128)(2,1)} %get-tuple-element.36), channel_id=1, source_target_pairs={{15,0},{8,1},{9,2},{10,3},{11,4},{12,5},{13,6},{14,7},{23,8},{16,9... | collective-permute-start | bytes 393224 | tf_op jit(solution)/shard_map/ppermute | solution.py:276
  59.2 12.6 %copy-start.1 = (bf16[128,512]{1,0:T(8,128)(2,1)}, bf16[128,512]{1,0:T(8,128)(2,1)S(1)}, u32[]{:S(2)}) copy-start(bf16[128,512]{1,0:T(8,128)(2,1)S(1)} %collective-permute-done.9.refs_2_) | copy-start | bytes 393220
  59.2 7.1 %collective-permute-start.14 = (bf16[128,512]{1,0:T(8,128)(2,1)}, bf16[128,512]{1,0:T(8,128)(2,1)S(1)}, u32[]{:S(2)}, u32[]{:S(2)}) collective-permute-start(bf16[128,512]{1,0:T(8,128)(2,1)} %get-tuple-element.37), channel_id=1, source_target_pairs={{8,0},{9,1},{10,2},{11,3},{12,4},{13,5},{14,6},{15,7},{16,8},{17,9... | collective-permute-start | bytes 393224 | tf_op jit(solution)/shard_map/ppermute | solution.py:276
  64.3 7.5 %copy-start.2 = (bf16[128,512]{1,0:T(8,128)(2,1)}, bf16[128,512]{1,0:T(8,128)(2,1)S(1)}, u32[]{:S(2)}) copy-start(bf16[128,512]{1,0:T(8,128)(2,1)S(1)} %collective-permute-done.10.refs_3_) | copy-start | bytes 393220
  64.4 7.5 %collective-permute-start.15 = (bf16[128,512]{1,0:T(8,128)(2,1)}, bf16[128,512]{1,0:T(8,128)(2,1)S(1)}, u32[]{:S(2)}, u32[]{:S(2)}) collective-permute-start(bf16[128,512]{1,0:T(8,128)(2,1)} %get-tuple-element.38), channel_id=1, source_target_pairs={{9,0},{10,1},{11,2},{12,3},{13,4},{14,5},{15,6},{8,7},{17,8},{18,9... | collective-permute-start | bytes 393224 | tf_op jit(solution)/shard_map/ppermute | solution.py:276
  64.4 7.5 %copy-start.3 = (bf16[128,512]{1,0:T(8,128)(2,1)}, bf16[128,512]{1,0:T(8,128)(2,1)S(1)}, u32[]{:S(2)}) copy-start(bf16[128,512]{1,0:T(8,128)(2,1)S(1)} %collective-permute-done.11.refs_4_) | copy-start | bytes 393220
  64.4 7.5 %copy-start.4 = (bf16[128,512]{1,0:T(8,128)(2,1)}, bf16[128,512]{1,0:T(8,128)(2,1)S(1)}, u32[]{:S(2)}) copy-start(bf16[128,512]{1,0:T(8,128)(2,1)S(1)} %collective-permute-done.12.refs_5_) | copy-start | bytes 393220
  64.7 7.1 %copy-start.5 = (bf16[128,512]{1,0:T(8,128)(2,1)}, bf16[128,512]{1,0:T(8,128)(2,1)S(1)}, u32[]{:S(2)}) copy-start(bf16[128,512]{1,0:T(8,128)(2,1)S(1)} %collective-permute-done.13.refs_6_) | copy-start | bytes 393220
  66.3 5.6 %copy-start.6 = (bf16[128,512]{1,0:T(8,128)(2,1)}, bf16[128,512]{1,0:T(8,128)(2,1)S(1)}, u32[]{:S(2)}) copy-start(bf16[128,512]{1,0:T(8,128)(2,1)S(1)} %collective-permute-done.14.refs_7_) | copy-start | bytes 393220
  71.9 0.7 copy-start.7
where the time goes:
time: 84.1 us; the launch traced here: 83.7 us
  Pallas kernels  36.3 us (43%)
  waiting for transfers between devices  23.8 us (28%)
  starting transfers between devices  18.3 us (22%)
  local copies, waits for them, and re-layouts  3.02 us (4%)
  other arithmetic  2.15 us (3%)
    pallas_call x2, Pallas kernels, down_call(): pl.pallas_call(functools.partial(down_kernel, first_window), out_shape=sh...  19.1 us
    ppermute x8, waiting for transfers between devices, local(): lax.ppermute(answers[1 + g], ('outer', 'inner'), group_route(g, -1))  17.1 us
    pallas_call x1, Pallas kernels, local(): up(brick_window, block_offset, xt, entry_rows, w_up_t, answers[0], *retur...  11.2 us
    ppermute x8, starting transfers between devices, local(): lax.ppermute(parts[1 + g], ('outer', 'inner'), group_route(g, 1))  10.8 us
    ppermute x8, starting transfers between devices, local(): lax.ppermute(answers[1 + g], ('outer', 'inner'), group_route(g, -1))  7.42 us
    ppermute x8, waiting for transfers between devices, local(): lax.ppermute(parts[1 + g], ('outer', 'inner'), group_route(g, 1))  6.76 us
    pallas_call x1, Pallas kernels, local(): coarse(cell_window, cells, b_down.reshape(1, out_width), parts[0], *arrived)  5.99 us
  transfers between devices with their start and end apart: 16, of which 11 were waited for; matrix products, arithmetic and copies ran while one was open for 1% of the time, Pallas kernels for 11%

commit v1 on v0

--- a/solution.py
+++ b/solution.py
@@ -55,10 +55,11 @@
             results = []
             for t in range(width):
                 position = first + u * width + t
-                j = order_ref[step * per_step + jnp.minimum(position, per_step - 1)]
-                brick = step * per_step + j
-                window = jnp.where(position < stop, win_ref[brick] - first_window, trash)
-                offset = off_ref[brick]
+                packed = order_ref[step * per_step + jnp.minimum(position, per_step - 1)]
+                j = jnp.bitwise_and(packed, 255)
+                window = jnp.bitwise_and(jnp.right_shift(packed, 8), 255)
+                window = jnp.where(position < stop, window - first_window, trash)
+                offset = jnp.right_shift(packed, 16)
                 inside = jnp.bitwise_and(e_ref[pl.ds(j, 1), :], WIN - 1)
                 pick = one_hot_rows(inside)
                 cols = pl.ds(pl.multiple_of(j * BLK, BLK), BLK)
@@ -213,9 +214,12 @@
     own_rank = jnp.cumsum(1 - is_far, axis=1) - (1 - is_far)
     position = jnp.where(is_far == 1, far_rank, far_count[:, None] + own_rank)
     local_ids = jnp.arange(BRICKS_PER_STEP, dtype=jnp.int32)
-    order = jnp.sum(
-        jnp.where(position[:, None, :] == local_ids[None, :, None], local_ids[None, None, :], 0), axis=2
+    packed = (
+        local_ids[None, :]
+        + brick_window.reshape(steps, BRICKS_PER_STEP) * 256
+        + block_offset.reshape(steps, BRICKS_PER_STEP) * 65536
     )
+    order = jnp.sum(jnp.where(position[:, None, :] == local_ids[None, :, None], packed[:, None, :], 0), axis=2)
     order = order.reshape(blocks).astype(jnp.int32)
     counts = far_count.astype(jnp.int32)
 

time: 84.1 us -> 85.1 us (1.012)
  waiting for transfers between devices: 23.8 us -> 24.7 us
  transfers between devices with their start and end apart: 16 -> 16, of which waited for: 11 -> 9; matrix products, arithmetic and copies ran while one was open for 1% -> 1% of each run, Pallas kernels for 11% -> 10%
where the time goes in v1:
time: 85.1 us; the launch traced here: 84.8 us
  Pallas kernels  36.3 us (43%)
  waiting for transfers between devices  24.7 us (29%)
  starting transfers between devices  17.6 us (21%)
  local copies, waits for them, and re-layouts  3.1 us (4%)
  other arithmetic  2.88 us (3%)
    pallas_call x2, Pallas kernels, down_call(): pl.pallas_call(functools.partial(down_kernel, first_window), out_shape=sh...  19.1 us
    ppermute x8, waiting for transfers between devices, local(): lax.ppermute(answers[1 + g], ('outer', 'inner'), group_route(g, -1))  17.1 us
    pallas_call x1, Pallas kernels, local(): up(brick_window, block_offset, xt, entry_rows, w_up_t, answers[0], *retur...  11.2 us
    ppermute x8, starting transfers between devices, local(): lax.ppermute(parts[1 + g], ('outer', 'inner'), group_route(g, 1))  10.5 us
    ppermute x8, waiting for transfers between devices, local(): lax.ppermute(parts[1 + g], ('outer', 'inner'), group_route(g, 1))  7.61 us
    ppermute x8, starting transfers between devices, local(): lax.ppermute(answers[1 + g], ('outer', 'inner'), group_route(g, -1))  7.1 us
    pallas_call x1, Pallas kernels, local(): coarse(cell_window, cells, b_down.reshape(1, out_width), parts[0], *arrived)  5.99 us
  transfers between devices with their start and end apart: 16, of which 9 were waited for; matrix products, arithmetic and copies ran while one was open for 1% of the time, Pallas kernels for 10%

profile of v1, /device:TPU:24, one launch (start us, length us, event | category | flops | bytes accessed | tf_op | source)
XLA Modules:
  0.0 84.8 jit_solution(14541115575311263113)
XLA Ops:
  0.0 1.0 %slice_reduce_fusion = s32[256]{0:T(256)S(1)} fusion(s32[256,128]{1,0:T(8,128)} %bitcast.9), kind=kLoop, calls=%fused_computation | loop fusion | bytes 2048 | tf_op jit(solution)/shard_map/slice | solution.py:200
  1.0 0.6 and_select_fusion.1.win_ref
  1.6 0.1 squeeze.6
  1.7 0.7 broadcast_multiply_fusion
  2.4 0.1 mul.27
  2.5 0.1 convert_reduce_fusion.count_ref
  2.6 0.2 reduce_window_sum.18
  2.9 0.2 reduce_window_sum.17
  3.1 0.1 fusion.1
  3.2 0.1 select_reduce_fusion
  3.3 0.7 reshape.141.order_ref
  4.0 0.0 copy-done.17
  4.0 10.5 %shard_map.74 = (bf16[512,128]{1,0:T(8,128)(2,1)}, bf16[512,128]{1,0:T(8,128)(2,1)}, bf16[512,128]{1,0:T(8,128)(2,1)}, bf16[512,128]{1,0:T(8,128)(2,1)}, bf16[51...) custom-call(s32[4]{0:T(128)} %copy-done.17, ...), custom_call_target="tpu_custom_call" | custom-call | flops 536870912 | bytes 5373952 | tf_op jit(solution)/shard_map/pallas_call | solution.py:228
  14.5 5.2 %collective-permute-start = (bf16[512,128]{1,0:T(8,128)(2,1)}, bf16[512,128]{1,0:T(8,128)(2,1)S(1)}, u32[]{:S(2)}, u32[]{:S(2)}) collective-permute-start(bf16[512,128]{1,0:T(8,128)(2,1)} %get-tuple-element.22), channel_id=1, source_target_pairs={{0,127},{1,120},{2,121},{3,122},{4,123},{5,124},{6,125},{7,126},{8... | collective-permute-start | bytes 393224 | tf_op jit(solution)/shard_map/ppermute | solution.py:254
  19.7 0.8 collective-permute-start.1
  20.6 0.1 collective-permute-start.2
  20.7 2.9 %collective-permute-start.3 = (bf16[512,128]{1,0:T(8,128)(2,1)}, bf16[512,128]{1,0:T(8,128)(2,1)S(1)}, u32[]{:S(2)}, u32[]{:S(2)}) collective-permute-start(bf16[512,128]{1,0:T(8,128)(2,1)} %get-tuple-element.25), channel_id=1, source_target_pairs={{0,7},{1,0},{2,1},{3,2},{4,3},{5,4},{6,5},{7,6},{8,15},{9,8},{10,9... | collective-permute-start | bytes 393224 | tf_op jit(solution)/shard_map/ppermute | solution.py:254
  23.6 0.2 collective-permute-start.4
  23.8 0.0 copy-done.8
  23.8 0.1 reduce_min.9
  23.9 0.0 collective-permute-done.refs_1_
  23.9 1.2 %collective-permute-start.5 = (bf16[512,128]{1,0:T(8,128)(2,1)}, bf16[512,128]{1,0:T(8,128)(2,1)S(1)}, u32[]{:S(2)}, u32[]{:S(2)}) collective-permute-start(bf16[512,128]{1,0:T(8,128)(2,1)} %get-tuple-element.27), channel_id=1, source_target_pairs={{0,15},{1,8},{2,9},{3,10},{4,11},{5,12},{6,13},{7,14},{8,23},{9,16... | collective-permute-start | bytes 393224 | tf_op jit(solution)/shard_map/ppermute | solution.py:254
  25.1 1.7 %collective-permute-done.1.refs_2_ = bf16[512,128]{1,0:T(8,128)(2,1)S(1)} collective-permute-done((bf16[512,128]{1,0:T(8,128)(2,1)}, bf16[512,128]{1,0:T(8,128)(2,1)S(1)}, u32[]{:S(2)}, u32[]{:S(2)}) %collective-permute-start.1) | collective-permute-done | bytes 131104 | tf_op jit(solution)/shard_map/ppermute | solution.py:254
  26.8 0.0 collective-permute-start.6
  26.8 2.6 %collective-permute-done.2.refs_3_ = bf16[512,128]{1,0:T(8,128)(2,1)S(1)} collective-permute-done((bf16[512,128]{1,0:T(8,128)(2,1)}, bf16[512,128]{1,0:T(8,128)(2,1)S(1)}, u32[]{:S(2)}, u32[]{:S(2)}) %collective-permute-start.2) | collective-permute-done | bytes 131104 | tf_op jit(solution)/shard_map/ppermute | solution.py:254
  29.4 0.0 collective-permute-start.7
  29.4 0.6 and_select_fusion.cw_ref
  30.1 8.6 %shard_map.73.refs_0_ = bf16[4096,128]{1,0:T(8,128)(2,1)} custom-call(s32[4]{0:T(128)} %copy-done.17, s32[256]{0:T(256)} %reshape.141.order_ref, s32[256]{0:T(256)} %and_select_fusion.1.win_ref, s32[256]{0:T(256)} %off_ref.5, bf16[64,32768]{1,0:T(8,128)(2,1)} %bitcast.7, s32[256,128]{1,0:T(8,128)} %bitcast.11, bf16[8,64,128]{2,1,0:T(8,128)(2,1)} %w_ref.3), custom_call_target="tpu_custom_call" | custom-call | flops 536870912 | bytes 5373952 | tf_op jit(solution)/shard_map/pallas_call | solution.py:228
  38.7 0.0 collective-permute-done.3.refs_4_
  38.7 0.0 collective-permute-done.4.refs_5_
  38.7 0.0 copy-start.13
  38.7 0.0 collective-permute-done.5.refs_6_
  38.7 0.0 copy-start.14
  38.7 2.0 %collective-permute-done.6.refs_7_ = bf16[512,128]{1,0:T(8,128)(2,1)S(1)} collective-permute-done((bf16[512,128]{1,0:T(8,128)(2,1)}, bf16[512,128]{1,0:T(8,128)(2,1)S(1)}, u32[]{:S(2)}, u32[]{:S(2)}) %collective-permute-start.6) | collective-permute-done | bytes 131104 | tf_op jit(solution)/shard_map/ppermute | solution.py:254
  40.7 1.3 %collective-permute-done.7.refs_8_ = bf16[512,128]{1,0:T(8,128)(2,1)S(1)} collective-permute-done((bf16[512,128]{1,0:T(8,128)(2,1)}, bf16[512,128]{1,0:T(8,128)(2,1)S(1)}, u32[]{:S(2)}, u32[]{:S(2)}) %collective-permute-start.7) | collective-permute-done | bytes 131104 | tf_op jit(solution)/shard_map/ppermute | solution.py:254
  42.0 0.0 copy-done.9
  42.0 0.0 copy-done.10
  42.0 0.0 copy-done.11
  42.0 0.0 copy-done.12
  42.0 0.0 copy-done.13
  42.1 0.0 copy-done.14
  42.1 0.0 copy-done.15
  42.1 0.6 copy-done.16
  42.7 6.0 %shard_map.75 = (bf16[128,4096]{1,0:T(8,128)(2,1)}, bf16[128,512]{1,0:T(8,128)(2,1)}, bf16[128,512]{1,0:T(8,128)(2,1)}, bf16[128,512]{1,0:T(8,128)(2,1)}, bf16[1...) custom-call(s32[64]{0:T(128)} %and_select_fusion.cw_ref, ...), custom_call_target="tpu_custom_call" | custom-call | flops 536870912 | bytes 4194304 | tf_op jit(solution)/shard_map/pallas_call | solution.py:277
  48.7 0.0 collective-permute-start.8
  48.7 2.5 %collective-permute-start.9 = (bf16[128,512]{1,0:T(8,128)(2,1)}, bf16[128,512]{1,0:T(8,128)(2,1)S(1)}, u32[]{:S(2)}, u32[]{:S(2)}) collective-permute-start(bf16[128,512]{1,0:T(8,128)(2,1)} %get-tuple-element.32), channel_id=1, source_target_pairs={{120,0},{121,1},{122,2},{123,3},{124,4},{125,5},{126,6},{127,7},{0... | collective-permute-start | bytes 393224 | tf_op jit(solution)/shard_map/ppermute | solution.py:280
  51.1 0.0 collective-permute-start.10
  51.1 0.1 collective-permute-start.11
  51.3 1.6 %collective-permute-start.12 = (bf16[128,512]{1,0:T(8,128)(2,1)}, bf16[128,512]{1,0:T(8,128)(2,1)S(1)}, u32[]{:S(2)}, u32[]{:S(2)}) collective-permute-start(bf16[128,512]{1,0:T(8,128)(2,1)} %get-tuple-element.35), channel_id=1, source_target_pairs={{1,0},{2,1},{3,2},{4,3},{5,4},{6,5},{7,6},{0,7},{9,8},{10,9},{11,1... | collective-permute-start | bytes 393224 | tf_op jit(solution)/shard_map/ppermute | solution.py:280
  52.9 6.9 %collective-permute-done.8.refs_1_ = bf16[128,512]{1,0:T(8,128)(2,1)S(1)} collective-permute-done((bf16[128,512]{1,0:T(8,128)(2,1)}, bf16[128,512]{1,0:T(8,128)(2,1)S(1)}, u32[]{:S(2)}, u32[]{:S(2)}) %collective-permute-start.8) | collective-permute-done | bytes 131104 | tf_op jit(solution)/shard_map/ppermute | solution.py:280
  59.8 0.3 collective-permute-start.13
  60.1 0.3 collective-permute-done.9.refs_2_
  60.4 2.2 %collective-permute-start.14 = (bf16[128,512]{1,0:T(8,128)(2,1)}, bf16[128,512]{1,0:T(8,128)(2,1)S(1)}, u32[]{:S(2)}, u32[]{:S(2)}) collective-permute-start(bf16[128,512]{1,0:T(8,128)(2,1)} %get-tuple-element.37), channel_id=1, source_target_pairs={{8,0},{9,1},{10,2},{11,3},{12,4},{13,5},{14,6},{15,7},{16,8},{17,9... | collective-permute-start | bytes 393224 | tf_op jit(solution)/shard_map/ppermute | solution.py:280
  62.6 2.7 %collective-permute-done.10.refs_3_ = bf16[128,512]{1,0:T(8,128)(2,1)S(1)} collective-permute-done((bf16[128,512]{1,0:T(8,128)(2,1)}, bf16[128,512]{1,0:T(8,128)(2,1)S(1)}, u32[]{:S(2)}, u32[]{:S(2)}) %collective-permute-start.10) | collective-permute-done | bytes 131104 | tf_op jit(solution)/shard_map/ppermute | solution.py:280
  65.3 0.4 collective-permute-start.15
  65.7 0.0 collective-permute-done.11.refs_4_
  65.7 0.0 collective-permute-done.12.refs_5_
  65.7 0.0 copy-start.4
  65.7 0.0 collective-permute-done.13.refs_6_
  65.7 0.0 copy-start.5
  65.7 1.1 %collective-permute-done.14.refs_7_ = bf16[128,512]{1,0:T(8,128)(2,1)S(1)} collective-permute-done((bf16[128,512]{1,0:T(8,128)(2,1)}, bf16[128,512]{1,0:T(8,128)(2,1)S(1)}, u32[]{:S(2)}, u32[]{:S(2)}) %collective-permute-start.14) | collective-permute-done | bytes 131104 | tf_op jit(solution)/shard_map/ppermute | solution.py:280
  66.8 6.1 %collective-permute-done.15.refs_8_ = bf16[128,512]{1,0:T(8,128)(2,1)S(1)} collective-permute-done((bf16[128,512]{1,0:T(8,128)(2,1)}, bf16[128,512]{1,0:T(8,128)(2,1)S(1)}, u32[]{:S(2)}, u32[]{:S(2)}) %collective-permute-start.15) | collective-permute-done | bytes 131104 | tf_op jit(solution)/shard_map/ppermute | solution.py:280
  72.9 0.6 copy-done.7
  73.5 11.2 %shard_map.76 = bf16[64,32768]{1,0:T(8,128)(2,1)} custom-call(s32[256]{0:T(256)} %and_select_fusion.1.win_ref, s32[256]{0:T(256)} %off_ref.5, bf16[64,32768]{1,0:T(8,128)(2,1)} %bitcast.8, s32[256,128]{1,0:T(8,128)} %bitcast.12, bf16[8,64,128]{2,1,0:T(8,128)(2,1)} %bitcast.13, bf16[128,4096]{1,0:T(8,128)(2,1)} %get-tuple-element.30.refs_0_, ...), custom_call_target="tpu_custom_call" | custom-call | flops 1610612736 | bytes 10616832 | tf_op jit(solution)/shard_map/pallas_call | solution.py:308
  (23 shorter events, 0.1 us)
Async XLA Ops:
  0.0 23.8 %copy-start.8 = (s32[1,8192]{1,0:T(1,128)S(1)}, s32[1,8192]{1,0:T(1,128)}, u32[]{:S(2)}) copy-start(s32[1,8192]{1,0:T(1,128)} %param.10) | copy-start | bytes 98308
  2.6 1.4 %copy-start.17 = (s32[4]{0:T(128)}, s32[4]{0:T(128)S(1)}, u32[]{:S(2)}) copy-start(s32[4]{0:T(128)S(1)} %convert_reduce_fusion.count_ref) | copy-start | bytes 52
  14.5 9.4 %collective-permute-start = (bf16[512,128]{1,0:T(8,128)(2,1)}, bf16[512,128]{1,0:T(8,128)(2,1)S(1)}, u32[]{:S(2)}, u32[]{:S(2)}) collective-permute-start(bf16[512,128]{1,0:T(8,128)(2,1)} %get-tuple-element.22), channel_id=1, source_target_pairs={{0,127},{1,120},{2,121},{3,122},{4,123},{5,124},{6,125},{7,126},{8... | collective-permute-start | bytes 393224 | tf_op jit(solution)/shard_map/ppermute | solution.py:254
  19.7 7.1 %collective-permute-start.1 = (bf16[512,128]{1,0:T(8,128)(2,1)}, bf16[512,128]{1,0:T(8,128)(2,1)S(1)}, u32[]{:S(2)}, u32[]{:S(2)}) collective-permute-start(bf16[512,128]{1,0:T(8,128)(2,1)} %get-tuple-element.23), channel_id=1, source_target_pairs={{0,120},{1,121},{2,122},{3,123},{4,124},{5,125},{6,126},{7,127},{8... | collective-permute-start | bytes 393224 | tf_op jit(solution)/shard_map/ppermute | solution.py:254
  20.6 8.9 %collective-permute-start.2 = (bf16[512,128]{1,0:T(8,128)(2,1)}, bf16[512,128]{1,0:T(8,128)(2,1)S(1)}, u32[]{:S(2)}, u32[]{:S(2)}) collective-permute-start(bf16[512,128]{1,0:T(8,128)(2,1)} %get-tuple-element.24), channel_id=1, source_target_pairs={{0,121},{1,122},{2,123},{3,124},{4,125},{5,126},{6,127},{7,120},{8... | collective-permute-start | bytes 393224 | tf_op jit(solution)/shard_map/ppermute | solution.py:254
  20.7 18.0 %collective-permute-start.3 = (bf16[512,128]{1,0:T(8,128)(2,1)}, bf16[512,128]{1,0:T(8,128)(2,1)S(1)}, u32[]{:S(2)}, u32[]{:S(2)}) collective-permute-start(bf16[512,128]{1,0:T(8,128)(2,1)} %get-tuple-element.25), channel_id=1, source_target_pairs={{0,7},{1,0},{2,1},{3,2},{4,3},{5,4},{6,5},{7,6},{8,15},{9,8},{10,9... | collective-permute-start | bytes 393224 | tf_op jit(solution)/shard_map/ppermute | solution.py:254
  23.6 15.1 %collective-permute-start.4 = (bf16[512,128]{1,0:T(8,128)(2,1)}, bf16[512,128]{1,0:T(8,128)(2,1)S(1)}, u32[]{:S(2)}, u32[]{:S(2)}) collective-permute-start(bf16[512,128]{1,0:T(8,128)(2,1)} %get-tuple-element.26), channel_id=1, source_target_pairs={{0,1},{1,2},{2,3},{3,4},{4,5},{5,6},{6,7},{7,0},{8,9},{9,10},{10,1... | collective-permute-start | bytes 393224 | tf_op jit(solution)/shard_map/ppermute | solution.py:254
  23.9 18.1 %copy-start.9 = (bf16[512,128]{1,0:T(8,128)(2,1)}, bf16[512,128]{1,0:T(8,128)(2,1)S(1)}, u32[]{:S(2)}) copy-start(bf16[512,128]{1,0:T(8,128)(2,1)S(1)} %collective-permute-done.refs_1_) | copy-start | bytes 393220
  23.9 14.8 %collective-permute-start.5 = (bf16[512,128]{1,0:T(8,128)(2,1)}, bf16[512,128]{1,0:T(8,128)(2,1)S(1)}, u32[]{:S(2)}, u32[]{:S(2)}) collective-permute-start(bf16[512,128]{1,0:T(8,128)(2,1)} %get-tuple-element.27), channel_id=1, source_target_pairs={{0,15},{1,8},{2,9},{3,10},{4,11},{5,12},{6,13},{7,14},{8,23},{9,16... | collective-permute-start | bytes 393224 | tf_op jit(solution)/shard_map/ppermute | solution.py:254
  26.8 15.2 %copy-start.10 = (bf16[512,128]{1,0:T(8,128)(2,1)}, bf16[512,128]{1,0:T(8,128)(2,1)S(1)}, u32[]{:S(2)}) copy-start(bf16[512,128]{1,0:T(8,128)(2,1)S(1)} %collective-permute-done.1.refs_2_) | copy-start | bytes 393220
  26.8 13.9 %collective-permute-start.6 = (bf16[512,128]{1,0:T(8,128)(2,1)}, bf16[512,128]{1,0:T(8,128)(2,1)S(1)}, u32[]{:S(2)}, u32[]{:S(2)}) collective-permute-start(bf16[512,128]{1,0:T(8,128)(2,1)} %get-tuple-element.28), channel_id=1, source_target_pairs={{0,8},{1,9},{2,10},{3,11},{4,12},{5,13},{6,14},{7,15},{8,16},{9,17... | collective-permute-start | bytes 393224 | tf_op jit(solution)/shard_map/ppermute | solution.py:254
  29.4 12.6 %copy-start.11 = (bf16[512,128]{1,0:T(8,128)(2,1)}, bf16[512,128]{1,0:T(8,128)(2,1)S(1)}, u32[]{:S(2)}) copy-start(bf16[512,128]{1,0:T(8,128)(2,1)S(1)} %collective-permute-done.2.refs_3_) | copy-start | bytes 393220
  29.4 12.6 %collective-permute-start.7 = (bf16[512,128]{1,0:T(8,128)(2,1)}, bf16[512,128]{1,0:T(8,128)(2,1)S(1)}, u32[]{:S(2)}, u32[]{:S(2)}) collective-permute-start(bf16[512,128]{1,0:T(8,128)(2,1)} %get-tuple-element.29), channel_id=1, source_target_pairs={{0,9},{1,10},{2,11},{3,12},{4,13},{5,14},{6,15},{7,8},{8,17},{9,18... | collective-permute-start | bytes 393224 | tf_op jit(solution)/shard_map/ppermute | solution.py:254
  38.7 3.4 %copy-start.12 = (bf16[512,128]{1,0:T(8,128)(2,1)}, bf16[512,128]{1,0:T(8,128)(2,1)S(1)}, u32[]{:S(2)}) copy-start(bf16[512,128]{1,0:T(8,128)(2,1)S(1)} %collective-permute-done.3.refs_4_) | copy-start | bytes 393220
  38.7 3.4 %copy-start.13 = (bf16[512,128]{1,0:T(8,128)(2,1)}, bf16[512,128]{1,0:T(8,128)(2,1)S(1)}, u32[]{:S(2)}) copy-start(bf16[512,128]{1,0:T(8,128)(2,1)S(1)} %collective-permute-done.4.refs_5_) | copy-start | bytes 393220
  38.7 3.3 %copy-start.14 = (bf16[512,128]{1,0:T(8,128)(2,1)}, bf16[512,128]{1,0:T(8,128)(2,1)S(1)}, u32[]{:S(2)}) copy-start(bf16[512,128]{1,0:T(8,128)(2,1)S(1)} %collective-permute-done.5.refs_6_) | copy-start | bytes 393220
  40.7 1.4 %copy-start.15 = (bf16[512,128]{1,0:T(8,128)(2,1)}, bf16[512,128]{1,0:T(8,128)(2,1)S(1)}, u32[]{:S(2)}) copy-start(bf16[512,128]{1,0:T(8,128)(2,1)S(1)} %collective-permute-done.6.refs_7_) | copy-start | bytes 393220
  42.0 0.6 copy-start.16
  48.7 11.2 %collective-permute-start.8 = (bf16[128,512]{1,0:T(8,128)(2,1)}, bf16[128,512]{1,0:T(8,128)(2,1)S(1)}, u32[]{:S(2)}, u32[]{:S(2)}) collective-permute-start(bf16[128,512]{1,0:T(8,128)(2,1)} %get-tuple-element.31), channel_id=1, source_target_pairs={{127,0},{120,1},{121,2},{122,3},{123,4},{124,5},{125,6},{126,7},{7... | collective-permute-start | bytes 393224 | tf_op jit(solution)/shard_map/ppermute | solution.py:280
  48.7 11.7 %collective-permute-start.9 = (bf16[128,512]{1,0:T(8,128)(2,1)}, bf16[128,512]{1,0:T(8,128)(2,1)S(1)}, u32[]{:S(2)}, u32[]{:S(2)}) collective-permute-start(bf16[128,512]{1,0:T(8,128)(2,1)} %get-tuple-element.32), channel_id=1, source_target_pairs={{120,0},{121,1},{122,2},{123,3},{124,4},{125,5},{126,6},{127,7},{0... | collective-permute-start | bytes 393224 | tf_op jit(solution)/shard_map/ppermute | solution.py:280
  51.1 14.1 %collective-permute-start.10 = (bf16[128,512]{1,0:T(8,128)(2,1)}, bf16[128,512]{1,0:T(8,128)(2,1)S(1)}, u32[]{:S(2)}, u32[]{:S(2)}) collective-permute-start(bf16[128,512]{1,0:T(8,128)(2,1)} %get-tuple-element.33), channel_id=1, source_target_pairs={{121,0},{122,1},{123,2},{124,3},{125,4},{126,5},{127,6},{120,7},{1... | collective-permute-start | bytes 393224 | tf_op jit(solution)/shard_map/ppermute | solution.py:280
  51.1 14.5 %collective-permute-start.11 = (bf16[128,512]{1,0:T(8,128)(2,1)}, bf16[128,512]{1,0:T(8,128)(2,1)S(1)}, u32[]{:S(2)}, u32[]{:S(2)}) collective-permute-start(bf16[128,512]{1,0:T(8,128)(2,1)} %get-tuple-element.34), channel_id=1, source_target_pairs={{7,0},{0,1},{1,2},{2,3},{3,4},{4,5},{5,6},{6,7},{15,8},{8,9},{9,10... | collective-permute-start | bytes 393224 | tf_op jit(solution)/shard_map/ppermute | solution.py:280
  51.3 14.4 %collective-permute-start.12 = (bf16[128,512]{1,0:T(8,128)(2,1)}, bf16[128,512]{1,0:T(8,128)(2,1)S(1)}, u32[]{:S(2)}, u32[]{:S(2)}) collective-permute-start(bf16[128,512]{1,0:T(8,128)(2,1)} %get-tuple-element.35), channel_id=1, source_target_pairs={{1,0},{2,1},{3,2},{4,3},{5,4},{6,5},{7,6},{0,7},{9,8},{10,9},{11,1... | collective-permute-start | bytes 393224 | tf_op jit(solution)/shard_map/ppermute | solution.py:280
  59.8 13.1 %copy-start = (bf16[128,512]{1,0:T(8,128)(2,1)}, bf16[128,512]{1,0:T(8,128)(2,1)S(1)}, u32[]{:S(2)}) copy-start(bf16[128,512]{1,0:T(8,128)(2,1)S(1)} %collective-permute-done.8.refs_1_) | copy-start | bytes 393220
  59.8 5.9 %collective-permute-start.13 = (bf16[128,512]{1,0:T(8,128)(2,1)}, bf16[128,512]{1,0:T(8,128)(2,1)S(1)}, u32[]{:S(2)}, u32[]{:S(2)}) collective-permute-start(bf16[128,512]{1,0:T(8,128)(2,1)} %get-tuple-element.36), channel_id=1, source_target_pairs={{15,0},{8,1},{9,2},{10,3},{11,4},{12,5},{13,6},{14,7},{23,8},{16,9... | collective-permute-start | bytes 393224 | tf_op jit(solution)/shard_map/ppermute | solution.py:280
  60.4 12.5 %copy-start.1 = (bf16[128,512]{1,0:T(8,128)(2,1)}, bf16[128,512]{1,0:T(8,128)(2,1)S(1)}, u32[]{:S(2)}) copy-start(bf16[128,512]{1,0:T(8,128)(2,1)S(1)} %collective-permute-done.9.refs_2_) | copy-start | bytes 393220
  60.4 6.4 %collective-permute-start.14 = (bf16[128,512]{1,0:T(8,128)(2,1)}, bf16[128,512]{1,0:T(8,128)(2,1)S(1)}, u32[]{:S(2)}, u32[]{:S(2)}) collective-permute-start(bf16[128,512]{1,0:T(8,128)(2,1)} %get-tuple-element.37), channel_id=1, source_target_pairs={{8,0},{9,1},{10,2},{11,3},{12,4},{13,5},{14,6},{15,7},{16,8},{17,9... | collective-permute-start | bytes 393224 | tf_op jit(solution)/shard_map/ppermute | solution.py:280
  65.3 7.6 %copy-start.2 = (bf16[128,512]{1,0:T(8,128)(2,1)}, bf16[128,512]{1,0:T(8,128)(2,1)S(1)}, u32[]{:S(2)}) copy-start(bf16[128,512]{1,0:T(8,128)(2,1)S(1)} %collective-permute-done.10.refs_3_) | copy-start | bytes 393220
  65.3 7.6 %collective-permute-start.15 = (bf16[128,512]{1,0:T(8,128)(2,1)}, bf16[128,512]{1,0:T(8,128)(2,1)S(1)}, u32[]{:S(2)}, u32[]{:S(2)}) collective-permute-start(bf16[128,512]{1,0:T(8,128)(2,1)} %get-tuple-element.38), channel_id=1, source_target_pairs={{9,0},{10,1},{11,2},{12,3},{13,4},{14,5},{15,6},{8,7},{17,8},{18,9... | collective-permute-start | bytes 393224 | tf_op jit(solution)/shard_map/ppermute | solution.py:280
  65.7 7.2 %copy-start.3 = (bf16[128,512]{1,0:T(8,128)(2,1)}, bf16[128,512]{1,0:T(8,128)(2,1)S(1)}, u32[]{:S(2)}) copy-start(bf16[128,512]{1,0:T(8,128)(2,1)S(1)} %collective-permute-done.11.refs_4_) | copy-start | bytes 393220
  65.7 7.2 %copy-start.4 = (bf16[128,512]{1,0:T(8,128)(2,1)}, bf16[128,512]{1,0:T(8,128)(2,1)S(1)}, u32[]{:S(2)}) copy-start(bf16[128,512]{1,0:T(8,128)(2,1)S(1)} %collective-permute-done.12.refs_5_) | copy-start | bytes 393220
  65.7 7.2 %copy-start.5 = (bf16[128,512]{1,0:T(8,128)(2,1)}, bf16[128,512]{1,0:T(8,128)(2,1)S(1)}, u32[]{:S(2)}) copy-start(bf16[128,512]{1,0:T(8,128)(2,1)S(1)} %collective-permute-done.13.refs_6_) | copy-start | bytes 393220
  66.8 6.1 %copy-start.6 = (bf16[128,512]{1,0:T(8,128)(2,1)}, bf16[128,512]{1,0:T(8,128)(2,1)S(1)}, u32[]{:S(2)}) copy-start(bf16[128,512]{1,0:T(8,128)(2,1)S(1)} %collective-permute-done.14.refs_7_) | copy-start | bytes 393220
  72.9 0.7 copy-start.7

commit v2 on v0

--- a/solution.py
+++ b/solution.py
@@ -11,7 +11,7 @@
 C_DEV = 4096
 SELF_CAP = 4096
 WIN = 128
-BRICKS_PER_STEP = 64
+BRICKS_PER_STEP = 128
 UNROLL = 16
 UP_UNROLL = 32
 WIN_UNROLL = 16

time: 84.1 us -> 83.2 us (0.989)
  starting transfers between devices: 18.3 us -> 16.6 us
    ppermute x8, waiting for transfers between devices: 6.76 us -> 8.1 us  [local(): lax.ppermute(parts[1 + g], ('outer', 'inner'), group_route(g, 1))]
    ppermute x8, starting transfers between devices: 7.42 us -> 6.26 us  [local(): lax.ppermute(answers[1 + g], ('outer', 'inner'), group_route(g, -1))]
    pallas_call x2, Pallas kernels: 19.1 us -> 18.3 us  [down_call(): pl.pallas_call(functools.partial(down_kernel, first_window), out_shape=sh...]
where the time goes in v2:
time: 83.2 us; the launch traced here: 82.4 us
  Pallas kernels  36.2 us (44%)
  waiting for transfers between devices  24.3 us (29%)
  starting transfers between devices  16.6 us (20%)
  other arithmetic  2.87 us (3%)
  local copies, waits for them, and re-layouts  2.27 us (3%)
    pallas_call x2, Pallas kernels, down_call(): pl.pallas_call(functools.partial(down_kernel, first_window), out_shape=sh...  18.3 us
    ppermute x8, waiting for transfers between devices, local(): lax.ppermute(answers[1 + g], ('outer', 'inner'), group_route(g, -1))  16.2 us
    pallas_call x1, Pallas kernels, local(): up(brick_window, block_offset, xt, entry_rows, w_up_t, answers[0], *retur...  11.9 us
    ppermute x8, starting transfers between devices, local(): lax.ppermute(parts[1 + g], ('outer', 'inner'), group_route(g, 1))  10.3 us
    ppermute x8, waiting for transfers between devices, local(): lax.ppermute(parts[1 + g], ('outer', 'inner'), group_route(g, 1))  8.1 us
    ppermute x8, starting transfers between devices, local(): lax.ppermute(answers[1 + g], ('outer', 'inner'), group_route(g, -1))  6.26 us
    pallas_call x1, Pallas kernels, local(): coarse(cell_window, cells, b_down.reshape(1, out_width), parts[0], *arrived)  6 us
  transfers between devices with their start and end apart: 16, of which 11 were waited for; matrix products, arithmetic and copies ran while one was open for 1% of the time, Pallas kernels for 11%

profile of v2, /device:TPU:24, one launch (start us, length us, event | category | flops | bytes accessed | tf_op | source)
XLA Modules:
  0.0 82.4 jit_solution(6647198362309974870)
XLA Ops:
  0.0 1.0 %slice_reduce_fusion = s32[256]{0:T(256)S(1)} fusion(s32[256,128]{1,0:T(8,128)} %bitcast.26), kind=kLoop, calls=%fused_computation | loop fusion | bytes 2048 | tf_op jit(solution)/shard_map/slice | solution.py:199
  1.0 0.6 and_select_fusion.2.win_ref
  1.6 0.1 broadcast_subtract_fusion
  1.8 0.3 reduce_window_sum.17
  2.1 0.3 reduce_window_sum.18
  2.4 0.1 compare_select_fusion
  2.5 0.7 select_reduce_fusion
  3.1 0.0 copy-done.17
  3.1 9.4 %shard_map.74 = (bf16[512,128]{1,0:T(8,128)(2,1)}, bf16[512,128]{1,0:T(8,128)(2,1)}, bf16[512,128]{1,0:T(8,128)(2,1)}, bf16[512,128]{1,0:T(8,128)(2,1)}, bf16[51...) custom-call(s32[2]{0:T(128)} %copy-done.17, s32[256]{0:T(256)} %bitcast.33, ...), custom_call_target="tpu_custom_call" | custom-call | flops 536870912 | bytes 5373952 | tf_op jit(solution)/shard_map/pallas_call | solution.py:224
  12.6 5.9 %collective-permute-start = (bf16[512,128]{1,0:T(8,128)(2,1)}, bf16[512,128]{1,0:T(8,128)(2,1)S(1)}, u32[]{:S(2)}, u32[]{:S(2)}) collective-permute-start(bf16[512,128]{1,0:T(8,128)(2,1)} %get-tuple-element.22), channel_id=1, source_target_pairs={{0,127},{1,120},{2,121},{3,122},{4,123},{5,124},{6,125},{7,126},{8... | collective-permute-start | bytes 393224 | tf_op jit(solution)/shard_map/ppermute | solution.py:250
  18.4 0.4 collective-permute-start.1
  18.9 0.7 collective-permute-start.2
  19.6 1.4 %collective-permute-start.3 = (bf16[512,128]{1,0:T(8,128)(2,1)}, bf16[512,128]{1,0:T(8,128)(2,1)S(1)}, u32[]{:S(2)}, u32[]{:S(2)}) collective-permute-start(bf16[512,128]{1,0:T(8,128)(2,1)} %get-tuple-element.25), channel_id=1, source_target_pairs={{0,7},{1,0},{2,1},{3,2},{4,3},{5,4},{6,5},{7,6},{8,15},{9,8},{10,9... | collective-permute-start | bytes 393224 | tf_op jit(solution)/shard_map/ppermute | solution.py:250
  21.0 0.9 %collective-permute-start.4 = (bf16[512,128]{1,0:T(8,128)(2,1)}, bf16[512,128]{1,0:T(8,128)(2,1)S(1)}, u32[]{:S(2)}, u32[]{:S(2)}) collective-permute-start(bf16[512,128]{1,0:T(8,128)(2,1)} %get-tuple-element.26), channel_id=1, source_target_pairs={{0,1},{1,2},{2,3},{3,4},{4,5},{5,6},{6,7},{7,0},{8,9},{9,10},{10,1... | collective-permute-start | bytes 393224 | tf_op jit(solution)/shard_map/ppermute | solution.py:250
  21.9 0.0 copy-done.8
  21.9 0.1 reduce_min.9
  22.0 0.7 collective-permute-done.refs_1_
  22.7 1.1 %collective-permute-start.5 = (bf16[512,128]{1,0:T(8,128)(2,1)}, bf16[512,128]{1,0:T(8,128)(2,1)S(1)}, u32[]{:S(2)}, u32[]{:S(2)}) collective-permute-start(bf16[512,128]{1,0:T(8,128)(2,1)} %get-tuple-element.27), channel_id=1, source_target_pairs={{0,15},{1,8},{2,9},{3,10},{4,11},{5,12},{6,13},{7,14},{8,23},{9,16... | collective-permute-start | bytes 393224 | tf_op jit(solution)/shard_map/ppermute | solution.py:250
  23.7 1.8 %collective-permute-done.1.refs_2_ = bf16[512,128]{1,0:T(8,128)(2,1)S(1)} collective-permute-done((bf16[512,128]{1,0:T(8,128)(2,1)}, bf16[512,128]{1,0:T(8,128)(2,1)S(1)}, u32[]{:S(2)}, u32[]{:S(2)}) %collective-permute-start.1) | collective-permute-done | bytes 131104 | tf_op jit(solution)/shard_map/ppermute | solution.py:250
  25.5 0.0 collective-permute-start.6
  25.5 2.6 %collective-permute-done.2.refs_3_ = bf16[512,128]{1,0:T(8,128)(2,1)S(1)} collective-permute-done((bf16[512,128]{1,0:T(8,128)(2,1)}, bf16[512,128]{1,0:T(8,128)(2,1)S(1)}, u32[]{:S(2)}, u32[]{:S(2)}) %collective-permute-start.2) | collective-permute-done | bytes 131104 | tf_op jit(solution)/shard_map/ppermute | solution.py:250
  28.1 0.0 collective-permute-start.7
  28.1 0.6 and_select_fusion.1.cw_ref
  28.8 8.8 %shard_map.73.refs_0_ = bf16[4096,128]{1,0:T(8,128)(2,1)} custom-call(s32[2]{0:T(128)} %copy-done.17, s32[256]{0:T(256)} %bitcast.34, s32[256]{0:T(256)} %and_select_fusion.2.win_ref, s32[256]{0:T(256)} %off_ref.5, bf16[64,32768]{1,0:T(8,128)(2,1)} %bitcast.24, s32[256,128]{1,0:T(8,128)} %bitcast.28, bf16[8,64,128]{2,1,0:T(8,128)(2,1)} %w_ref.3), custom_call_target="tpu_custom_call" | custom-call | flops 536870912 | bytes 5373952 | tf_op jit(solution)/shard_map/pallas_call | solution.py:224
  37.6 0.0 collective-permute-done.3.refs_4_
  37.6 0.0 collective-permute-done.4.refs_5_
  37.6 0.0 copy-start.13
  37.6 0.0 collective-permute-done.5.refs_6_
  37.6 0.0 copy-start.14
  37.6 0.2 collective-permute-done.6.refs_7_
  37.9 2.8 %collective-permute-done.7.refs_8_ = bf16[512,128]{1,0:T(8,128)(2,1)S(1)} collective-permute-done((bf16[512,128]{1,0:T(8,128)(2,1)}, bf16[512,128]{1,0:T(8,128)(2,1)S(1)}, u32[]{:S(2)}, u32[]{:S(2)}) %collective-permute-start.7) | collective-permute-done | bytes 131104 | tf_op jit(solution)/shard_map/ppermute | solution.py:250
  40.7 0.0 copy-done.9
  40.7 0.0 copy-done.10
  40.7 0.0 copy-done.11
  40.7 0.0 copy-done.12
  40.7 0.0 copy-done.13
  40.7 0.0 copy-done.14
  40.7 0.0 copy-done.15
  40.7 0.6 copy-done.16
  41.3 6.0 %shard_map.75 = (bf16[128,4096]{1,0:T(8,128)(2,1)}, bf16[128,512]{1,0:T(8,128)(2,1)}, bf16[128,512]{1,0:T(8,128)(2,1)}, bf16[128,512]{1,0:T(8,128)(2,1)}, bf16[1...) custom-call(s32[64]{0:T(128)} %and_select_fusion.1.cw_ref, ...), custom_call_target="tpu_custom_call" | custom-call | flops 536870912 | bytes 4194304 | tf_op jit(solution)/shard_map/pallas_call | solution.py:273
  47.3 0.0 collective-permute-start.8
  47.3 2.7 %collective-permute-start.9 = (bf16[128,512]{1,0:T(8,128)(2,1)}, bf16[128,512]{1,0:T(8,128)(2,1)S(1)}, u32[]{:S(2)}, u32[]{:S(2)}) collective-permute-start(bf16[128,512]{1,0:T(8,128)(2,1)} %get-tuple-element.32), channel_id=1, source_target_pairs={{120,0},{121,1},{122,2},{123,3},{124,4},{125,5},{126,6},{127,7},{0... | collective-permute-start | bytes 393224 | tf_op jit(solution)/shard_map/ppermute | solution.py:276
  50.0 0.0 collective-permute-start.10
  50.0 0.1 collective-permute-start.11
  50.1 1.6 %collective-permute-start.12 = (bf16[128,512]{1,0:T(8,128)(2,1)}, bf16[128,512]{1,0:T(8,128)(2,1)S(1)}, u32[]{:S(2)}, u32[]{:S(2)}) collective-permute-start(bf16[128,512]{1,0:T(8,128)(2,1)} %get-tuple-element.35), channel_id=1, source_target_pairs={{1,0},{2,1},{3,2},{4,3},{5,4},{6,5},{7,6},{0,7},{9,8},{10,9},{11,1... | collective-permute-start | bytes 393224 | tf_op jit(solution)/shard_map/ppermute | solution.py:276
  51.7 6.0 %collective-permute-done.8.refs_1_ = bf16[128,512]{1,0:T(8,128)(2,1)S(1)} collective-permute-done((bf16[128,512]{1,0:T(8,128)(2,1)}, bf16[128,512]{1,0:T(8,128)(2,1)S(1)}, u32[]{:S(2)}, u32[]{:S(2)}) %collective-permute-start.8) | collective-permute-done | bytes 131104 | tf_op jit(solution)/shard_map/ppermute | solution.py:276
  57.7 0.0 collective-permute-start.13
  57.7 1.3 %collective-permute-done.9.refs_2_ = bf16[128,512]{1,0:T(8,128)(2,1)S(1)} collective-permute-done((bf16[128,512]{1,0:T(8,128)(2,1)}, bf16[128,512]{1,0:T(8,128)(2,1)S(1)}, u32[]{:S(2)}, u32[]{:S(2)}) %collective-permute-start.9) | collective-permute-done | bytes 131104 | tf_op jit(solution)/shard_map/ppermute | solution.py:276
  59.0 1.6 %collective-permute-start.14 = (bf16[128,512]{1,0:T(8,128)(2,1)}, bf16[128,512]{1,0:T(8,128)(2,1)S(1)}, u32[]{:S(2)}, u32[]{:S(2)}) collective-permute-start(bf16[128,512]{1,0:T(8,128)(2,1)} %get-tuple-element.37), channel_id=1, source_target_pairs={{8,0},{9,1},{10,2},{11,3},{12,4},{13,5},{14,6},{15,7},{16,8},{17,9... | collective-permute-start | bytes 393224 | tf_op jit(solution)/shard_map/ppermute | solution.py:276
  60.6 1.8 %collective-permute-done.10.refs_3_ = bf16[128,512]{1,0:T(8,128)(2,1)S(1)} collective-permute-done((bf16[128,512]{1,0:T(8,128)(2,1)}, bf16[128,512]{1,0:T(8,128)(2,1)S(1)}, u32[]{:S(2)}, u32[]{:S(2)}) %collective-permute-start.10) | collective-permute-done | bytes 131104 | tf_op jit(solution)/shard_map/ppermute | solution.py:276
  62.4 0.2 collective-permute-start.15
  62.7 0.0 collective-permute-done.11.refs_4_
  62.7 0.0 collective-permute-done.12.refs_5_
  62.7 0.0 copy-start.4
  62.7 1.6 %collective-permute-done.13.refs_6_ = bf16[128,512]{1,0:T(8,128)(2,1)S(1)} collective-permute-done((bf16[128,512]{1,0:T(8,128)(2,1)}, bf16[128,512]{1,0:T(8,128)(2,1)S(1)}, u32[]{:S(2)}, u32[]{:S(2)}) %collective-permute-start.13) | collective-permute-done | bytes 131104 | tf_op jit(solution)/shard_map/ppermute | solution.py:276
  64.3 0.4 collective-permute-done.14.refs_7_
  64.8 5.1 %collective-permute-done.15.refs_8_ = bf16[128,512]{1,0:T(8,128)(2,1)S(1)} collective-permute-done((bf16[128,512]{1,0:T(8,128)(2,1)}, bf16[128,512]{1,0:T(8,128)(2,1)S(1)}, u32[]{:S(2)}, u32[]{:S(2)}) %collective-permute-start.15) | collective-permute-done | bytes 131104 | tf_op jit(solution)/shard_map/ppermute | solution.py:276
  69.8 0.0 copy-done
  69.8 0.0 copy-done.1
  69.8 0.0 copy-done.2
  69.8 0.0 copy-done.3
  69.9 0.0 copy-done.4
  69.9 0.6 copy-done.7
  70.5 11.9 %shard_map.76 = bf16[64,32768]{1,0:T(8,128)(2,1)} custom-call(s32[256]{0:T(256)} %and_select_fusion.2.win_ref, s32[256]{0:T(256)} %off_ref.5, bf16[64,32768]{1,0:T(8,128)(2,1)} %bitcast.25, s32[256,128]{1,0:T(8,128)} %bitcast.29, bf16[8,64,128]{2,1,0:T(8,128)(2,1)} %bitcast.30, bf16[128,4096]{1,0:T(8,128)(2,1)} %get-tuple-element.30.refs_0_, ...), custom_call_target="tpu_custom_call" | custom-call | flops 1610612736 | bytes 10616832 | tf_op jit(solution)/shard_map/pallas_call | solution.py:304
  (18 shorter events, 0.0 us)
Async XLA Ops:
  0.0 21.9 %copy-start.8 = (s32[1,8192]{1,0:T(1,128)S(1)}, s32[1,8192]{1,0:T(1,128)}, u32[]{:S(2)}) copy-start(s32[1,8192]{1,0:T(1,128)} %param.10) | copy-start | bytes 98308
  1.8 1.4 %copy-start.17 = (s32[2]{0:T(128)}, s32[2]{0:T(128)S(1)}, u32[]{:S(2)}) copy-start(s32[2]{0:T(128)S(1)} %get-tuple-element.40.count_ref) | copy-start | bytes 28
  12.6 10.1 %collective-permute-start = (bf16[512,128]{1,0:T(8,128)(2,1)}, bf16[512,128]{1,0:T(8,128)(2,1)S(1)}, u32[]{:S(2)}, u32[]{:S(2)}) collective-permute-start(bf16[512,128]{1,0:T(8,128)(2,1)} %get-tuple-element.22), channel_id=1, source_target_pairs={{0,127},{1,120},{2,121},{3,122},{4,123},{5,124},{6,125},{7,126},{8... | collective-permute-start | bytes 393224 | tf_op jit(solution)/shard_map/ppermute | solution.py:250
  18.4 7.1 %collective-permute-start.1 = (bf16[512,128]{1,0:T(8,128)(2,1)}, bf16[512,128]{1,0:T(8,128)(2,1)S(1)}, u32[]{:S(2)}, u32[]{:S(2)}) collective-permute-start(bf16[512,128]{1,0:T(8,128)(2,1)} %get-tuple-element.23), channel_id=1, source_target_pairs={{0,120},{1,121},{2,122},{3,123},{4,124},{5,125},{6,126},{7,127},{8... | collective-permute-start | bytes 393224 | tf_op jit(solution)/shard_map/ppermute | solution.py:250
  18.9 9.2 %collective-permute-start.2 = (bf16[512,128]{1,0:T(8,128)(2,1)}, bf16[512,128]{1,0:T(8,128)(2,1)S(1)}, u32[]{:S(2)}, u32[]{:S(2)}) collective-permute-start(bf16[512,128]{1,0:T(8,128)(2,1)} %get-tuple-element.24), channel_id=1, source_target_pairs={{0,121},{1,122},{2,123},{3,124},{4,125},{5,126},{6,127},{7,120},{8... | collective-permute-start | bytes 393224 | tf_op jit(solution)/shard_map/ppermute | solution.py:250
  19.6 18.0 %collective-permute-start.3 = (bf16[512,128]{1,0:T(8,128)(2,1)}, bf16[512,128]{1,0:T(8,128)(2,1)S(1)}, u32[]{:S(2)}, u32[]{:S(2)}) collective-permute-start(bf16[512,128]{1,0:T(8,128)(2,1)} %get-tuple-element.25), channel_id=1, source_target_pairs={{0,7},{1,0},{2,1},{3,2},{4,3},{5,4},{6,5},{7,6},{8,15},{9,8},{10,9... | collective-permute-start | bytes 393224 | tf_op jit(solution)/shard_map/ppermute | solution.py:250
  21.0 16.6 %collective-permute-start.4 = (bf16[512,128]{1,0:T(8,128)(2,1)}, bf16[512,128]{1,0:T(8,128)(2,1)S(1)}, u32[]{:S(2)}, u32[]{:S(2)}) collective-permute-start(bf16[512,128]{1,0:T(8,128)(2,1)} %get-tuple-element.26), channel_id=1, source_target_pairs={{0,1},{1,2},{2,3},{3,4},{4,5},{5,6},{6,7},{7,0},{8,9},{9,10},{10,1... | collective-permute-start | bytes 393224 | tf_op jit(solution)/shard_map/ppermute | solution.py:250
  22.7 18.0 %copy-start.9 = (bf16[512,128]{1,0:T(8,128)(2,1)}, bf16[512,128]{1,0:T(8,128)(2,1)S(1)}, u32[]{:S(2)}) copy-start(bf16[512,128]{1,0:T(8,128)(2,1)S(1)} %collective-permute-done.refs_1_) | copy-start | bytes 393220
  22.7 15.0 %collective-permute-start.5 = (bf16[512,128]{1,0:T(8,128)(2,1)}, bf16[512,128]{1,0:T(8,128)(2,1)S(1)}, u32[]{:S(2)}, u32[]{:S(2)}) collective-permute-start(bf16[512,128]{1,0:T(8,128)(2,1)} %get-tuple-element.27), channel_id=1, source_target_pairs={{0,15},{1,8},{2,9},{3,10},{4,11},{5,12},{6,13},{7,14},{8,23},{9,16... | collective-permute-start | bytes 393224 | tf_op jit(solution)/shard_map/ppermute | solution.py:250
  25.5 15.1 %copy-start.10 = (bf16[512,128]{1,0:T(8,128)(2,1)}, bf16[512,128]{1,0:T(8,128)(2,1)S(1)}, u32[]{:S(2)}) copy-start(bf16[512,128]{1,0:T(8,128)(2,1)S(1)} %collective-permute-done.1.refs_2_) | copy-start | bytes 393220
  25.5 12.3 %collective-permute-start.6 = (bf16[512,128]{1,0:T(8,128)(2,1)}, bf16[512,128]{1,0:T(8,128)(2,1)S(1)}, u32[]{:S(2)}, u32[]{:S(2)}) collective-permute-start(bf16[512,128]{1,0:T(8,128)(2,1)} %get-tuple-element.28), channel_id=1, source_target_pairs={{0,8},{1,9},{2,10},{3,11},{4,12},{5,13},{6,14},{7,15},{8,16},{9,17... | collective-permute-start | bytes 393224 | tf_op jit(solution)/shard_map/ppermute | solution.py:250
  28.1 12.5 %copy-start.11 = (bf16[512,128]{1,0:T(8,128)(2,1)}, bf16[512,128]{1,0:T(8,128)(2,1)S(1)}, u32[]{:S(2)}) copy-start(bf16[512,128]{1,0:T(8,128)(2,1)S(1)} %collective-permute-done.2.refs_3_) | copy-start | bytes 393220
  28.1 12.5 %collective-permute-start.7 = (bf16[512,128]{1,0:T(8,128)(2,1)}, bf16[512,128]{1,0:T(8,128)(2,1)S(1)}, u32[]{:S(2)}, u32[]{:S(2)}) collective-permute-start(bf16[512,128]{1,0:T(8,128)(2,1)} %get-tuple-element.29), channel_id=1, source_target_pairs={{0,9},{1,10},{2,11},{3,12},{4,13},{5,14},{6,15},{7,8},{8,17},{9,18... | collective-permute-start | bytes 393224 | tf_op jit(solution)/shard_map/ppermute | solution.py:250
  37.6 3.1 %copy-start.12 = (bf16[512,128]{1,0:T(8,128)(2,1)}, bf16[512,128]{1,0:T(8,128)(2,1)S(1)}, u32[]{:S(2)}) copy-start(bf16[512,128]{1,0:T(8,128)(2,1)S(1)} %collective-permute-done.3.refs_4_) | copy-start | bytes 393220
  37.6 3.1 %copy-start.13 = (bf16[512,128]{1,0:T(8,128)(2,1)}, bf16[512,128]{1,0:T(8,128)(2,1)S(1)}, u32[]{:S(2)}) copy-start(bf16[512,128]{1,0:T(8,128)(2,1)S(1)} %collective-permute-done.4.refs_5_) | copy-start | bytes 393220
  37.6 3.1 %copy-start.14 = (bf16[512,128]{1,0:T(8,128)(2,1)}, bf16[512,128]{1,0:T(8,128)(2,1)S(1)}, u32[]{:S(2)}) copy-start(bf16[512,128]{1,0:T(8,128)(2,1)S(1)} %collective-permute-done.5.refs_6_) | copy-start | bytes 393220
  37.8 2.9 %copy-start.15 = (bf16[512,128]{1,0:T(8,128)(2,1)}, bf16[512,128]{1,0:T(8,128)(2,1)S(1)}, u32[]{:S(2)}) copy-start(bf16[512,128]{1,0:T(8,128)(2,1)S(1)} %collective-permute-done.6.refs_7_) | copy-start | bytes 393220
  40.7 0.6 copy-start.16
  47.3 10.4 %collective-permute-start.8 = (bf16[128,512]{1,0:T(8,128)(2,1)}, bf16[128,512]{1,0:T(8,128)(2,1)S(1)}, u32[]{:S(2)}, u32[]{:S(2)}) collective-permute-start(bf16[128,512]{1,0:T(8,128)(2,1)} %get-tuple-element.31), channel_id=1, source_target_pairs={{127,0},{120,1},{121,2},{122,3},{123,4},{124,5},{125,6},{126,7},{7... | collective-permute-start | bytes 393224 | tf_op jit(solution)/shard_map/ppermute | solution.py:276
  47.3 11.7 %collective-permute-start.9 = (bf16[128,512]{1,0:T(8,128)(2,1)}, bf16[128,512]{1,0:T(8,128)(2,1)S(1)}, u32[]{:S(2)}, u32[]{:S(2)}) collective-permute-start(bf16[128,512]{1,0:T(8,128)(2,1)} %get-tuple-element.32), channel_id=1, source_target_pairs={{120,0},{121,1},{122,2},{123,3},{124,4},{125,5},{126,6},{127,7},{0... | collective-permute-start | bytes 393224 | tf_op jit(solution)/shard_map/ppermute | solution.py:276
  50.0 12.5 %collective-permute-start.10 = (bf16[128,512]{1,0:T(8,128)(2,1)}, bf16[128,512]{1,0:T(8,128)(2,1)S(1)}, u32[]{:S(2)}, u32[]{:S(2)}) collective-permute-start(bf16[128,512]{1,0:T(8,128)(2,1)} %get-tuple-element.33), channel_id=1, source_target_pairs={{121,0},{122,1},{123,2},{124,3},{125,4},{126,5},{127,6},{120,7},{1... | collective-permute-start | bytes 393224 | tf_op jit(solution)/shard_map/ppermute | solution.py:276
  50.0 12.7 %collective-permute-start.11 = (bf16[128,512]{1,0:T(8,128)(2,1)}, bf16[128,512]{1,0:T(8,128)(2,1)S(1)}, u32[]{:S(2)}, u32[]{:S(2)}) collective-permute-start(bf16[128,512]{1,0:T(8,128)(2,1)} %get-tuple-element.34), channel_id=1, source_target_pairs={{7,0},{0,1},{1,2},{2,3},{3,4},{4,5},{5,6},{6,7},{15,8},{8,9},{9,10... | collective-permute-start | bytes 393224 | tf_op jit(solution)/shard_map/ppermute | solution.py:276
  50.1 12.5 %collective-permute-start.12 = (bf16[128,512]{1,0:T(8,128)(2,1)}, bf16[128,512]{1,0:T(8,128)(2,1)S(1)}, u32[]{:S(2)}, u32[]{:S(2)}) collective-permute-start(bf16[128,512]{1,0:T(8,128)(2,1)} %get-tuple-element.35), channel_id=1, source_target_pairs={{1,0},{2,1},{3,2},{4,3},{5,4},{6,5},{7,6},{0,7},{9,8},{10,9},{11,1... | collective-permute-start | bytes 393224 | tf_op jit(solution)/shard_map/ppermute | solution.py:276
  57.7 12.1 %copy-start = (bf16[128,512]{1,0:T(8,128)(2,1)}, bf16[128,512]{1,0:T(8,128)(2,1)S(1)}, u32[]{:S(2)}) copy-start(bf16[128,512]{1,0:T(8,128)(2,1)S(1)} %collective-permute-done.8.refs_1_) | copy-start | bytes 393220
  57.7 6.6 %collective-permute-start.13 = (bf16[128,512]{1,0:T(8,128)(2,1)}, bf16[128,512]{1,0:T(8,128)(2,1)S(1)}, u32[]{:S(2)}, u32[]{:S(2)}) collective-permute-start(bf16[128,512]{1,0:T(8,128)(2,1)} %get-tuple-element.36), channel_id=1, source_target_pairs={{15,0},{8,1},{9,2},{10,3},{11,4},{12,5},{13,6},{14,7},{23,8},{16,9... | collective-permute-start | bytes 393224 | tf_op jit(solution)/shard_map/ppermute | solution.py:276
  59.0 10.8 %copy-start.1 = (bf16[128,512]{1,0:T(8,128)(2,1)}, bf16[128,512]{1,0:T(8,128)(2,1)S(1)}, u32[]{:S(2)}) copy-start(bf16[128,512]{1,0:T(8,128)(2,1)S(1)} %collective-permute-done.9.refs_2_) | copy-start | bytes 393220
  59.0 5.7 %collective-permute-start.14 = (bf16[128,512]{1,0:T(8,128)(2,1)}, bf16[128,512]{1,0:T(8,128)(2,1)S(1)}, u32[]{:S(2)}, u32[]{:S(2)}) collective-permute-start(bf16[128,512]{1,0:T(8,128)(2,1)} %get-tuple-element.37), channel_id=1, source_target_pairs={{8,0},{9,1},{10,2},{11,3},{12,4},{13,5},{14,6},{15,7},{16,8},{17,9... | collective-permute-start | bytes 393224 | tf_op jit(solution)/shard_map/ppermute | solution.py:276
  62.4 7.4 %copy-start.2 = (bf16[128,512]{1,0:T(8,128)(2,1)}, bf16[128,512]{1,0:T(8,128)(2,1)S(1)}, u32[]{:S(2)}) copy-start(bf16[128,512]{1,0:T(8,128)(2,1)S(1)} %collective-permute-done.10.refs_3_) | copy-start | bytes 393220
  62.4 7.4 %collective-permute-start.15 = (bf16[128,512]{1,0:T(8,128)(2,1)}, bf16[128,512]{1,0:T(8,128)(2,1)S(1)}, u32[]{:S(2)}, u32[]{:S(2)}) collective-permute-start(bf16[128,512]{1,0:T(8,128)(2,1)} %get-tuple-element.38), channel_id=1, source_target_pairs={{9,0},{10,1},{11,2},{12,3},{13,4},{14,5},{15,6},{8,7},{17,8},{18,9... | collective-permute-start | bytes 393224 | tf_op jit(solution)/shard_map/ppermute | solution.py:276
  62.7 7.2 %copy-start.3 = (bf16[128,512]{1,0:T(8,128)(2,1)}, bf16[128,512]{1,0:T(8,128)(2,1)S(1)}, u32[]{:S(2)}) copy-start(bf16[128,512]{1,0:T(8,128)(2,1)S(1)} %collective-permute-done.11.refs_4_) | copy-start | bytes 393220
  62.7 7.2 %copy-start.4 = (bf16[128,512]{1,0:T(8,128)(2,1)}, bf16[128,512]{1,0:T(8,128)(2,1)S(1)}, u32[]{:S(2)}) copy-start(bf16[128,512]{1,0:T(8,128)(2,1)S(1)} %collective-permute-done.12.refs_5_) | copy-start | bytes 393220
  64.3 5.5 %copy-start.5 = (bf16[128,512]{1,0:T(8,128)(2,1)}, bf16[128,512]{1,0:T(8,128)(2,1)S(1)}, u32[]{:S(2)}) copy-start(bf16[128,512]{1,0:T(8,128)(2,1)S(1)} %collective-permute-done.13.refs_6_) | copy-start | bytes 393220
  64.8 5.1 %copy-start.6 = (bf16[128,512]{1,0:T(8,128)(2,1)}, bf16[128,512]{1,0:T(8,128)(2,1)S(1)}, u32[]{:S(2)}) copy-start(bf16[128,512]{1,0:T(8,128)(2,1)S(1)} %collective-permute-done.14.refs_7_) | copy-start | bytes 393220
  69.8 0.7 copy-start.7

commit v3 on v0

--- a/solution.py
+++ b/solution.py
@@ -13,8 +13,8 @@
 WIN = 128
 BRICKS_PER_STEP = 64
 UNROLL = 16
-UP_UNROLL = 32
-WIN_UNROLL = 16
+UP_UNROLL = 64
+WIN_UNROLL = 32
 
 step_table = ((-1, -1), (-1, 0), (-1, 1), (0, -1), (0, 1), (1, -1), (1, 0), (1, 1))
 

time: 84.1 us -> 82.1 us (0.976)
  Pallas kernels: 36.3 us -> 34.8 us
  waiting for transfers between devices: 23.8 us -> 22.6 us
  starting transfers between devices: 18.3 us -> 19.2 us
    ppermute x8, starting transfers between devices: 10.8 us -> 12.3 us  [local(): lax.ppermute(parts[1 + g], ('outer', 'inner'), group_route(g, 1))]
    ppermute x8, waiting for transfers between devices: 6.76 us -> 5.42 us  [local(): lax.ppermute(parts[1 + g], ('outer', 'inner'), group_route(g, 1))]
  transfers between devices with their start and end apart: 16 -> 16, of which waited for: 11 -> 7; matrix products, arithmetic and copies ran while one was open for 1% -> 1% of each run, Pallas kernels for 11% -> 11%
where the time goes in v3:
time: 82.1 us; the launch traced here: 82 us
  Pallas kernels  34.8 us (42%)
  waiting for transfers between devices  22.6 us (28%)
  starting transfers between devices  19.2 us (23%)
  local copies, waits for them, and re-layouts  3.02 us (4%)
  other arithmetic  2.2 us (3%)
    pallas_call x2, Pallas kernels, down_call(): pl.pallas_call(functools.partial(down_kernel, first_window), out_shape=sh...  19.1 us
    ppermute x8, waiting for transfers between devices, local(): lax.ppermute(answers[1 + g], ('outer', 'inner'), group_route(g, -1))  17.2 us
    ppermute x8, starting transfers between devices, local(): lax.ppermute(parts[1 + g], ('outer', 'inner'), group_route(g, 1))  12.3 us
    pallas_call x1, Pallas kernels, local(): up(brick_window, block_offset, xt, entry_rows, w_up_t, answers[0], *retur...  10.4 us
    ppermute x8, starting transfers between devices, local(): lax.ppermute(answers[1 + g], ('outer', 'inner'), group_route(g, -1))  6.94 us
    ppermute x8, waiting for transfers between devices, local(): lax.ppermute(parts[1 + g], ('outer', 'inner'), group_route(g, 1))  5.42 us
    pallas_call x1, Pallas kernels, local(): coarse(cell_window, cells, b_down.reshape(1, out_width), parts[0], *arrived)  5.26 us
  transfers between devices with their start and end apart: 16, of which 7 were waited for; matrix products, arithmetic and copies ran while one was open for 1% of the time, Pallas kernels for 11%

profile of v3, /device:TPU:24, one launch (start us, length us, event | category | flops | bytes accessed | tf_op | source)
XLA Modules:
  0.0 82.0 jit_solution(9119972622060344664)
XLA Ops:
  0.0 1.0 %slice_reduce_fusion = s32[256]{0:T(256)S(1)} fusion(s32[256,128]{1,0:T(8,128)} %bitcast.9), kind=kLoop, calls=%fused_computation | loop fusion | bytes 2048 | tf_op jit(solution)/shard_map/slice | solution.py:199
  1.0 0.6 and_select_fusion.1.win_ref
  1.6 0.1 squeeze.6
  1.7 0.1 convert_reduce_fusion.count_ref
  1.9 0.2 reduce_window_sum.18
  2.1 0.2 reduce_window_sum.17
  2.3 0.1 fusion.2
  2.4 0.1 select_reduce_fusion
  2.6 0.7 reshape.114.order_ref
  3.2 0.0 copy-done.17
  3.2 9.9 %shard_map.74 = (bf16[512,128]{1,0:T(8,128)(2,1)}, bf16[512,128]{1,0:T(8,128)(2,1)}, bf16[512,128]{1,0:T(8,128)(2,1)}, bf16[512,128]{1,0:T(8,128)(2,1)}, bf16[51...) custom-call(s32[4]{0:T(128)} %copy-done.17, ...), custom_call_target="tpu_custom_call" | custom-call | flops 536870912 | bytes 5373952 | tf_op jit(solution)/shard_map/pallas_call | solution.py:224
  13.1 5.2 %collective-permute-start = (bf16[512,128]{1,0:T(8,128)(2,1)}, bf16[512,128]{1,0:T(8,128)(2,1)S(1)}, u32[]{:S(2)}, u32[]{:S(2)}) collective-permute-start(bf16[512,128]{1,0:T(8,128)(2,1)} %get-tuple-element.22), channel_id=1, source_target_pairs={{0,127},{1,120},{2,121},{3,122},{4,123},{5,124},{6,125},{7,126},{8... | collective-permute-start | bytes 393224 | tf_op jit(solution)/shard_map/ppermute | solution.py:250
  18.3 2.4 %collective-permute-start.1 = (bf16[512,128]{1,0:T(8,128)(2,1)}, bf16[512,128]{1,0:T(8,128)(2,1)S(1)}, u32[]{:S(2)}, u32[]{:S(2)}) collective-permute-start(bf16[512,128]{1,0:T(8,128)(2,1)} %get-tuple-element.23), channel_id=1, source_target_pairs={{0,120},{1,121},{2,122},{3,123},{4,124},{5,125},{6,126},{7,127},{8... | collective-permute-start | bytes 393224 | tf_op jit(solution)/shard_map/ppermute | solution.py:250
  20.7 0.0 collective-permute-start.2
  20.7 1.4 %collective-permute-start.3 = (bf16[512,128]{1,0:T(8,128)(2,1)}, bf16[512,128]{1,0:T(8,128)(2,1)S(1)}, u32[]{:S(2)}, u32[]{:S(2)}) collective-permute-start(bf16[512,128]{1,0:T(8,128)(2,1)} %get-tuple-element.25), channel_id=1, source_target_pairs={{0,7},{1,0},{2,1},{3,2},{4,3},{5,4},{6,5},{7,6},{8,15},{9,8},{10,9... | collective-permute-start | bytes 393224 | tf_op jit(solution)/shard_map/ppermute | solution.py:250
  22.1 0.3 collective-permute-start.4
  22.4 0.0 copy-done.8
  22.4 0.1 reduce_min.9
  22.5 0.0 collective-permute-done.refs_1_
  22.5 0.0 copy-start.9
  22.5 2.8 %collective-permute-start.5 = (bf16[512,128]{1,0:T(8,128)(2,1)}, bf16[512,128]{1,0:T(8,128)(2,1)S(1)}, u32[]{:S(2)}, u32[]{:S(2)}) collective-permute-start(bf16[512,128]{1,0:T(8,128)(2,1)} %get-tuple-element.27), channel_id=1, source_target_pairs={{0,15},{1,8},{2,9},{3,10},{4,11},{5,12},{6,13},{7,14},{8,23},{9,16... | collective-permute-start | bytes 393224 | tf_op jit(solution)/shard_map/ppermute | solution.py:250
  25.3 0.0 collective-permute-done.1.refs_2_
  25.3 0.2 collective-permute-start.6
  25.5 3.0 %collective-permute-done.2.refs_3_ = bf16[512,128]{1,0:T(8,128)(2,1)S(1)} collective-permute-done((bf16[512,128]{1,0:T(8,128)(2,1)}, bf16[512,128]{1,0:T(8,128)(2,1)S(1)}, u32[]{:S(2)}, u32[]{:S(2)}) %collective-permute-start.2) | collective-permute-done | bytes 131104 | tf_op jit(solution)/shard_map/ppermute | solution.py:250
  28.5 0.0 collective-permute-start.7
  28.5 0.6 and_select_fusion.cw_ref
  29.2 9.2 %shard_map.73.refs_0_ = bf16[4096,128]{1,0:T(8,128)(2,1)} custom-call(s32[4]{0:T(128)} %copy-done.17, s32[256]{0:T(256)} %reshape.114.order_ref, s32[256]{0:T(256)} %and_select_fusion.1.win_ref, s32[256]{0:T(256)} %off_ref.5, bf16[64,32768]{1,0:T(8,128)(2,1)} %bitcast.7, s32[256,128]{1,0:T(8,128)} %bitcast.11, bf16[8,64,128]{2,1,0:T(8,128)(2,1)} %w_ref.3), custom_call_target="tpu_custom_call" | custom-call | flops 536870912 | bytes 5373952 | tf_op jit(solution)/shard_map/pallas_call | solution.py:224
  38.4 0.0 collective-permute-done.3.refs_4_
  38.4 0.0 collective-permute-done.4.refs_5_
  38.4 0.0 copy-start.13
  38.4 0.0 collective-permute-done.5.refs_6_
  38.4 0.0 copy-start.14
  38.4 0.0 collective-permute-done.6.refs_7_
  38.4 0.0 copy-start.15
  38.5 2.4 %collective-permute-done.7.refs_8_ = bf16[512,128]{1,0:T(8,128)(2,1)S(1)} collective-permute-done((bf16[512,128]{1,0:T(8,128)(2,1)}, bf16[512,128]{1,0:T(8,128)(2,1)S(1)}, u32[]{:S(2)}, u32[]{:S(2)}) %collective-permute-start.7) | collective-permute-done | bytes 131104 | tf_op jit(solution)/shard_map/ppermute | solution.py:250
  40.9 0.0 copy-done.9
  40.9 0.0 copy-done.10
  40.9 0.0 copy-done.11
  40.9 0.6 copy-done.16
  41.5 5.3 %shard_map.75 = (bf16[128,4096]{1,0:T(8,128)(2,1)}, bf16[128,512]{1,0:T(8,128)(2,1)}, bf16[128,512]{1,0:T(8,128)(2,1)}, bf16[128,512]{1,0:T(8,128)(2,1)}, bf16[1...) custom-call(s32[64]{0:T(128)} %and_select_fusion.cw_ref, ...), custom_call_target="tpu_custom_call" | custom-call | flops 536870912 | bytes 4194304 | tf_op jit(solution)/shard_map/pallas_call | solution.py:273
  46.8 0.0 collective-permute-start.8
  46.8 3.7 %collective-permute-start.9 = (bf16[128,512]{1,0:T(8,128)(2,1)}, bf16[128,512]{1,0:T(8,128)(2,1)S(1)}, u32[]{:S(2)}, u32[]{:S(2)}) collective-permute-start(bf16[128,512]{1,0:T(8,128)(2,1)} %get-tuple-element.32), channel_id=1, source_target_pairs={{120,0},{121,1},{122,2},{123,3},{124,4},{125,5},{126,6},{127,7},{0... | collective-permute-start | bytes 393224 | tf_op jit(solution)/shard_map/ppermute | solution.py:276
  50.5 0.0 collective-permute-start.10
  50.5 0.1 collective-permute-start.11
  50.6 1.6 %collective-permute-start.12 = (bf16[128,512]{1,0:T(8,128)(2,1)}, bf16[128,512]{1,0:T(8,128)(2,1)S(1)}, u32[]{:S(2)}, u32[]{:S(2)}) collective-permute-start(bf16[128,512]{1,0:T(8,128)(2,1)} %get-tuple-element.35), channel_id=1, source_target_pairs={{1,0},{2,1},{3,2},{4,3},{5,4},{6,5},{7,6},{0,7},{9,8},{10,9},{11,1... | collective-permute-start | bytes 393224 | tf_op jit(solution)/shard_map/ppermute | solution.py:276
  52.2 4.9 %collective-permute-done.8.refs_1_ = bf16[128,512]{1,0:T(8,128)(2,1)S(1)} collective-permute-done((bf16[128,512]{1,0:T(8,128)(2,1)}, bf16[128,512]{1,0:T(8,128)(2,1)S(1)}, u32[]{:S(2)}, u32[]{:S(2)}) %collective-permute-start.8) | collective-permute-done | bytes 131104 | tf_op jit(solution)/shard_map/ppermute | solution.py:276
  57.1 0.2 collective-permute-start.13
  57.4 2.8 %collective-permute-done.9.refs_2_ = bf16[128,512]{1,0:T(8,128)(2,1)S(1)} collective-permute-done((bf16[128,512]{1,0:T(8,128)(2,1)}, bf16[128,512]{1,0:T(8,128)(2,1)S(1)}, u32[]{:S(2)}, u32[]{:S(2)}) %collective-permute-start.9) | collective-permute-done | bytes 131104 | tf_op jit(solution)/shard_map/ppermute | solution.py:276
  60.2 1.3 %collective-permute-start.14 = (bf16[128,512]{1,0:T(8,128)(2,1)}, bf16[128,512]{1,0:T(8,128)(2,1)S(1)}, u32[]{:S(2)}, u32[]{:S(2)}) collective-permute-start(bf16[128,512]{1,0:T(8,128)(2,1)} %get-tuple-element.37), channel_id=1, source_target_pairs={{8,0},{9,1},{10,2},{11,3},{12,4},{13,5},{14,6},{15,7},{16,8},{17,9... | collective-permute-start | bytes 393224 | tf_op jit(solution)/shard_map/ppermute | solution.py:276
  61.5 2.0 %collective-permute-done.10.refs_3_ = bf16[128,512]{1,0:T(8,128)(2,1)S(1)} collective-permute-done((bf16[128,512]{1,0:T(8,128)(2,1)}, bf16[128,512]{1,0:T(8,128)(2,1)S(1)}, u32[]{:S(2)}, u32[]{:S(2)}) %collective-permute-start.10) | collective-permute-done | bytes 131104 | tf_op jit(solution)/shard_map/ppermute | solution.py:276
  63.5 0.0 collective-permute-start.15
  63.5 0.0 collective-permute-done.11.refs_4_
  63.5 0.0 collective-permute-done.12.refs_5_
  63.6 0.0 collective-permute-done.13.refs_6_
  63.6 0.0 copy-start.5
  63.6 2.7 %collective-permute-done.14.refs_7_ = bf16[128,512]{1,0:T(8,128)(2,1)S(1)} collective-permute-done((bf16[128,512]{1,0:T(8,128)(2,1)}, bf16[128,512]{1,0:T(8,128)(2,1)S(1)}, u32[]{:S(2)}, u32[]{:S(2)}) %collective-permute-start.14) | collective-permute-done | bytes 131104 | tf_op jit(solution)/shard_map/ppermute | solution.py:276
  66.3 4.7 %collective-permute-done.15.refs_8_ = bf16[128,512]{1,0:T(8,128)(2,1)S(1)} collective-permute-done((bf16[128,512]{1,0:T(8,128)(2,1)}, bf16[128,512]{1,0:T(8,128)(2,1)S(1)}, u32[]{:S(2)}, u32[]{:S(2)}) %collective-permute-start.15) | collective-permute-done | bytes 131104 | tf_op jit(solution)/shard_map/ppermute | solution.py:276
  71.0 0.0 copy-done.1
  71.0 0.0 copy-done.3
  71.0 0.0 copy-done.4
  71.0 0.0 copy-done.5
  71.0 0.0 copy-done.6
  71.0 0.6 copy-done.7
  71.6 10.4 %shard_map.76 = bf16[64,32768]{1,0:T(8,128)(2,1)} custom-call(s32[256]{0:T(256)} %and_select_fusion.1.win_ref, s32[256]{0:T(256)} %off_ref.5, bf16[64,32768]{1,0:T(8,128)(2,1)} %bitcast.8, s32[256,128]{1,0:T(8,128)} %bitcast.12, bf16[8,64,128]{2,1,0:T(8,128)(2,1)} %bitcast.13, bf16[128,4096]{1,0:T(8,128)(2,1)} %get-tuple-element.30.refs_0_, ...), custom_call_target="tpu_custom_call" | custom-call | flops 1610612736 | bytes 10616832 | tf_op jit(solution)/shard_map/pallas_call | solution.py:304
  (21 shorter events, 0.1 us)
Async XLA Ops:
  0.0 22.4 %copy-start.8 = (s32[1,8192]{1,0:T(1,128)S(1)}, s32[1,8192]{1,0:T(1,128)}, u32[]{:S(2)}) copy-start(s32[1,8192]{1,0:T(1,128)} %param.10) | copy-start | bytes 98308
  1.8 1.4 %copy-start.17 = (s32[4]{0:T(128)}, s32[4]{0:T(128)S(1)}, u32[]{:S(2)}) copy-start(s32[4]{0:T(128)S(1)} %convert_reduce_fusion.count_ref) | copy-start | bytes 52
  13.1 9.4 %collective-permute-start = (bf16[512,128]{1,0:T(8,128)(2,1)}, bf16[512,128]{1,0:T(8,128)(2,1)S(1)}, u32[]{:S(2)}, u32[]{:S(2)}) collective-permute-start(bf16[512,128]{1,0:T(8,128)(2,1)} %get-tuple-element.22), channel_id=1, source_target_pairs={{0,127},{1,120},{2,121},{3,122},{4,123},{5,124},{6,125},{7,126},{8... | collective-permute-start | bytes 393224 | tf_op jit(solution)/shard_map/ppermute | solution.py:250
  18.3 7.0 %collective-permute-start.1 = (bf16[512,128]{1,0:T(8,128)(2,1)}, bf16[512,128]{1,0:T(8,128)(2,1)S(1)}, u32[]{:S(2)}, u32[]{:S(2)}) collective-permute-start(bf16[512,128]{1,0:T(8,128)(2,1)} %get-tuple-element.23), channel_id=1, source_target_pairs={{0,120},{1,121},{2,122},{3,123},{4,124},{5,125},{6,126},{7,127},{8... | collective-permute-start | bytes 393224 | tf_op jit(solution)/shard_map/ppermute | solution.py:250
  20.7 7.8 %collective-permute-start.2 = (bf16[512,128]{1,0:T(8,128)(2,1)}, bf16[512,128]{1,0:T(8,128)(2,1)S(1)}, u32[]{:S(2)}, u32[]{:S(2)}) collective-permute-start(bf16[512,128]{1,0:T(8,128)(2,1)} %get-tuple-element.24), channel_id=1, source_target_pairs={{0,121},{1,122},{2,123},{3,124},{4,125},{5,126},{6,127},{7,120},{8... | collective-permute-start | bytes 393224 | tf_op jit(solution)/shard_map/ppermute | solution.py:250
  20.7 17.7 %collective-permute-start.3 = (bf16[512,128]{1,0:T(8,128)(2,1)}, bf16[512,128]{1,0:T(8,128)(2,1)S(1)}, u32[]{:S(2)}, u32[]{:S(2)}) collective-permute-start(bf16[512,128]{1,0:T(8,128)(2,1)} %get-tuple-element.25), channel_id=1, source_target_pairs={{0,7},{1,0},{2,1},{3,2},{4,3},{5,4},{6,5},{7,6},{8,15},{9,8},{10,9... | collective-permute-start | bytes 393224 | tf_op jit(solution)/shard_map/ppermute | solution.py:250
  22.1 16.3 %collective-permute-start.4 = (bf16[512,128]{1,0:T(8,128)(2,1)}, bf16[512,128]{1,0:T(8,128)(2,1)S(1)}, u32[]{:S(2)}, u32[]{:S(2)}) collective-permute-start(bf16[512,128]{1,0:T(8,128)(2,1)} %get-tuple-element.26), channel_id=1, source_target_pairs={{0,1},{1,2},{2,3},{3,4},{4,5},{5,6},{6,7},{7,0},{8,9},{9,10},{10,1... | collective-permute-start | bytes 393224 | tf_op jit(solution)/shard_map/ppermute | solution.py:250
  22.5 18.4 %copy-start.9 = (bf16[512,128]{1,0:T(8,128)(2,1)}, bf16[512,128]{1,0:T(8,128)(2,1)S(1)}, u32[]{:S(2)}) copy-start(bf16[512,128]{1,0:T(8,128)(2,1)S(1)} %collective-permute-done.refs_1_) | copy-start | bytes 393220
  22.5 15.9 %collective-permute-start.5 = (bf16[512,128]{1,0:T(8,128)(2,1)}, bf16[512,128]{1,0:T(8,128)(2,1)S(1)}, u32[]{:S(2)}, u32[]{:S(2)}) collective-permute-start(bf16[512,128]{1,0:T(8,128)(2,1)} %get-tuple-element.27), channel_id=1, source_target_pairs={{0,15},{1,8},{2,9},{3,10},{4,11},{5,12},{6,13},{7,14},{8,23},{9,16... | collective-permute-start | bytes 393224 | tf_op jit(solution)/shard_map/ppermute | solution.py:250
  25.3 15.6 %copy-start.10 = (bf16[512,128]{1,0:T(8,128)(2,1)}, bf16[512,128]{1,0:T(8,128)(2,1)S(1)}, u32[]{:S(2)}) copy-start(bf16[512,128]{1,0:T(8,128)(2,1)S(1)} %collective-permute-done.1.refs_2_) | copy-start | bytes 393220
  25.3 13.1 %collective-permute-start.6 = (bf16[512,128]{1,0:T(8,128)(2,1)}, bf16[512,128]{1,0:T(8,128)(2,1)S(1)}, u32[]{:S(2)}, u32[]{:S(2)}) collective-permute-start(bf16[512,128]{1,0:T(8,128)(2,1)} %get-tuple-element.28), channel_id=1, source_target_pairs={{0,8},{1,9},{2,10},{3,11},{4,12},{5,13},{6,14},{7,15},{8,16},{9,17... | collective-permute-start | bytes 393224 | tf_op jit(solution)/shard_map/ppermute | solution.py:250
  28.5 12.4 %copy-start.11 = (bf16[512,128]{1,0:T(8,128)(2,1)}, bf16[512,128]{1,0:T(8,128)(2,1)S(1)}, u32[]{:S(2)}) copy-start(bf16[512,128]{1,0:T(8,128)(2,1)S(1)} %collective-permute-done.2.refs_3_) | copy-start | bytes 393220
  28.5 12.4 %collective-permute-start.7 = (bf16[512,128]{1,0:T(8,128)(2,1)}, bf16[512,128]{1,0:T(8,128)(2,1)S(1)}, u32[]{:S(2)}, u32[]{:S(2)}) collective-permute-start(bf16[512,128]{1,0:T(8,128)(2,1)} %get-tuple-element.29), channel_id=1, source_target_pairs={{0,9},{1,10},{2,11},{3,12},{4,13},{5,14},{6,15},{7,8},{8,17},{9,18... | collective-permute-start | bytes 393224 | tf_op jit(solution)/shard_map/ppermute | solution.py:250
  38.4 2.5 %copy-start.12 = (bf16[512,128]{1,0:T(8,128)(2,1)}, bf16[512,128]{1,0:T(8,128)(2,1)S(1)}, u32[]{:S(2)}) copy-start(bf16[512,128]{1,0:T(8,128)(2,1)S(1)} %collective-permute-done.3.refs_4_) | copy-start | bytes 393220
  38.4 2.5 %copy-start.13 = (bf16[512,128]{1,0:T(8,128)(2,1)}, bf16[512,128]{1,0:T(8,128)(2,1)S(1)}, u32[]{:S(2)}) copy-start(bf16[512,128]{1,0:T(8,128)(2,1)S(1)} %collective-permute-done.4.refs_5_) | copy-start | bytes 393220
  38.4 2.5 %copy-start.14 = (bf16[512,128]{1,0:T(8,128)(2,1)}, bf16[512,128]{1,0:T(8,128)(2,1)S(1)}, u32[]{:S(2)}) copy-start(bf16[512,128]{1,0:T(8,128)(2,1)S(1)} %collective-permute-done.5.refs_6_) | copy-start | bytes 393220
  38.4 2.5 %copy-start.15 = (bf16[512,128]{1,0:T(8,128)(2,1)}, bf16[512,128]{1,0:T(8,128)(2,1)S(1)}, u32[]{:S(2)}) copy-start(bf16[512,128]{1,0:T(8,128)(2,1)S(1)} %collective-permute-done.6.refs_7_) | copy-start | bytes 393220
  40.9 0.6 copy-start.16
  46.8 10.4 %collective-permute-start.8 = (bf16[128,512]{1,0:T(8,128)(2,1)}, bf16[128,512]{1,0:T(8,128)(2,1)S(1)}, u32[]{:S(2)}, u32[]{:S(2)}) collective-permute-start(bf16[128,512]{1,0:T(8,128)(2,1)} %get-tuple-element.31), channel_id=1, source_target_pairs={{127,0},{120,1},{121,2},{122,3},{123,4},{124,5},{125,6},{126,7},{7... | collective-permute-start | bytes 393224 | tf_op jit(solution)/shard_map/ppermute | solution.py:276
  46.8 13.4 %collective-permute-start.9 = (bf16[128,512]{1,0:T(8,128)(2,1)}, bf16[128,512]{1,0:T(8,128)(2,1)S(1)}, u32[]{:S(2)}, u32[]{:S(2)}) collective-permute-start(bf16[128,512]{1,0:T(8,128)(2,1)} %get-tuple-element.32), channel_id=1, source_target_pairs={{120,0},{121,1},{122,2},{123,3},{124,4},{125,5},{126,6},{127,7},{0... | collective-permute-start | bytes 393224 | tf_op jit(solution)/shard_map/ppermute | solution.py:276
  50.5 13.1 %collective-permute-start.10 = (bf16[128,512]{1,0:T(8,128)(2,1)}, bf16[128,512]{1,0:T(8,128)(2,1)S(1)}, u32[]{:S(2)}, u32[]{:S(2)}) collective-permute-start(bf16[128,512]{1,0:T(8,128)(2,1)} %get-tuple-element.33), channel_id=1, source_target_pairs={{121,0},{122,1},{123,2},{124,3},{125,4},{126,5},{127,6},{120,7},{1... | collective-permute-start | bytes 393224 | tf_op jit(solution)/shard_map/ppermute | solution.py:276
  50.5 13.1 %collective-permute-start.11 = (bf16[128,512]{1,0:T(8,128)(2,1)}, bf16[128,512]{1,0:T(8,128)(2,1)S(1)}, u32[]{:S(2)}, u32[]{:S(2)}) collective-permute-start(bf16[128,512]{1,0:T(8,128)(2,1)} %get-tuple-element.34), channel_id=1, source_target_pairs={{7,0},{0,1},{1,2},{2,3},{3,4},{4,5},{5,6},{6,7},{15,8},{8,9},{9,10... | collective-permute-start | bytes 393224 | tf_op jit(solution)/shard_map/ppermute | solution.py:276
  50.6 12.9 %collective-permute-start.12 = (bf16[128,512]{1,0:T(8,128)(2,1)}, bf16[128,512]{1,0:T(8,128)(2,1)S(1)}, u32[]{:S(2)}, u32[]{:S(2)}) collective-permute-start(bf16[128,512]{1,0:T(8,128)(2,1)} %get-tuple-element.35), channel_id=1, source_target_pairs={{1,0},{2,1},{3,2},{4,3},{5,4},{6,5},{7,6},{0,7},{9,8},{10,9},{11,1... | collective-permute-start | bytes 393224 | tf_op jit(solution)/shard_map/ppermute | solution.py:276
  57.1 13.8 %copy-start = (bf16[128,512]{1,0:T(8,128)(2,1)}, bf16[128,512]{1,0:T(8,128)(2,1)S(1)}, u32[]{:S(2)}) copy-start(bf16[128,512]{1,0:T(8,128)(2,1)S(1)} %collective-permute-done.8.refs_1_) | copy-start | bytes 393220
  57.1 6.4 %collective-permute-start.13 = (bf16[128,512]{1,0:T(8,128)(2,1)}, bf16[128,512]{1,0:T(8,128)(2,1)S(1)}, u32[]{:S(2)}, u32[]{:S(2)}) collective-permute-start(bf16[128,512]{1,0:T(8,128)(2,1)} %get-tuple-element.36), channel_id=1, source_target_pairs={{15,0},{8,1},{9,2},{10,3},{11,4},{12,5},{13,6},{14,7},{23,8},{16,9... | collective-permute-start | bytes 393224 | tf_op jit(solution)/shard_map/ppermute | solution.py:276
  60.2 10.8 %copy-start.1 = (bf16[128,512]{1,0:T(8,128)(2,1)}, bf16[128,512]{1,0:T(8,128)(2,1)S(1)}, u32[]{:S(2)}) copy-start(bf16[128,512]{1,0:T(8,128)(2,1)S(1)} %collective-permute-done.9.refs_2_) | copy-start | bytes 393220
  60.2 6.1 %collective-permute-start.14 = (bf16[128,512]{1,0:T(8,128)(2,1)}, bf16[128,512]{1,0:T(8,128)(2,1)S(1)}, u32[]{:S(2)}, u32[]{:S(2)}) collective-permute-start(bf16[128,512]{1,0:T(8,128)(2,1)} %get-tuple-element.37), channel_id=1, source_target_pairs={{8,0},{9,1},{10,2},{11,3},{12,4},{13,5},{14,6},{15,7},{16,8},{17,9... | collective-permute-start | bytes 393224 | tf_op jit(solution)/shard_map/ppermute | solution.py:276
  63.5 7.5 %copy-start.2 = (bf16[128,512]{1,0:T(8,128)(2,1)}, bf16[128,512]{1,0:T(8,128)(2,1)S(1)}, u32[]{:S(2)}) copy-start(bf16[128,512]{1,0:T(8,128)(2,1)S(1)} %collective-permute-done.10.refs_3_) | copy-start | bytes 393220
  63.5 7.5 %collective-permute-start.15 = (bf16[128,512]{1,0:T(8,128)(2,1)}, bf16[128,512]{1,0:T(8,128)(2,1)S(1)}, u32[]{:S(2)}, u32[]{:S(2)}) collective-permute-start(bf16[128,512]{1,0:T(8,128)(2,1)} %get-tuple-element.38), channel_id=1, source_target_pairs={{9,0},{10,1},{11,2},{12,3},{13,4},{14,5},{15,6},{8,7},{17,8},{18,9... | collective-permute-start | bytes 393224 | tf_op jit(solution)/shard_map/ppermute | solution.py:276
  63.5 7.5 %copy-start.3 = (bf16[128,512]{1,0:T(8,128)(2,1)}, bf16[128,512]{1,0:T(8,128)(2,1)S(1)}, u32[]{:S(2)}) copy-start(bf16[128,512]{1,0:T(8,128)(2,1)S(1)} %collective-permute-done.11.refs_4_) | copy-start | bytes 393220
  63.5 7.5 %copy-start.4 = (bf16[128,512]{1,0:T(8,128)(2,1)}, bf16[128,512]{1,0:T(8,128)(2,1)S(1)}, u32[]{:S(2)}) copy-start(bf16[128,512]{1,0:T(8,128)(2,1)S(1)} %collective-permute-done.12.refs_5_) | copy-start | bytes 393220
  63.6 7.5 %copy-start.5 = (bf16[128,512]{1,0:T(8,128)(2,1)}, bf16[128,512]{1,0:T(8,128)(2,1)S(1)}, u32[]{:S(2)}) copy-start(bf16[128,512]{1,0:T(8,128)(2,1)S(1)} %collective-permute-done.13.refs_6_) | copy-start | bytes 393220
  66.3 4.8 %copy-start.6 = (bf16[128,512]{1,0:T(8,128)(2,1)}, bf16[128,512]{1,0:T(8,128)(2,1)S(1)}, u32[]{:S(2)}) copy-start(bf16[128,512]{1,0:T(8,128)(2,1)S(1)} %collective-permute-done.14.refs_7_) | copy-start | bytes 393220
  71.0 0.7 copy-start.7

commit v4 on v3

--- a/solution.py
+++ b/solution.py
@@ -13,7 +13,7 @@
 WIN = 128
 BRICKS_PER_STEP = 64
 UNROLL = 16
-UP_UNROLL = 64
+UP_UNROLL = 128
 WIN_UNROLL = 32
 
 step_table = ((-1, -1), (-1, 0), (-1, 1), (0, -1), (0, 1), (1, -1), (1, 0), (1, 1))
@@ -281,14 +281,14 @@
         out_shape=jax.ShapeDtypeStruct((in_width, fine_rows), features.dtype),
         grid_spec=pltpu.PrefetchScalarGridSpec(
             num_scalar_prefetch=2,
-            grid=(steps,),
+            grid=(blocks // UP_UNROLL,),
             in_specs=[
-                pl.BlockSpec((in_width, BRICKS_PER_STEP * BLK), lambda i, *_: (0, i)),
-                pl.BlockSpec((BRICKS_PER_STEP, BLK), lambda i, *_: (i, 0)),
+                pl.BlockSpec((in_width, UP_UNROLL * BLK), lambda i, *_: (0, i)),
+                pl.BlockSpec((UP_UNROLL, BLK), lambda i, *_: (i, 0)),
                 whole(w_up_t.shape),
             ]
             + [pl.BlockSpec(memory_space=pl.ANY)] * (1 + n_groups),
-            out_specs=pl.BlockSpec((in_width, BRICKS_PER_STEP * BLK), lambda i, *_: (0, i)),
+            out_specs=pl.BlockSpec((in_width, UP_UNROLL * BLK), lambda i, *_: (0, i)),
             scratch_shapes=[
                 pltpu.VMEM((out_width, entries), jnp.bfloat16),
                 pltpu.SemaphoreType.DMA((1 + n_groups,)),

time: 82.1 us -> 82.3 us (level)
  no operation moved by 1% of the time
where the time goes in v4:
time: 82.3 us; the launch traced here: 82.5 us
  Pallas kernels  35.4 us (43%)
  waiting for transfers between devices  22.6 us (27%)
  starting transfers between devices  19.1 us (23%)
  local copies, waits for them, and re-layouts  3.02 us (4%)
  other arithmetic  2.15 us (3%)
    pallas_call x2, Pallas kernels, down_call(): pl.pallas_call(functools.partial(down_kernel, first_window), out_shape=sh...  19.8 us
    ppermute x8, waiting for transfers between devices, local(): lax.ppermute(answers[1 + g], ('outer', 'inner'), group_route(g, -1))  18 us
    ppermute x8, starting transfers between devices, local(): lax.ppermute(parts[1 + g], ('outer', 'inner'), group_route(g, 1))  12 us
    pallas_call x1, Pallas kernels, local(): up(brick_window, block_offset, xt, entry_rows, w_up_t, answers[0], *retur...  10.4 us
    ppermute x8, starting transfers between devices, local(): lax.ppermute(answers[1 + g], ('outer', 'inner'), group_route(g, -1))  7.08 us
    pallas_call x1, Pallas kernels, local(): coarse(cell_window, cells, b_down.reshape(1, out_width), parts[0], *arrived)  5.27 us
    ppermute x8, waiting for transfers between devices, local(): lax.ppermute(parts[1 + g], ('outer', 'inner'), group_route(g, 1))  4.62 us
  transfers between devices with their start and end apart: 16, of which 7 were waited for; matrix products, arithmetic and copies ran while one was open for 1% of the time, Pallas kernels for 11%

profile of v4, /device:TPU:24, one launch (start us, length us, event | category | flops | bytes accessed | tf_op | source)
XLA Modules:
  0.0 82.5 jit_solution(7975044578872749483)
XLA Ops:
  0.0 1.0 %slice_reduce_fusion = s32[256]{0:T(256)S(1)} fusion(s32[256,128]{1,0:T(8,128)} %bitcast.9), kind=kLoop, calls=%fused_computation | loop fusion | bytes 2048 | tf_op jit(solution)/shard_map/slice | solution.py:199
  1.0 0.6 and_select_fusion.1.win_ref
  1.6 0.1 squeeze.6
  1.7 0.1 convert_reduce_fusion.count_ref
  1.9 0.2 reduce_window_sum.18
  2.1 0.2 reduce_window_sum.17
  2.3 0.1 fusion.2
  2.4 0.1 select_reduce_fusion
  2.6 0.7 reshape.114.order_ref
  3.2 0.0 copy-done.17
  3.2 10.5 %shard_map.74 = (bf16[512,128]{1,0:T(8,128)(2,1)}, bf16[512,128]{1,0:T(8,128)(2,1)}, bf16[512,128]{1,0:T(8,128)(2,1)}, bf16[512,128]{1,0:T(8,128)(2,1)}, bf16[51...) custom-call(s32[4]{0:T(128)} %copy-done.17, ...), custom_call_target="tpu_custom_call" | custom-call | flops 536870912 | bytes 5373952 | tf_op jit(solution)/shard_map/pallas_call | solution.py:224
  13.8 3.9 %collective-permute-start = (bf16[512,128]{1,0:T(8,128)(2,1)}, bf16[512,128]{1,0:T(8,128)(2,1)S(1)}, u32[]{:S(2)}, u32[]{:S(2)}) collective-permute-start(bf16[512,128]{1,0:T(8,128)(2,1)} %get-tuple-element.22), channel_id=1, source_target_pairs={{0,127},{1,120},{2,121},{3,122},{4,123},{5,124},{6,125},{7,126},{8... | collective-permute-start | bytes 393224 | tf_op jit(solution)/shard_map/ppermute | solution.py:250
  17.7 1.7 %collective-permute-start.1 = (bf16[512,128]{1,0:T(8,128)(2,1)}, bf16[512,128]{1,0:T(8,128)(2,1)S(1)}, u32[]{:S(2)}, u32[]{:S(2)}) collective-permute-start(bf16[512,128]{1,0:T(8,128)(2,1)} %get-tuple-element.23), channel_id=1, source_target_pairs={{0,120},{1,121},{2,122},{3,123},{4,124},{5,125},{6,126},{7,127},{8... | collective-permute-start | bytes 393224 | tf_op jit(solution)/shard_map/ppermute | solution.py:250
  19.4 1.4 %collective-permute-start.2 = (bf16[512,128]{1,0:T(8,128)(2,1)}, bf16[512,128]{1,0:T(8,128)(2,1)S(1)}, u32[]{:S(2)}, u32[]{:S(2)}) collective-permute-start(bf16[512,128]{1,0:T(8,128)(2,1)} %get-tuple-element.24), channel_id=1, source_target_pairs={{0,121},{1,122},{2,123},{3,124},{4,125},{5,126},{6,127},{7,120},{8... | collective-permute-start | bytes 393224 | tf_op jit(solution)/shard_map/ppermute | solution.py:250
  20.8 0.7 collective-permute-start.3
  21.5 0.3 collective-permute-start.4
  21.8 0.0 copy-done.8
  21.8 0.1 reduce_min.9
  21.9 0.0 collective-permute-done.refs_1_
  22.0 0.0 copy-start.9
  22.0 2.0 %collective-permute-start.5 = (bf16[512,128]{1,0:T(8,128)(2,1)}, bf16[512,128]{1,0:T(8,128)(2,1)S(1)}, u32[]{:S(2)}, u32[]{:S(2)}) collective-permute-start(bf16[512,128]{1,0:T(8,128)(2,1)} %get-tuple-element.27), channel_id=1, source_target_pairs={{0,15},{1,8},{2,9},{3,10},{4,11},{5,12},{6,13},{7,14},{8,23},{9,16... | collective-permute-start | bytes 393224 | tf_op jit(solution)/shard_map/ppermute | solution.py:250
  24.0 0.0 collective-permute-done.1.refs_2_
  24.0 0.3 collective-permute-start.6
  24.3 2.4 %collective-permute-done.2.refs_3_ = bf16[512,128]{1,0:T(8,128)(2,1)S(1)} collective-permute-done((bf16[512,128]{1,0:T(8,128)(2,1)}, bf16[512,128]{1,0:T(8,128)(2,1)S(1)}, u32[]{:S(2)}, u32[]{:S(2)}) %collective-permute-start.2) | collective-permute-done | bytes 131104 | tf_op jit(solution)/shard_map/ppermute | solution.py:250
  26.6 1.6 %collective-permute-start.7 = (bf16[512,128]{1,0:T(8,128)(2,1)}, bf16[512,128]{1,0:T(8,128)(2,1)S(1)}, u32[]{:S(2)}, u32[]{:S(2)}) collective-permute-start(bf16[512,128]{1,0:T(8,128)(2,1)} %get-tuple-element.29), channel_id=1, source_target_pairs={{0,9},{1,10},{2,11},{3,12},{4,13},{5,14},{6,15},{7,8},{8,17},{9,18... | collective-permute-start | bytes 393224 | tf_op jit(solution)/shard_map/ppermute | solution.py:250
  28.3 0.6 and_select_fusion.cw_ref
  28.9 9.2 %shard_map.73.refs_0_ = bf16[4096,128]{1,0:T(8,128)(2,1)} custom-call(s32[4]{0:T(128)} %copy-done.17, s32[256]{0:T(256)} %reshape.114.order_ref, s32[256]{0:T(256)} %and_select_fusion.1.win_ref, s32[256]{0:T(256)} %off_ref.5, bf16[64,32768]{1,0:T(8,128)(2,1)} %bitcast.7, s32[256,128]{1,0:T(8,128)} %bitcast.11, bf16[8,64,128]{2,1,0:T(8,128)(2,1)} %w_ref.3), custom_call_target="tpu_custom_call" | custom-call | flops 536870912 | bytes 5373952 | tf_op jit(solution)/shard_map/pallas_call | solution.py:224
  38.1 0.0 collective-permute-done.3.refs_4_
  38.1 0.0 collective-permute-done.4.refs_5_
  38.1 0.0 copy-start.13
  38.1 0.0 collective-permute-done.5.refs_6_
  38.2 0.0 copy-start.14
  38.2 0.0 collective-permute-done.6.refs_7_
  38.2 0.0 copy-start.15
  38.2 2.2 %collective-permute-done.7.refs_8_ = bf16[512,128]{1,0:T(8,128)(2,1)S(1)} collective-permute-done((bf16[512,128]{1,0:T(8,128)(2,1)}, bf16[512,128]{1,0:T(8,128)(2,1)S(1)}, u32[]{:S(2)}, u32[]{:S(2)}) %collective-permute-start.7) | collective-permute-done | bytes 131104 | tf_op jit(solution)/shard_map/ppermute | solution.py:250
  40.4 0.0 copy-done.9
  40.4 0.0 copy-done.10
  40.4 0.0 copy-done.11
  40.4 0.0 copy-done.12
  40.5 0.0 copy-done.13
  40.5 0.0 copy-done.14
  40.5 0.0 copy-done.15
  40.5 0.6 copy-done.16
  41.1 5.3 %shard_map.75 = (bf16[128,4096]{1,0:T(8,128)(2,1)}, bf16[128,512]{1,0:T(8,128)(2,1)}, bf16[128,512]{1,0:T(8,128)(2,1)}, bf16[128,512]{1,0:T(8,128)(2,1)}, bf16[1...) custom-call(s32[64]{0:T(128)} %and_select_fusion.cw_ref, ...), custom_call_target="tpu_custom_call" | custom-call | flops 536870912 | bytes 4194304 | tf_op jit(solution)/shard_map/pallas_call | solution.py:273
  46.3 0.0 collective-permute-start.8
  46.4 2.7 %collective-permute-start.9 = (bf16[128,512]{1,0:T(8,128)(2,1)}, bf16[128,512]{1,0:T(8,128)(2,1)S(1)}, u32[]{:S(2)}, u32[]{:S(2)}) collective-permute-start(bf16[128,512]{1,0:T(8,128)(2,1)} %get-tuple-element.32), channel_id=1, source_target_pairs={{120,0},{121,1},{122,2},{123,3},{124,4},{125,5},{126,6},{127,7},{0... | collective-permute-start | bytes 393224 | tf_op jit(solution)/shard_map/ppermute | solution.py:276
  49.1 0.0 collective-permute-start.10
  49.1 0.2 collective-permute-start.11
  49.3 1.5 %collective-permute-start.12 = (bf16[128,512]{1,0:T(8,128)(2,1)}, bf16[128,512]{1,0:T(8,128)(2,1)S(1)}, u32[]{:S(2)}, u32[]{:S(2)}) collective-permute-start(bf16[128,512]{1,0:T(8,128)(2,1)} %get-tuple-element.35), channel_id=1, source_target_pairs={{1,0},{2,1},{3,2},{4,3},{5,4},{6,5},{7,6},{0,7},{9,8},{10,9},{11,1... | collective-permute-start | bytes 393224 | tf_op jit(solution)/shard_map/ppermute | solution.py:276
  50.8 5.8 %collective-permute-done.8.refs_1_ = bf16[128,512]{1,0:T(8,128)(2,1)S(1)} collective-permute-done((bf16[128,512]{1,0:T(8,128)(2,1)}, bf16[128,512]{1,0:T(8,128)(2,1)S(1)}, u32[]{:S(2)}, u32[]{:S(2)}) %collective-permute-start.8) | collective-permute-done | bytes 131104 | tf_op jit(solution)/shard_map/ppermute | solution.py:276
  56.6 1.3 %collective-permute-start.13 = (bf16[128,512]{1,0:T(8,128)(2,1)}, bf16[128,512]{1,0:T(8,128)(2,1)S(1)}, u32[]{:S(2)}, u32[]{:S(2)}) collective-permute-start(bf16[128,512]{1,0:T(8,128)(2,1)} %get-tuple-element.36), channel_id=1, source_target_pairs={{15,0},{8,1},{9,2},{10,3},{11,4},{12,5},{13,6},{14,7},{23,8},{16,9... | collective-permute-start | bytes 393224 | tf_op jit(solution)/shard_map/ppermute | solution.py:276
  57.9 2.8 %collective-permute-done.9.refs_2_ = bf16[128,512]{1,0:T(8,128)(2,1)S(1)} collective-permute-done((bf16[128,512]{1,0:T(8,128)(2,1)}, bf16[128,512]{1,0:T(8,128)(2,1)S(1)}, u32[]{:S(2)}, u32[]{:S(2)}) %collective-permute-start.9) | collective-permute-done | bytes 131104 | tf_op jit(solution)/shard_map/ppermute | solution.py:276
  60.7 0.3 collective-permute-start.14
  61.0 2.2 %collective-permute-done.10.refs_3_ = bf16[128,512]{1,0:T(8,128)(2,1)S(1)} collective-permute-done((bf16[128,512]{1,0:T(8,128)(2,1)}, bf16[128,512]{1,0:T(8,128)(2,1)S(1)}, u32[]{:S(2)}, u32[]{:S(2)}) %collective-permute-start.10) | collective-permute-done | bytes 131104 | tf_op jit(solution)/shard_map/ppermute | solution.py:276
  63.2 1.0 %collective-permute-start.15 = (bf16[128,512]{1,0:T(8,128)(2,1)}, bf16[128,512]{1,0:T(8,128)(2,1)S(1)}, u32[]{:S(2)}, u32[]{:S(2)}) collective-permute-start(bf16[128,512]{1,0:T(8,128)(2,1)} %get-tuple-element.38), channel_id=1, source_target_pairs={{9,0},{10,1},{11,2},{12,3},{13,4},{14,5},{15,6},{8,7},{17,8},{18,9... | collective-permute-start | bytes 393224 | tf_op jit(solution)/shard_map/ppermute | solution.py:276
  64.1 0.0 collective-permute-done.11.refs_4_
  64.1 0.0 collective-permute-done.12.refs_5_
  64.1 0.0 copy-start.4
  64.2 0.0 collective-permute-done.13.refs_6_
  64.2 0.0 copy-start.5
  64.2 3.0 %collective-permute-done.14.refs_7_ = bf16[128,512]{1,0:T(8,128)(2,1)S(1)} collective-permute-done((bf16[128,512]{1,0:T(8,128)(2,1)}, bf16[128,512]{1,0:T(8,128)(2,1)S(1)}, u32[]{:S(2)}, u32[]{:S(2)}) %collective-permute-start.14) | collective-permute-done | bytes 131104 | tf_op jit(solution)/shard_map/ppermute | solution.py:276
  67.2 4.3 %collective-permute-done.15.refs_8_ = bf16[128,512]{1,0:T(8,128)(2,1)S(1)} collective-permute-done((bf16[128,512]{1,0:T(8,128)(2,1)}, bf16[128,512]{1,0:T(8,128)(2,1)S(1)}, u32[]{:S(2)}, u32[]{:S(2)}) %collective-permute-start.15) | collective-permute-done | bytes 131104 | tf_op jit(solution)/shard_map/ppermute | solution.py:276
  71.5 0.6 copy-done.7
  72.1 10.4 %shard_map.76 = bf16[64,32768]{1,0:T(8,128)(2,1)} custom-call(s32[256]{0:T(256)} %and_select_fusion.1.win_ref, s32[256]{0:T(256)} %off_ref.5, bf16[64,32768]{1,0:T(8,128)(2,1)} %bitcast.8, s32[256,128]{1,0:T(8,128)} %bitcast.12, bf16[8,64,128]{2,1,0:T(8,128)(2,1)} %bitcast.13, bf16[128,4096]{1,0:T(8,128)(2,1)} %get-tuple-element.30.refs_0_, ...), custom_call_target="tpu_custom_call" | custom-call | flops 1610612736 | bytes 10616832 | tf_op jit(solution)/shard_map/pallas_call | solution.py:304
  (21 shorter events, 0.1 us)
Async XLA Ops:
  0.0 21.8 %copy-start.8 = (s32[1,8192]{1,0:T(1,128)S(1)}, s32[1,8192]{1,0:T(1,128)}, u32[]{:S(2)}) copy-start(s32[1,8192]{1,0:T(1,128)} %param.10) | copy-start | bytes 98308
  1.8 1.4 %copy-start.17 = (s32[4]{0:T(128)}, s32[4]{0:T(128)S(1)}, u32[]{:S(2)}) copy-start(s32[4]{0:T(128)S(1)} %convert_reduce_fusion.count_ref) | copy-start | bytes 52
  13.8 8.2 %collective-permute-start = (bf16[512,128]{1,0:T(8,128)(2,1)}, bf16[512,128]{1,0:T(8,128)(2,1)S(1)}, u32[]{:S(2)}, u32[]{:S(2)}) collective-permute-start(bf16[512,128]{1,0:T(8,128)(2,1)} %get-tuple-element.22), channel_id=1, source_target_pairs={{0,127},{1,120},{2,121},{3,122},{4,123},{5,124},{6,125},{7,126},{8... | collective-permute-start | bytes 393224 | tf_op jit(solution)/shard_map/ppermute | solution.py:250
  17.7 6.3 %collective-permute-start.1 = (bf16[512,128]{1,0:T(8,128)(2,1)}, bf16[512,128]{1,0:T(8,128)(2,1)S(1)}, u32[]{:S(2)}, u32[]{:S(2)}) collective-permute-start(bf16[512,128]{1,0:T(8,128)(2,1)} %get-tuple-element.23), channel_id=1, source_target_pairs={{0,120},{1,121},{2,122},{3,123},{4,124},{5,125},{6,126},{7,127},{8... | collective-permute-start | bytes 393224 | tf_op jit(solution)/shard_map/ppermute | solution.py:250
  19.4 7.2 %collective-permute-start.2 = (bf16[512,128]{1,0:T(8,128)(2,1)}, bf16[512,128]{1,0:T(8,128)(2,1)S(1)}, u32[]{:S(2)}, u32[]{:S(2)}) collective-permute-start(bf16[512,128]{1,0:T(8,128)(2,1)} %get-tuple-element.24), channel_id=1, source_target_pairs={{0,121},{1,122},{2,123},{3,124},{4,125},{5,126},{6,127},{7,120},{8... | collective-permute-start | bytes 393224 | tf_op jit(solution)/shard_map/ppermute | solution.py:250
  20.8 17.3 %collective-permute-start.3 = (bf16[512,128]{1,0:T(8,128)(2,1)}, bf16[512,128]{1,0:T(8,128)(2,1)S(1)}, u32[]{:S(2)}, u32[]{:S(2)}) collective-permute-start(bf16[512,128]{1,0:T(8,128)(2,1)} %get-tuple-element.25), channel_id=1, source_target_pairs={{0,7},{1,0},{2,1},{3,2},{4,3},{5,4},{6,5},{7,6},{8,15},{9,8},{10,9... | collective-permute-start | bytes 393224 | tf_op jit(solution)/shard_map/ppermute | solution.py:250
  21.5 16.6 %collective-permute-start.4 = (bf16[512,128]{1,0:T(8,128)(2,1)}, bf16[512,128]{1,0:T(8,128)(2,1)S(1)}, u32[]{:S(2)}, u32[]{:S(2)}) collective-permute-start(bf16[512,128]{1,0:T(8,128)(2,1)} %get-tuple-element.26), channel_id=1, source_target_pairs={{0,1},{1,2},{2,3},{3,4},{4,5},{5,6},{6,7},{7,0},{8,9},{9,10},{10,1... | collective-permute-start | bytes 393224 | tf_op jit(solution)/shard_map/ppermute | solution.py:250
  22.0 18.5 %copy-start.9 = (bf16[512,128]{1,0:T(8,128)(2,1)}, bf16[512,128]{1,0:T(8,128)(2,1)S(1)}, u32[]{:S(2)}) copy-start(bf16[512,128]{1,0:T(8,128)(2,1)S(1)} %collective-permute-done.refs_1_) | copy-start | bytes 393220
  22.0 16.2 %collective-permute-start.5 = (bf16[512,128]{1,0:T(8,128)(2,1)}, bf16[512,128]{1,0:T(8,128)(2,1)S(1)}, u32[]{:S(2)}, u32[]{:S(2)}) collective-permute-start(bf16[512,128]{1,0:T(8,128)(2,1)} %get-tuple-element.27), channel_id=1, source_target_pairs={{0,15},{1,8},{2,9},{3,10},{4,11},{5,12},{6,13},{7,14},{8,23},{9,16... | collective-permute-start | bytes 393224 | tf_op jit(solution)/shard_map/ppermute | solution.py:250
  24.0 16.4 %copy-start.10 = (bf16[512,128]{1,0:T(8,128)(2,1)}, bf16[512,128]{1,0:T(8,128)(2,1)S(1)}, u32[]{:S(2)}) copy-start(bf16[512,128]{1,0:T(8,128)(2,1)S(1)} %collective-permute-done.1.refs_2_) | copy-start | bytes 393220
  24.0 14.2 %collective-permute-start.6 = (bf16[512,128]{1,0:T(8,128)(2,1)}, bf16[512,128]{1,0:T(8,128)(2,1)S(1)}, u32[]{:S(2)}, u32[]{:S(2)}) collective-permute-start(bf16[512,128]{1,0:T(8,128)(2,1)} %get-tuple-element.28), channel_id=1, source_target_pairs={{0,8},{1,9},{2,10},{3,11},{4,12},{5,13},{6,14},{7,15},{8,16},{9,17... | collective-permute-start | bytes 393224 | tf_op jit(solution)/shard_map/ppermute | solution.py:250
  26.6 13.8 %copy-start.11 = (bf16[512,128]{1,0:T(8,128)(2,1)}, bf16[512,128]{1,0:T(8,128)(2,1)S(1)}, u32[]{:S(2)}) copy-start(bf16[512,128]{1,0:T(8,128)(2,1)S(1)} %collective-permute-done.2.refs_3_) | copy-start | bytes 393220
  26.6 13.8 %collective-permute-start.7 = (bf16[512,128]{1,0:T(8,128)(2,1)}, bf16[512,128]{1,0:T(8,128)(2,1)S(1)}, u32[]{:S(2)}, u32[]{:S(2)}) collective-permute-start(bf16[512,128]{1,0:T(8,128)(2,1)} %get-tuple-element.29), channel_id=1, source_target_pairs={{0,9},{1,10},{2,11},{3,12},{4,13},{5,14},{6,15},{7,8},{8,17},{9,18... | collective-permute-start | bytes 393224 | tf_op jit(solution)/shard_map/ppermute | solution.py:250
  38.1 2.3 %copy-start.12 = (bf16[512,128]{1,0:T(8,128)(2,1)}, bf16[512,128]{1,0:T(8,128)(2,1)S(1)}, u32[]{:S(2)}) copy-start(bf16[512,128]{1,0:T(8,128)(2,1)S(1)} %collective-permute-done.3.refs_4_) | copy-start | bytes 393220
  38.1 2.3 %copy-start.13 = (bf16[512,128]{1,0:T(8,128)(2,1)}, bf16[512,128]{1,0:T(8,128)(2,1)S(1)}, u32[]{:S(2)}) copy-start(bf16[512,128]{1,0:T(8,128)(2,1)S(1)} %collective-permute-done.4.refs_5_) | copy-start | bytes 393220
  38.2 2.3 %copy-start.14 = (bf16[512,128]{1,0:T(8,128)(2,1)}, bf16[512,128]{1,0:T(8,128)(2,1)S(1)}, u32[]{:S(2)}) copy-start(bf16[512,128]{1,0:T(8,128)(2,1)S(1)} %collective-permute-done.5.refs_6_) | copy-start | bytes 393220
  38.2 2.3 %copy-start.15 = (bf16[512,128]{1,0:T(8,128)(2,1)}, bf16[512,128]{1,0:T(8,128)(2,1)S(1)}, u32[]{:S(2)}) copy-start(bf16[512,128]{1,0:T(8,128)(2,1)S(1)} %collective-permute-done.6.refs_7_) | copy-start | bytes 393220
  40.4 0.6 copy-start.16
  46.3 10.2 %collective-permute-start.8 = (bf16[128,512]{1,0:T(8,128)(2,1)}, bf16[128,512]{1,0:T(8,128)(2,1)S(1)}, u32[]{:S(2)}, u32[]{:S(2)}) collective-permute-start(bf16[128,512]{1,0:T(8,128)(2,1)} %get-tuple-element.31), channel_id=1, source_target_pairs={{127,0},{120,1},{121,2},{122,3},{123,4},{124,5},{125,6},{126,7},{7... | collective-permute-start | bytes 393224 | tf_op jit(solution)/shard_map/ppermute | solution.py:276
  46.4 14.3 %collective-permute-start.9 = (bf16[128,512]{1,0:T(8,128)(2,1)}, bf16[128,512]{1,0:T(8,128)(2,1)S(1)}, u32[]{:S(2)}, u32[]{:S(2)}) collective-permute-start(bf16[128,512]{1,0:T(8,128)(2,1)} %get-tuple-element.32), channel_id=1, source_target_pairs={{120,0},{121,1},{122,2},{123,3},{124,4},{125,5},{126,6},{127,7},{0... | collective-permute-start | bytes 393224 | tf_op jit(solution)/shard_map/ppermute | solution.py:276
  49.1 14.1 %collective-permute-start.10 = (bf16[128,512]{1,0:T(8,128)(2,1)}, bf16[128,512]{1,0:T(8,128)(2,1)S(1)}, u32[]{:S(2)}, u32[]{:S(2)}) collective-permute-start(bf16[128,512]{1,0:T(8,128)(2,1)} %get-tuple-element.33), channel_id=1, source_target_pairs={{121,0},{122,1},{123,2},{124,3},{125,4},{126,5},{127,6},{120,7},{1... | collective-permute-start | bytes 393224 | tf_op jit(solution)/shard_map/ppermute | solution.py:276
  49.1 15.1 %collective-permute-start.11 = (bf16[128,512]{1,0:T(8,128)(2,1)}, bf16[128,512]{1,0:T(8,128)(2,1)S(1)}, u32[]{:S(2)}, u32[]{:S(2)}) collective-permute-start(bf16[128,512]{1,0:T(8,128)(2,1)} %get-tuple-element.34), channel_id=1, source_target_pairs={{7,0},{0,1},{1,2},{2,3},{3,4},{4,5},{5,6},{6,7},{15,8},{8,9},{9,10... | collective-permute-start | bytes 393224 | tf_op jit(solution)/shard_map/ppermute | solution.py:276
  49.3 14.8 %collective-permute-start.12 = (bf16[128,512]{1,0:T(8,128)(2,1)}, bf16[128,512]{1,0:T(8,128)(2,1)S(1)}, u32[]{:S(2)}, u32[]{:S(2)}) collective-permute-start(bf16[128,512]{1,0:T(8,128)(2,1)} %get-tuple-element.35), channel_id=1, source_target_pairs={{1,0},{2,1},{3,2},{4,3},{5,4},{6,5},{7,6},{0,7},{9,8},{10,9},{11,1... | collective-permute-start | bytes 393224 | tf_op jit(solution)/shard_map/ppermute | solution.py:276
  56.6 14.9 %copy-start = (bf16[128,512]{1,0:T(8,128)(2,1)}, bf16[128,512]{1,0:T(8,128)(2,1)S(1)}, u32[]{:S(2)}) copy-start(bf16[128,512]{1,0:T(8,128)(2,1)S(1)} %collective-permute-done.8.refs_1_) | copy-start | bytes 393220
  56.6 7.6 %collective-permute-start.13 = (bf16[128,512]{1,0:T(8,128)(2,1)}, bf16[128,512]{1,0:T(8,128)(2,1)S(1)}, u32[]{:S(2)}, u32[]{:S(2)}) collective-permute-start(bf16[128,512]{1,0:T(8,128)(2,1)} %get-tuple-element.36), channel_id=1, source_target_pairs={{15,0},{8,1},{9,2},{10,3},{11,4},{12,5},{13,6},{14,7},{23,8},{16,9... | collective-permute-start | bytes 393224 | tf_op jit(solution)/shard_map/ppermute | solution.py:276
  60.7 10.8 %copy-start.1 = (bf16[128,512]{1,0:T(8,128)(2,1)}, bf16[128,512]{1,0:T(8,128)(2,1)S(1)}, u32[]{:S(2)}) copy-start(bf16[128,512]{1,0:T(8,128)(2,1)S(1)} %collective-permute-done.9.refs_2_) | copy-start | bytes 393220
  60.7 6.5 %collective-permute-start.14 = (bf16[128,512]{1,0:T(8,128)(2,1)}, bf16[128,512]{1,0:T(8,128)(2,1)S(1)}, u32[]{:S(2)}, u32[]{:S(2)}) collective-permute-start(bf16[128,512]{1,0:T(8,128)(2,1)} %get-tuple-element.37), channel_id=1, source_target_pairs={{8,0},{9,1},{10,2},{11,3},{12,4},{13,5},{14,6},{15,7},{16,8},{17,9... | collective-permute-start | bytes 393224 | tf_op jit(solution)/shard_map/ppermute | solution.py:276
  63.2 8.3 %copy-start.2 = (bf16[128,512]{1,0:T(8,128)(2,1)}, bf16[128,512]{1,0:T(8,128)(2,1)S(1)}, u32[]{:S(2)}) copy-start(bf16[128,512]{1,0:T(8,128)(2,1)S(1)} %collective-permute-done.10.refs_3_) | copy-start | bytes 393220
  63.2 8.3 %collective-permute-start.15 = (bf16[128,512]{1,0:T(8,128)(2,1)}, bf16[128,512]{1,0:T(8,128)(2,1)S(1)}, u32[]{:S(2)}, u32[]{:S(2)}) collective-permute-start(bf16[128,512]{1,0:T(8,128)(2,1)} %get-tuple-element.38), channel_id=1, source_target_pairs={{9,0},{10,1},{11,2},{12,3},{13,4},{14,5},{15,6},{8,7},{17,8},{18,9... | collective-permute-start | bytes 393224 | tf_op jit(solution)/shard_map/ppermute | solution.py:276
  64.1 7.4 %copy-start.3 = (bf16[128,512]{1,0:T(8,128)(2,1)}, bf16[128,512]{1,0:T(8,128)(2,1)S(1)}, u32[]{:S(2)}) copy-start(bf16[128,512]{1,0:T(8,128)(2,1)S(1)} %collective-permute-done.11.refs_4_) | copy-start | bytes 393220
  64.1 7.4 %copy-start.4 = (bf16[128,512]{1,0:T(8,128)(2,1)}, bf16[128,512]{1,0:T(8,128)(2,1)S(1)}, u32[]{:S(2)}) copy-start(bf16[128,512]{1,0:T(8,128)(2,1)S(1)} %collective-permute-done.12.refs_5_) | copy-start | bytes 393220
  64.2 7.4 %copy-start.5 = (bf16[128,512]{1,0:T(8,128)(2,1)}, bf16[128,512]{1,0:T(8,128)(2,1)S(1)}, u32[]{:S(2)}) copy-start(bf16[128,512]{1,0:T(8,128)(2,1)S(1)} %collective-permute-done.13.refs_6_) | copy-start | bytes 393220
  67.2 4.3 %copy-start.6 = (bf16[128,512]{1,0:T(8,128)(2,1)}, bf16[128,512]{1,0:T(8,128)(2,1)S(1)}, u32[]{:S(2)}) copy-start(bf16[128,512]{1,0:T(8,128)(2,1)S(1)} %collective-permute-done.14.refs_7_) | copy-start | bytes 393220
  71.5 0.7 copy-start.7

commit v5 on v3

--- a/solution.py
+++ b/solution.py
@@ -33,7 +33,7 @@
     return (span == index_row).astype(jnp.bfloat16)
 
 
-def down_kernel(first_window, count_ref, order_ref, win_ref, off_ref, xt_ref, e_ref, w_ref, *refs):
+def down_kernel(first_window, count_ref, order_ref, win_ref, off_ref, cw_ref, xt_ref, e_ref, w_ref, cells_ref, *refs):
     outs = refs[:-1]
     acc = refs[-1]
     step = pl.program_id(0)
@@ -74,20 +74,46 @@
 
     run(start, UNROLL, (stop - start + UNROLL - 1) // UNROLL)
 
-    @pl.when(step == pl.num_programs(0) - 1)
-    def _():
-        size = outs[0].shape[0]
-        for g, out in enumerate(outs):
-            out[...] = acc[g * size : (g + 1) * size, :].astype(out.dtype)
-
-
-def coarse_kernel(cw_ref, cells_ref, bias_ref, *refs):
+    if first_window == 0:
+
+        @pl.when(step == pl.num_programs(0) - 1)
+        def _():
+            cell_sum = outs[0]
+            cell_sum[...] = jnp.zeros_like(cell_sum)
+            cell_windows = cell_sum.shape[0] // WIN
+
+            def gather_body(u, carry):
+                results = []
+                for t in range(WIN_UNROLL):
+                    w = u * WIN_UNROLL + t
+                    window = jnp.minimum(cw_ref[w], cell_windows - 1)
+                    cells = cells_ref[pl.ds(w, 1), :]
+                    inside = jnp.where(cells < C_DEV, cells - window * WIN, -1)
+                    entries = acc[pl.ds(pl.multiple_of(w * WIN, WIN), WIN), :].astype(jnp.bfloat16)
+                    rows = pl.ds(pl.multiple_of(window * WIN, WIN), WIN)
+                    results.append((rows, jnp.dot(one_hot_rows(inside), entries, preferred_element_type=jnp.float32)))
+                for rows, value in results:
+                    cell_sum[rows, :] += value
+                return carry
+
+            lax.fori_loop(0, SELF_CAP // WIN // WIN_UNROLL, gather_body, 0)
+
+    else:
+
+        @pl.when(step == pl.num_programs(0) - 1)
+        def _():
+            size = outs[0].shape[0]
+            for g, out in enumerate(outs):
+                out[...] = acc[g * size : (g + 1) * size, :].astype(out.dtype)
+
+
+def coarse_kernel(cw_ref, cells_ref, bias_ref, partial_ref, *refs):
     n_groups = len(step_table)
-    sources = refs[: 1 + n_groups]
-    outs = refs[1 + n_groups : 2 + 2 * n_groups]
-    acc, coarse = refs[2 + 2 * n_groups :]
+    sources = refs[:n_groups]
+    outs = refs[n_groups : 1 + 2 * n_groups]
+    acc, coarse = refs[1 + 2 * n_groups :]
     cell_windows = acc.shape[0] // WIN
-    acc[...] = jnp.zeros_like(acc)
+    acc[...] = partial_ref[...]
 
     def pick_of(w):
         window = jnp.minimum(cw_ref[w], cell_windows - 1)
@@ -96,7 +122,7 @@
         rows = pl.ds(pl.multiple_of(window * WIN, WIN), WIN)
         return one_hot_rows(inside), rows
 
-    base = 0
+    base = SELF_CAP // WIN
     for src in sources:
         count = src.shape[0] // WIN
         unroll = min(WIN_UNROLL, count)
@@ -225,12 +251,13 @@
             functools.partial(down_kernel, first_window),
             out_shape=shapes,
             grid_spec=pltpu.PrefetchScalarGridSpec(
-                num_scalar_prefetch=4,
+                num_scalar_prefetch=5,
                 grid=(steps,),
                 in_specs=[
                     pl.BlockSpec((in_width, BRICKS_PER_STEP * BLK), lambda i, *_: (0, i)),
                     pl.BlockSpec((BRICKS_PER_STEP, BLK), lambda i, *_: (i, 0)),
                     whole(w_down.shape),
+                    whole(cells.shape),
                 ],
                 out_specs=[whole(s.shape) for s in shapes],
                 scratch_shapes=[pltpu.VMEM((rows + WIN, out_width), jnp.float32)],
@@ -241,10 +268,10 @@
                 transcendentals=0,
                 bytes_accessed=fine_rows * (in_width * 2 + 4) + rows * out_width * 2,
             ),
-        )(counts, order, brick_window, block_offset, xt, entry_rows, w_down)
+        )(counts, order, brick_window, block_offset, cell_window, xt, entry_rows, w_down, cells)
 
     parts = [None] + list(down_call(SELF_CAP // WIN, part_shapes[1:]))
-    parts[0] = down_call(0, part_shapes[:1])[0]
+    cell_partial = down_call(0, [jax.ShapeDtypeStruct((C_DEV, out_width), jnp.float32)])[0]
 
     arrived = [
         lax.ppermute(parts[1 + g], ("outer", "inner"), group_route(g, 1)) for g in range(n_groups)
@@ -256,8 +283,8 @@
         grid_spec=pltpu.PrefetchScalarGridSpec(
             num_scalar_prefetch=1,
             grid=(1,),
-            in_specs=[whole(cells.shape), whole((1, out_width))]
-            + [whole(s.shape) for s in part_shapes],
+            in_specs=[whole(cells.shape), whole((1, out_width)), whole((C_DEV, out_width))]
+            + [whole(s.shape) for s in part_shapes[1:]],
             out_specs=[whole(s.shape) for s in answer_shapes],
             scratch_shapes=[
                 pltpu.VMEM((C_DEV, out_width), jnp.float32),
@@ -270,7 +297,7 @@
             bytes_accessed=4 * entries * out_width,
         ),
     )
-    answers = coarse(cell_window, cells, b_down.reshape(1, out_width), parts[0], *arrived)
+    answers = coarse(cell_window, cells, b_down.reshape(1, out_width), cell_partial, *arrived)
 
     returned = [
         lax.ppermute(answers[1 + g], ("outer", "inner"), group_route(g, -1)) for g in range(n_groups)

time: 82.1 us -> 84.2 us (1.026)
  waiting for transfers between devices: 22.6 us -> 17.6 us
  starting transfers between devices: 19.2 us -> 24.1 us
  Pallas kernels: 34.8 us -> 36.3 us
    ppermute x8, starting transfers between devices: 6.94 us -> 11.7 us  [local(): lax.ppermute(answers[1 + g], ('outer', 'inner'), group_route(g, -1))]
    ppermute x8, waiting for transfers between devices: 17.2 us -> 13.2 us  [local(): lax.ppermute(answers[1 + g], ('outer', 'inner'), group_route(g, -1))]
    pallas_call x2, Pallas kernels: 19.1 us -> 20.6 us  [down_call(): pl.pallas_call(functools.partial(down_kernel, first_window), out_shape=sh...]
    ppermute x8, waiting for transfers between devices: 5.42 us -> 4.38 us  [local(): lax.ppermute(parts[1 + g], ('outer', 'inner'), group_route(g, 1))]
  transfers between devices with their start and end apart: 16 -> 16, of which waited for: 7 -> 7; matrix products, arithmetic and copies ran while one was open for 1% -> 0% of each run, Pallas kernels for 11% -> 13%
where the time goes in v5:
time: 84.2 us; the launch traced here: 84.1 us
  Pallas kernels  36.3 us (43%)
  starting transfers between devices  24.1 us (29%)
  waiting for transfers between devices  17.6 us (21%)
  local copies, waits for them, and re-layouts  3.04 us (4%)
  other arithmetic  2.82 us (3%)
    pallas_call x2, Pallas kernels, down_call(): pl.pallas_call(functools.partial(down_kernel, first_window), out_shape=sh...  20.6 us
    ppermute x8, waiting for transfers between devices, local(): lax.ppermute(answers[1 + g], ('outer', 'inner'), group_route(g, -1))  13.2 us
    ppermute x8, starting transfers between devices, local(): lax.ppermute(parts[1 + g], ('outer', 'inner'), group_route(g, 1))  12.4 us
    ppermute x8, starting transfers between devices, local(): lax.ppermute(answers[1 + g], ('outer', 'inner'), group_route(g, -1))  11.7 us
    pallas_call x1, Pallas kernels, local(): up(brick_window, block_offset, xt, entry_rows, w_up_t, answers[0], *retur...  10.4 us
    pallas_call x1, Pallas kernels, local(): coarse(cell_window, cells, b_down.reshape(1, out_width), cell_partial, *a...  5.28 us
    ppermute x8, waiting for transfers between devices, local(): lax.ppermute(parts[1 + g], ('outer', 'inner'), group_route(g, 1))  4.38 us
  transfers between devices with their start and end apart: 16, of which 7 were waited for; matrix products, arithmetic and copies ran while one was open for 0% of the time, Pallas kernels for 13%

profile of v5, /device:TPU:24, one launch (start us, length us, event | category | flops | bytes accessed | tf_op | source)
XLA Modules:
  0.0 84.1 jit_solution(12630976013977319482)
XLA Ops:
  0.0 1.0 %slice_reduce_fusion = s32[256]{0:T(256)S(1)} fusion(s32[256,128]{1,0:T(8,128)} %bitcast.9), kind=kLoop, calls=%fused_computation | loop fusion | bytes 2048 | tf_op jit(solution)/shard_map/slice | solution.py:225
  1.0 0.6 and_select_fusion.1.win_ref
  1.6 0.1 squeeze.6
  1.7 0.1 convert_reduce_fusion.count_ref
  1.8 0.9 %reduce_min.9 = s32[64]{0:T(128)S(1)} reduce(s32[64,128]{1,0:T(8,128)} %bitcast.13, s32[]{:T(128)} %constant.33.clone.1), dimensions={1}, to_apply=%region_0.1 | reduce | flops 8128 | bytes 33028 | tf_op jit(solution)/shard_map/reduce_min | solution.py:227
  2.7 0.5 and_select_fusion.cw_ref
  3.2 0.2 reduce_window_sum.18
  3.5 0.2 reduce_window_sum.17
  3.7 0.1 fusion.2
  3.8 0.1 select_reduce_fusion
  3.9 0.7 reshape.114.order_ref
  4.6 0.0 copy-done.16
  4.6 9.9 %shard_map.74 = (bf16[512,128]{1,0:T(8,128)(2,1)}, bf16[512,128]{1,0:T(8,128)(2,1)}, bf16[512,128]{1,0:T(8,128)(2,1)}, bf16[512,128]{1,0:T(8,128)(2,1)}, bf16[51...) custom-call(s32[4]{0:T(128)} %copy-done.16, ...), custom_call_target="tpu_custom_call" | custom-call | flops 536870912 | bytes 5373952 | tf_op jit(solution)/shard_map/pallas_call | solution.py:250
  14.5 5.9 %collective-permute-start = (bf16[512,128]{1,0:T(8,128)(2,1)}, bf16[512,128]{1,0:T(8,128)(2,1)S(1)}, u32[]{:S(2)}, u32[]{:S(2)}) collective-permute-start(bf16[512,128]{1,0:T(8,128)(2,1)} %get-tuple-element.22), channel_id=1, source_target_pairs={{0,127},{1,120},{2,121},{3,122},{4,123},{5,124},{6,125},{7,126},{8... | collective-permute-start | bytes 393224 | tf_op jit(solution)/shard_map/ppermute | solution.py:277
  20.4 2.1 %collective-permute-start.1 = (bf16[512,128]{1,0:T(8,128)(2,1)}, bf16[512,128]{1,0:T(8,128)(2,1)S(1)}, u32[]{:S(2)}, u32[]{:S(2)}) collective-permute-start(bf16[512,128]{1,0:T(8,128)(2,1)} %get-tuple-element.23), channel_id=1, source_target_pairs={{0,120},{1,121},{2,122},{3,123},{4,124},{5,125},{6,126},{7,127},{8... | collective-permute-start | bytes 393224 | tf_op jit(solution)/shard_map/ppermute | solution.py:277
  22.5 0.0 collective-permute-start.2
  22.5 1.2 %collective-permute-start.3 = (bf16[512,128]{1,0:T(8,128)(2,1)}, bf16[512,128]{1,0:T(8,128)(2,1)S(1)}, u32[]{:S(2)}, u32[]{:S(2)}) collective-permute-start(bf16[512,128]{1,0:T(8,128)(2,1)} %get-tuple-element.25), channel_id=1, source_target_pairs={{0,7},{1,0},{2,1},{3,2},{4,3},{5,4},{6,5},{7,6},{8,15},{9,8},{10,9... | collective-permute-start | bytes 393224 | tf_op jit(solution)/shard_map/ppermute | solution.py:277
  23.7 0.7 collective-permute-start.4
  24.4 0.0 collective-permute-done.refs_0_
  24.4 2.5 %collective-permute-start.5 = (bf16[512,128]{1,0:T(8,128)(2,1)}, bf16[512,128]{1,0:T(8,128)(2,1)S(1)}, u32[]{:S(2)}, u32[]{:S(2)}) collective-permute-start(bf16[512,128]{1,0:T(8,128)(2,1)} %get-tuple-element.27), channel_id=1, source_target_pairs={{0,15},{1,8},{2,9},{3,10},{4,11},{5,12},{6,13},{7,14},{8,23},{9,16... | collective-permute-start | bytes 393224 | tf_op jit(solution)/shard_map/ppermute | solution.py:277
  26.9 0.3 collective-permute-done.1.refs_1_
  27.2 0.0 collective-permute-start.6
  27.2 3.8 %collective-permute-done.2.refs_2_ = bf16[512,128]{1,0:T(8,128)(2,1)S(1)} collective-permute-done((bf16[512,128]{1,0:T(8,128)(2,1)}, bf16[512,128]{1,0:T(8,128)(2,1)S(1)}, u32[]{:S(2)}, u32[]{:S(2)}) %collective-permute-start.2) | collective-permute-done | bytes 131104 | tf_op jit(solution)/shard_map/ppermute | solution.py:277
  31.0 0.0 collective-permute-start.7
  31.0 10.7 %shard_map.73.partial_ref = f32[4096,128]{1,0:T(8,128)} custom-call(s32[4]{0:T(128)} %copy-done.16, s32[256]{0:T(256)} %reshape.114.order_ref, s32[256]{0:T(256)} %and_select_fusion.1.win_ref, s32[256]{0:T(256)} %off_ref.5, s32[64]{0:T(128)} %and_select_fusion.cw_ref, bf16[64,32768]{1,0:T(8,128)(2,1)} %bitcast.7, s32[256,128]{1,0:T(8,128)} %bitcast.11, ...), custom_call_target="tpu_custom_call" | custom-call | flops 536870912 | bytes 5373952 | tf_op jit(solution)/shard_map/pallas_call | solution.py:250
  41.8 0.0 collective-permute-done.3.refs_3_
  41.8 0.0 collective-permute-done.4.refs_4_
  41.8 0.0 copy-start.12
  41.8 0.0 collective-permute-done.5.refs_5_
  41.8 0.0 copy-start.13
  41.8 0.0 collective-permute-done.6.refs_6_
  41.8 0.2 collective-permute-done.7.refs_7_
  42.1 0.0 copy-done.8
  42.1 0.0 copy-done.10
  42.1 0.4 copy-done.11
  42.4 0.0 copy-done.12
  42.5 0.1 copy-done.13
  42.5 0.0 copy-done.14
  42.6 0.1 copy-done.15
  42.7 5.3 %shard_map.75 = (bf16[128,4096]{1,0:T(8,128)(2,1)}, bf16[128,512]{1,0:T(8,128)(2,1)}, bf16[128,512]{1,0:T(8,128)(2,1)}, bf16[128,512]{1,0:T(8,128)(2,1)}, bf16[1...) custom-call(s32[64]{0:T(128)} %and_select_fusion.cw_ref, ...), custom_call_target="tpu_custom_call" | custom-call | flops 536870912 | bytes 4194304 | tf_op jit(solution)/shard_map/pallas_call | solution.py:300
  48.0 0.0 collective-permute-start.8
  48.0 3.9 %collective-permute-start.9 = (bf16[128,512]{1,0:T(8,128)(2,1)}, bf16[128,512]{1,0:T(8,128)(2,1)S(1)}, u32[]{:S(2)}, u32[]{:S(2)}) collective-permute-start(bf16[128,512]{1,0:T(8,128)(2,1)} %get-tuple-element.32), channel_id=1, source_target_pairs={{120,0},{121,1},{122,2},{123,3},{124,4},{125,5},{126,6},{127,7},{0... | collective-permute-start | bytes 393224 | tf_op jit(solution)/shard_map/ppermute | solution.py:303
  51.9 0.0 collective-permute-start.10
  51.9 0.1 collective-permute-start.11
  52.1 1.6 %collective-permute-start.12 = (bf16[128,512]{1,0:T(8,128)(2,1)}, bf16[128,512]{1,0:T(8,128)(2,1)S(1)}, u32[]{:S(2)}, u32[]{:S(2)}) collective-permute-start(bf16[128,512]{1,0:T(8,128)(2,1)} %get-tuple-element.35), channel_id=1, source_target_pairs={{1,0},{2,1},{3,2},{4,3},{5,4},{6,5},{7,6},{0,7},{9,8},{10,9},{11,1... | collective-permute-start | bytes 393224 | tf_op jit(solution)/shard_map/ppermute | solution.py:303
  53.7 4.0 %collective-permute-done.8.refs_1_ = bf16[128,512]{1,0:T(8,128)(2,1)S(1)} collective-permute-done((bf16[128,512]{1,0:T(8,128)(2,1)}, bf16[128,512]{1,0:T(8,128)(2,1)S(1)}, u32[]{:S(2)}, u32[]{:S(2)}) %collective-permute-start.8) | collective-permute-done | bytes 131104 | tf_op jit(solution)/shard_map/ppermute | solution.py:303
  57.7 2.5 %collective-permute-start.13 = (bf16[128,512]{1,0:T(8,128)(2,1)}, bf16[128,512]{1,0:T(8,128)(2,1)S(1)}, u32[]{:S(2)}, u32[]{:S(2)}) collective-permute-start(bf16[128,512]{1,0:T(8,128)(2,1)} %get-tuple-element.36), channel_id=1, source_target_pairs={{15,0},{8,1},{9,2},{10,3},{11,4},{12,5},{13,6},{14,7},{23,8},{16,9... | collective-permute-start | bytes 393224 | tf_op jit(solution)/shard_map/ppermute | solution.py:303
  60.2 0.0 collective-permute-done.9.refs_2_
  60.2 3.5 %collective-permute-start.14 = (bf16[128,512]{1,0:T(8,128)(2,1)}, bf16[128,512]{1,0:T(8,128)(2,1)S(1)}, u32[]{:S(2)}, u32[]{:S(2)}) collective-permute-start(bf16[128,512]{1,0:T(8,128)(2,1)} %get-tuple-element.37), channel_id=1, source_target_pairs={{8,0},{9,1},{10,2},{11,3},{12,4},{13,5},{14,6},{15,7},{16,8},{17,9... | collective-permute-start | bytes 393224 | tf_op jit(solution)/shard_map/ppermute | solution.py:303
  63.7 2.0 %collective-permute-done.10.refs_3_ = bf16[128,512]{1,0:T(8,128)(2,1)S(1)} collective-permute-done((bf16[128,512]{1,0:T(8,128)(2,1)}, bf16[128,512]{1,0:T(8,128)(2,1)S(1)}, u32[]{:S(2)}, u32[]{:S(2)}) %collective-permute-start.10) | collective-permute-done | bytes 131104 | tf_op jit(solution)/shard_map/ppermute | solution.py:303
  65.7 0.0 collective-permute-start.15
  65.7 0.0 collective-permute-done.11.refs_4_
  65.8 0.0 collective-permute-done.12.refs_5_
  65.8 0.0 collective-permute-done.13.refs_6_
  65.8 0.0 copy-start.5
  65.8 1.6 %collective-permute-done.14.refs_7_ = bf16[128,512]{1,0:T(8,128)(2,1)S(1)} collective-permute-done((bf16[128,512]{1,0:T(8,128)(2,1)}, bf16[128,512]{1,0:T(8,128)(2,1)S(1)}, u32[]{:S(2)}, u32[]{:S(2)}) %collective-permute-start.14) | collective-permute-done | bytes 131104 | tf_op jit(solution)/shard_map/ppermute | solution.py:303
  67.4 5.6 %collective-permute-done.15.refs_8_ = bf16[128,512]{1,0:T(8,128)(2,1)S(1)} collective-permute-done((bf16[128,512]{1,0:T(8,128)(2,1)}, bf16[128,512]{1,0:T(8,128)(2,1)S(1)}, u32[]{:S(2)}, u32[]{:S(2)}) %collective-permute-start.15) | collective-permute-done | bytes 131104 | tf_op jit(solution)/shard_map/ppermute | solution.py:303
  73.0 0.0 copy-done.1
  73.0 0.0 copy-done.3
  73.0 0.0 copy-done.4
  73.0 0.0 copy-done.5
  73.1 0.0 copy-done.6
  73.1 0.6 copy-done.7
  73.7 10.4 %shard_map.76 = bf16[64,32768]{1,0:T(8,128)(2,1)} custom-call(s32[256]{0:T(256)} %and_select_fusion.1.win_ref, s32[256]{0:T(256)} %off_ref.5, bf16[64,32768]{1,0:T(8,128)(2,1)} %bitcast.8, s32[256,128]{1,0:T(8,128)} %bitcast.12, bf16[8,64,128]{2,1,0:T(8,128)(2,1)} %bitcast.17, bf16[128,4096]{1,0:T(8,128)(2,1)} %get-tuple-element.30.refs_0_, ...), custom_call_target="tpu_custom_call" | custom-call | flops 1610612736 | bytes 10616832 | tf_op jit(solution)/shard_map/pallas_call | solution.py:331
  (19 shorter events, 0.0 us)
Async XLA Ops:
  1.8 2.8 %copy-start.16 = (s32[4]{0:T(128)}, s32[4]{0:T(128)S(1)}, u32[]{:S(2)}) copy-start(s32[4]{0:T(128)S(1)} %convert_reduce_fusion.count_ref) | copy-start | bytes 52
  14.5 9.9 %collective-permute-start = (bf16[512,128]{1,0:T(8,128)(2,1)}, bf16[512,128]{1,0:T(8,128)(2,1)S(1)}, u32[]{:S(2)}, u32[]{:S(2)}) collective-permute-start(bf16[512,128]{1,0:T(8,128)(2,1)} %get-tuple-element.22), channel_id=1, source_target_pairs={{0,127},{1,120},{2,121},{3,122},{4,123},{5,124},{6,125},{7,126},{8... | collective-permute-start | bytes 393224 | tf_op jit(solution)/shard_map/ppermute | solution.py:277
  20.4 6.8 %collective-permute-start.1 = (bf16[512,128]{1,0:T(8,128)(2,1)}, bf16[512,128]{1,0:T(8,128)(2,1)S(1)}, u32[]{:S(2)}, u32[]{:S(2)}) collective-permute-start(bf16[512,128]{1,0:T(8,128)(2,1)} %get-tuple-element.23), channel_id=1, source_target_pairs={{0,120},{1,121},{2,122},{3,123},{4,124},{5,125},{6,126},{7,127},{8... | collective-permute-start | bytes 393224 | tf_op jit(solution)/shard_map/ppermute | solution.py:277
  22.5 8.5 %collective-permute-start.2 = (bf16[512,128]{1,0:T(8,128)(2,1)}, bf16[512,128]{1,0:T(8,128)(2,1)S(1)}, u32[]{:S(2)}, u32[]{:S(2)}) collective-permute-start(bf16[512,128]{1,0:T(8,128)(2,1)} %get-tuple-element.24), channel_id=1, source_target_pairs={{0,121},{1,122},{2,123},{3,124},{4,125},{5,126},{6,127},{7,120},{8... | collective-permute-start | bytes 393224 | tf_op jit(solution)/shard_map/ppermute | solution.py:277
  22.5 19.3 %collective-permute-start.3 = (bf16[512,128]{1,0:T(8,128)(2,1)}, bf16[512,128]{1,0:T(8,128)(2,1)S(1)}, u32[]{:S(2)}, u32[]{:S(2)}) collective-permute-start(bf16[512,128]{1,0:T(8,128)(2,1)} %get-tuple-element.25), channel_id=1, source_target_pairs={{0,7},{1,0},{2,1},{3,2},{4,3},{5,4},{6,5},{7,6},{8,15},{9,8},{10,9... | collective-permute-start | bytes 393224 | tf_op jit(solution)/shard_map/ppermute | solution.py:277
  23.7 18.1 %collective-permute-start.4 = (bf16[512,128]{1,0:T(8,128)(2,1)}, bf16[512,128]{1,0:T(8,128)(2,1)S(1)}, u32[]{:S(2)}, u32[]{:S(2)}) collective-permute-start(bf16[512,128]{1,0:T(8,128)(2,1)} %get-tuple-element.26), channel_id=1, source_target_pairs={{0,1},{1,2},{2,3},{3,4},{4,5},{5,6},{6,7},{7,0},{8,9},{9,10},{10,1... | collective-permute-start | bytes 393224 | tf_op jit(solution)/shard_map/ppermute | solution.py:277
  24.4 17.7 %copy-start.8 = (bf16[512,128]{1,0:T(8,128)(2,1)}, bf16[512,128]{1,0:T(8,128)(2,1)S(1)}, u32[]{:S(2)}) copy-start(bf16[512,128]{1,0:T(8,128)(2,1)S(1)} %collective-permute-done.refs_0_) | copy-start | bytes 393220
  24.4 17.4 %collective-permute-start.5 = (bf16[512,128]{1,0:T(8,128)(2,1)}, bf16[512,128]{1,0:T(8,128)(2,1)S(1)}, u32[]{:S(2)}, u32[]{:S(2)}) collective-permute-start(bf16[512,128]{1,0:T(8,128)(2,1)} %get-tuple-element.27), channel_id=1, source_target_pairs={{0,15},{1,8},{2,9},{3,10},{4,11},{5,12},{6,13},{7,14},{8,23},{9,16... | collective-permute-start | bytes 393224 | tf_op jit(solution)/shard_map/ppermute | solution.py:277
  27.2 14.9 %copy-start.9 = (bf16[512,128]{1,0:T(8,128)(2,1)}, bf16[512,128]{1,0:T(8,128)(2,1)S(1)}, u32[]{:S(2)}) copy-start(bf16[512,128]{1,0:T(8,128)(2,1)S(1)} %collective-permute-done.1.refs_1_) | copy-start | bytes 393220
  27.2 14.6 %collective-permute-start.6 = (bf16[512,128]{1,0:T(8,128)(2,1)}, bf16[512,128]{1,0:T(8,128)(2,1)S(1)}, u32[]{:S(2)}, u32[]{:S(2)}) collective-permute-start(bf16[512,128]{1,0:T(8,128)(2,1)} %get-tuple-element.28), channel_id=1, source_target_pairs={{0,8},{1,9},{2,10},{3,11},{4,12},{5,13},{6,14},{7,15},{8,16},{9,17... | collective-permute-start | bytes 393224 | tf_op jit(solution)/shard_map/ppermute | solution.py:277
  31.0 11.1 %copy-start.10 = (bf16[512,128]{1,0:T(8,128)(2,1)}, bf16[512,128]{1,0:T(8,128)(2,1)S(1)}, u32[]{:S(2)}) copy-start(bf16[512,128]{1,0:T(8,128)(2,1)S(1)} %collective-permute-done.2.refs_2_) | copy-start | bytes 393220
  31.0 11.0 %collective-permute-start.7 = (bf16[512,128]{1,0:T(8,128)(2,1)}, bf16[512,128]{1,0:T(8,128)(2,1)S(1)}, u32[]{:S(2)}, u32[]{:S(2)}) collective-permute-start(bf16[512,128]{1,0:T(8,128)(2,1)} %get-tuple-element.29), channel_id=1, source_target_pairs={{0,9},{1,10},{2,11},{3,12},{4,13},{5,14},{6,15},{7,8},{8,17},{9,18... | collective-permute-start | bytes 393224 | tf_op jit(solution)/shard_map/ppermute | solution.py:277
  41.8 0.7 copy-start.11
  41.8 0.7 copy-start.12
  41.8 0.7 copy-start.13
  41.8 0.7 copy-start.14
  42.1 0.6 copy-start.15
  48.0 9.7 %collective-permute-start.8 = (bf16[128,512]{1,0:T(8,128)(2,1)}, bf16[128,512]{1,0:T(8,128)(2,1)S(1)}, u32[]{:S(2)}, u32[]{:S(2)}) collective-permute-start(bf16[128,512]{1,0:T(8,128)(2,1)} %get-tuple-element.31), channel_id=1, source_target_pairs={{127,0},{120,1},{121,2},{122,3},{123,4},{124,5},{125,6},{126,7},{7... | collective-permute-start | bytes 393224 | tf_op jit(solution)/shard_map/ppermute | solution.py:303
  48.0 12.2 %collective-permute-start.9 = (bf16[128,512]{1,0:T(8,128)(2,1)}, bf16[128,512]{1,0:T(8,128)(2,1)S(1)}, u32[]{:S(2)}, u32[]{:S(2)}) collective-permute-start(bf16[128,512]{1,0:T(8,128)(2,1)} %get-tuple-element.32), channel_id=1, source_target_pairs={{120,0},{121,1},{122,2},{123,3},{124,4},{125,5},{126,6},{127,7},{0... | collective-permute-start | bytes 393224 | tf_op jit(solution)/shard_map/ppermute | solution.py:303
  51.9 13.8 %collective-permute-start.10 = (bf16[128,512]{1,0:T(8,128)(2,1)}, bf16[128,512]{1,0:T(8,128)(2,1)S(1)}, u32[]{:S(2)}, u32[]{:S(2)}) collective-permute-start(bf16[128,512]{1,0:T(8,128)(2,1)} %get-tuple-element.33), channel_id=1, source_target_pairs={{121,0},{122,1},{123,2},{124,3},{125,4},{126,5},{127,6},{120,7},{1... | collective-permute-start | bytes 393224 | tf_op jit(solution)/shard_map/ppermute | solution.py:303
  51.9 13.8 %collective-permute-start.11 = (bf16[128,512]{1,0:T(8,128)(2,1)}, bf16[128,512]{1,0:T(8,128)(2,1)S(1)}, u32[]{:S(2)}, u32[]{:S(2)}) collective-permute-start(bf16[128,512]{1,0:T(8,128)(2,1)} %get-tuple-element.34), channel_id=1, source_target_pairs={{7,0},{0,1},{1,2},{2,3},{3,4},{4,5},{5,6},{6,7},{15,8},{8,9},{9,10... | collective-permute-start | bytes 393224 | tf_op jit(solution)/shard_map/ppermute | solution.py:303
  52.1 13.7 %collective-permute-start.12 = (bf16[128,512]{1,0:T(8,128)(2,1)}, bf16[128,512]{1,0:T(8,128)(2,1)S(1)}, u32[]{:S(2)}, u32[]{:S(2)}) collective-permute-start(bf16[128,512]{1,0:T(8,128)(2,1)} %get-tuple-element.35), channel_id=1, source_target_pairs={{1,0},{2,1},{3,2},{4,3},{5,4},{6,5},{7,6},{0,7},{9,8},{10,9},{11,1... | collective-permute-start | bytes 393224 | tf_op jit(solution)/shard_map/ppermute | solution.py:303
  57.7 15.3 %copy-start = (bf16[128,512]{1,0:T(8,128)(2,1)}, bf16[128,512]{1,0:T(8,128)(2,1)S(1)}, u32[]{:S(2)}) copy-start(bf16[128,512]{1,0:T(8,128)(2,1)S(1)} %collective-permute-done.8.refs_1_) | copy-start | bytes 393220
  57.7 8.1 %collective-permute-start.13 = (bf16[128,512]{1,0:T(8,128)(2,1)}, bf16[128,512]{1,0:T(8,128)(2,1)S(1)}, u32[]{:S(2)}, u32[]{:S(2)}) collective-permute-start(bf16[128,512]{1,0:T(8,128)(2,1)} %get-tuple-element.36), channel_id=1, source_target_pairs={{15,0},{8,1},{9,2},{10,3},{11,4},{12,5},{13,6},{14,7},{23,8},{16,9... | collective-permute-start | bytes 393224 | tf_op jit(solution)/shard_map/ppermute | solution.py:303
  60.2 12.8 %copy-start.1 = (bf16[128,512]{1,0:T(8,128)(2,1)}, bf16[128,512]{1,0:T(8,128)(2,1)S(1)}, u32[]{:S(2)}) copy-start(bf16[128,512]{1,0:T(8,128)(2,1)S(1)} %collective-permute-done.9.refs_2_) | copy-start | bytes 393220
  60.2 7.2 %collective-permute-start.14 = (bf16[128,512]{1,0:T(8,128)(2,1)}, bf16[128,512]{1,0:T(8,128)(2,1)S(1)}, u32[]{:S(2)}, u32[]{:S(2)}) collective-permute-start(bf16[128,512]{1,0:T(8,128)(2,1)} %get-tuple-element.37), channel_id=1, source_target_pairs={{8,0},{9,1},{10,2},{11,3},{12,4},{13,5},{14,6},{15,7},{16,8},{17,9... | collective-permute-start | bytes 393224 | tf_op jit(solution)/shard_map/ppermute | solution.py:303
  65.7 7.3 %copy-start.2 = (bf16[128,512]{1,0:T(8,128)(2,1)}, bf16[128,512]{1,0:T(8,128)(2,1)S(1)}, u32[]{:S(2)}) copy-start(bf16[128,512]{1,0:T(8,128)(2,1)S(1)} %collective-permute-done.10.refs_3_) | copy-start | bytes 393220
  65.7 7.3 %collective-permute-start.15 = (bf16[128,512]{1,0:T(8,128)(2,1)}, bf16[128,512]{1,0:T(8,128)(2,1)S(1)}, u32[]{:S(2)}, u32[]{:S(2)}) collective-permute-start(bf16[128,512]{1,0:T(8,128)(2,1)} %get-tuple-element.38), channel_id=1, source_target_pairs={{9,0},{10,1},{11,2},{12,3},{13,4},{14,5},{15,6},{8,7},{17,8},{18,9... | collective-permute-start | bytes 393224 | tf_op jit(solution)/shard_map/ppermute | solution.py:303
  65.8 7.3 %copy-start.3 = (bf16[128,512]{1,0:T(8,128)(2,1)}, bf16[128,512]{1,0:T(8,128)(2,1)S(1)}, u32[]{:S(2)}) copy-start(bf16[128,512]{1,0:T(8,128)(2,1)S(1)} %collective-permute-done.11.refs_4_) | copy-start | bytes 393220
  65.8 7.3 %copy-start.4 = (bf16[128,512]{1,0:T(8,128)(2,1)}, bf16[128,512]{1,0:T(8,128)(2,1)S(1)}, u32[]{:S(2)}) copy-start(bf16[128,512]{1,0:T(8,128)(2,1)S(1)} %collective-permute-done.12.refs_5_) | copy-start | bytes 393220
  65.8 7.3 %copy-start.5 = (bf16[128,512]{1,0:T(8,128)(2,1)}, bf16[128,512]{1,0:T(8,128)(2,1)S(1)}, u32[]{:S(2)}) copy-start(bf16[128,512]{1,0:T(8,128)(2,1)S(1)} %collective-permute-done.13.refs_6_) | copy-start | bytes 393220
  67.4 5.6 %copy-start.6 = (bf16[128,512]{1,0:T(8,128)(2,1)}, bf16[128,512]{1,0:T(8,128)(2,1)S(1)}, u32[]{:S(2)}) copy-start(bf16[128,512]{1,0:T(8,128)(2,1)S(1)} %collective-permute-done.14.refs_7_) | copy-start | bytes 393220
  73.0 0.7 copy-start.7

commit v6 on v3

--- a/solution.py
+++ b/solution.py
@@ -57,7 +57,7 @@
                 position = first + u * width + t
                 j = order_ref[step * per_step + jnp.minimum(position, per_step - 1)]
                 brick = step * per_step + j
-                window = jnp.where(position < stop, win_ref[brick] - first_window, trash)
+                window = jnp.where(position < stop, jnp.right_shift(win_ref[brick], 7) - first_window, trash)
                 offset = off_ref[brick]
                 inside = jnp.bitwise_and(e_ref[pl.ds(j, 1), :], WIN - 1)
                 pick = one_hot_rows(inside)
@@ -159,7 +159,7 @@
         for t in range(UP_UNROLL):
             j = u * UP_UNROLL + t
             brick = step * per_step + j
-            window = win_ref[brick]
+            window = jnp.right_shift(win_ref[brick], 7)
             offset = off_ref[brick]
             inside = jnp.bitwise_and(e_ref[pl.ds(j, 1), :], WIN - 1)
             pick = one_hot_rows(inside)
@@ -196,7 +196,7 @@
 
     xt = features.T
     entry_rows = parent_entry.reshape(blocks, BLK)
-    brick_window = entry_rows[:, 0] // WIN
+    brick_first = entry_rows[:, 0]
     cells = owner_cell.reshape(entries // WIN, WIN)
     cell_window = jnp.min(cells, axis=1) // WIN
     w_up_t = jnp.swapaxes(w_up, 1, 2)
@@ -207,7 +207,7 @@
     answer_shapes = [jax.ShapeDtypeStruct((s.shape[1], s.shape[0]), s.dtype) for s in part_shapes]
     whole = lambda shape: pl.BlockSpec(shape, lambda *idx: (0,) * len(shape))
 
-    is_far = (brick_window >= SELF_CAP // WIN).astype(jnp.int32).reshape(steps, BRICKS_PER_STEP)
+    is_far = (brick_first >= SELF_CAP).astype(jnp.int32).reshape(steps, BRICKS_PER_STEP)
     far_count = jnp.sum(is_far, axis=1)
     far_rank = jnp.cumsum(is_far, axis=1) - is_far
     own_rank = jnp.cumsum(1 - is_far, axis=1) - (1 - is_far)
@@ -241,7 +241,7 @@
                 transcendentals=0,
                 bytes_accessed=fine_rows * (in_width * 2 + 4) + rows * out_width * 2,
             ),
-        )(counts, order, brick_window, block_offset, xt, entry_rows, w_down)
+        )(counts, order, brick_first, block_offset, xt, entry_rows, w_down)
 
     parts = [None] + list(down_call(SELF_CAP // WIN, part_shapes[1:]))
     parts[0] = down_call(0, part_shapes[:1])[0]
@@ -301,7 +301,7 @@
             bytes_accessed=fine_rows * (in_width * 4 + 4) + entries * out_width * 2,
         ),
     )
-    out_t = up(brick_window, block_offset, xt, entry_rows, w_up_t, answers[0], *returned)
+    out_t = up(brick_first, block_offset, xt, entry_rows, w_up_t, answers[0], *returned)
     return out_t.T
 
 

time: 82.1 us -> 82 us (level); the launches traced: 82 us -> 80.6 us
  waiting for transfers between devices: 22.6 us -> 18.5 us
  starting transfers between devices: 19.2 us -> 21.3 us
  local copies, waits for them, and re-layouts: 3.02 us -> 1.98 us
  other arithmetic: 2.2 us -> 3.2 us
    ppermute x8, waiting for transfers between devices: 17.2 us -> 11.7 us  [local(): lax.ppermute(answers[1 + g], ('outer', 'inner'), group_route(g, -1))]
    ppermute x8, starting transfers between devices: 6.94 us -> 11 us  [local(): lax.ppermute(answers[1 + g], ('outer', 'inner'), group_route(g, -1))]
    ppermute x8, starting transfers between devices: 12.3 us -> 10.3 us  [local(): lax.ppermute(parts[1 + g], ('outer', 'inner'), group_route(g, 1))]
    convert_element_type x1, other arithmetic: 0.01 us -> 1.65 us  [local(): (brick_first >= SELF_CAP).astype(jnp.int32).reshape(steps, BRICKS_PER_STEP)]
    ppermute x8, waiting for transfers between devices: 5.42 us -> 6.81 us  [local(): lax.ppermute(parts[1 + g], ('outer', 'inner'), group_route(g, 1))]
    slice x1 -> x0, local copies, waits for them, and re-layouts: 1.01 us -> none  [local(): brick_window = entry_rows[:, 0] // WIN]
  transfers between devices with their start and end apart: 16 -> 16, of which waited for: 7 -> 9; matrix products, arithmetic and copies ran while one was open for 1% -> 1% of each run, Pallas kernels for 11% -> 12%
where the time goes in v6:
time: 82 us; the launch traced here: 80.6 us
  Pallas kernels  35.5 us (43%)
  starting transfers between devices  21.3 us (26%)
  waiting for transfers between devices  18.5 us (23%)
  other arithmetic  3.2 us (4%)
  local copies, waits for them, and re-layouts  1.98 us (2%)
    pallas_call x2, Pallas kernels, down_call(): pl.pallas_call(functools.partial(down_kernel, first_window), out_shape=sh...  19.8 us
    ppermute x8, waiting for transfers between devices, local(): lax.ppermute(answers[1 + g], ('outer', 'inner'), group_route(g, -1))  11.7 us
    ppermute x8, starting transfers between devices, local(): lax.ppermute(answers[1 + g], ('outer', 'inner'), group_route(g, -1))  11 us
    pallas_call x1, Pallas kernels, local(): up(brick_first, block_offset, xt, entry_rows, w_up_t, answers[0], *returned)  10.4 us
    ppermute x8, starting transfers between devices, local(): lax.ppermute(parts[1 + g], ('outer', 'inner'), group_route(g, 1))  10.3 us
    ppermute x8, waiting for transfers between devices, local(): lax.ppermute(parts[1 + g], ('outer', 'inner'), group_route(g, 1))  6.81 us
    pallas_call x1, Pallas kernels, local(): coarse(cell_window, cells, b_down.reshape(1, out_width), parts[0], *arrived)  5.31 us
    convert_element_type x1, other arithmetic, local(): (brick_first >= SELF_CAP).astype(jnp.int32).reshape(steps, BRICKS_PER_STEP)  1.65 us
  transfers between devices with their start and end apart: 16, of which 9 were waited for; matrix products, arithmetic and copies ran while one was open for 1% of the time, Pallas kernels for 12%

profile of v6, /device:TPU:24, one launch (start us, length us, event | category | flops | bytes accessed | tf_op | source)
XLA Modules:
  0.0 80.6 jit_solution(5843699439170038690)
XLA Ops:
  0.0 1.7 %convert_reduce_fusion = (s32[256]{0:T(256)S(1)}, s32[256]{0:T(256)}) fusion(s32[256,128]{1,0:T(8,128)} %bitcast.9), kind=kLoop, calls=%fused_computation | loop fusion | flops 512 | bytes 3072 | tf_op jit(solution)/shard_map/convert_element_type | solution.py:210
  1.7 0.1 reshape.65
  1.7 0.1 broadcast_subtract_fusion
  1.9 0.2 reduce_window_sum.17
  2.1 0.2 reduce_window_sum.18
  2.3 0.1 add_select_fusion
  2.4 0.1 select_reduce_fusion
  2.6 0.6 reshape.64.order_ref
  3.2 0.0 copy-done.17
  3.2 9.9 %shard_map.74 = (bf16[512,128]{1,0:T(8,128)(2,1)}, bf16[512,128]{1,0:T(8,128)(2,1)}, bf16[512,128]{1,0:T(8,128)(2,1)}, bf16[512,128]{1,0:T(8,128)(2,1)}, bf16[51...) custom-call(s32[4]{0:T(128)} %copy-done.17, ...), custom_call_target="tpu_custom_call" | custom-call | flops 536870912 | bytes 5373952 | tf_op jit(solution)/shard_map/pallas_call | solution.py:224
  13.1 7.2 %collective-permute-start = (bf16[512,128]{1,0:T(8,128)(2,1)}, bf16[512,128]{1,0:T(8,128)(2,1)S(1)}, u32[]{:S(2)}, u32[]{:S(2)}) collective-permute-start(bf16[512,128]{1,0:T(8,128)(2,1)} %get-tuple-element.22), channel_id=1, source_target_pairs={{0,127},{1,120},{2,121},{3,122},{4,123},{5,124},{6,125},{7,126},{8... | collective-permute-start | bytes 393224 | tf_op jit(solution)/shard_map/ppermute | solution.py:250
  20.2 0.0 collective-permute-start.1
  20.2 1.0 %collective-permute-start.2 = (bf16[512,128]{1,0:T(8,128)(2,1)}, bf16[512,128]{1,0:T(8,128)(2,1)S(1)}, u32[]{:S(2)}, u32[]{:S(2)}) collective-permute-start(bf16[512,128]{1,0:T(8,128)(2,1)} %get-tuple-element.24), channel_id=1, source_target_pairs={{0,121},{1,122},{2,123},{3,124},{4,125},{5,126},{6,127},{7,120},{8... | collective-permute-start | bytes 393224 | tf_op jit(solution)/shard_map/ppermute | solution.py:250
  21.2 1.5 %collective-permute-start.3 = (bf16[512,128]{1,0:T(8,128)(2,1)}, bf16[512,128]{1,0:T(8,128)(2,1)S(1)}, u32[]{:S(2)}, u32[]{:S(2)}) collective-permute-start(bf16[512,128]{1,0:T(8,128)(2,1)} %get-tuple-element.25), channel_id=1, source_target_pairs={{0,7},{1,0},{2,1},{3,2},{4,3},{5,4},{6,5},{7,6},{8,15},{9,8},{10,9... | collective-permute-start | bytes 393224 | tf_op jit(solution)/shard_map/ppermute | solution.py:250
  22.7 0.0 collective-permute-start.4
  22.7 0.0 copy-done.8
  22.7 0.1 reduce_min.9
  22.8 1.4 %collective-permute-done.refs_1_ = bf16[512,128]{1,0:T(8,128)(2,1)S(1)} collective-permute-done((bf16[512,128]{1,0:T(8,128)(2,1)}, bf16[512,128]{1,0:T(8,128)(2,1)S(1)}, u32[]{:S(2)}, u32[]{:S(2)}) %collective-permute-start) | collective-permute-done | bytes 131104 | tf_op jit(solution)/shard_map/ppermute | solution.py:250
  24.2 0.7 collective-permute-start.5
  24.8 2.2 %collective-permute-done.1.refs_2_ = bf16[512,128]{1,0:T(8,128)(2,1)S(1)} collective-permute-done((bf16[512,128]{1,0:T(8,128)(2,1)}, bf16[512,128]{1,0:T(8,128)(2,1)S(1)}, u32[]{:S(2)}, u32[]{:S(2)}) %collective-permute-start.1) | collective-permute-done | bytes 131104 | tf_op jit(solution)/shard_map/ppermute | solution.py:250
  27.0 0.0 collective-permute-start.6
  27.0 1.7 %collective-permute-done.2.refs_3_ = bf16[512,128]{1,0:T(8,128)(2,1)S(1)} collective-permute-done((bf16[512,128]{1,0:T(8,128)(2,1)}, bf16[512,128]{1,0:T(8,128)(2,1)S(1)}, u32[]{:S(2)}, u32[]{:S(2)}) %collective-permute-start.2) | collective-permute-done | bytes 131104 | tf_op jit(solution)/shard_map/ppermute | solution.py:250
  28.6 0.0 collective-permute-start.7
  28.6 0.6 and_select_fusion.cw_ref
  29.3 9.9 %shard_map.73.refs_0_ = bf16[4096,128]{1,0:T(8,128)(2,1)} custom-call(s32[4]{0:T(128)} %copy-done.17, s32[256]{0:T(256)} %reshape.64.order_ref, s32[256]{0:T(256)} %get-tuple-element.40.win_ref, s32[256]{0:T(256)} %off_ref.5, bf16[64,32768]{1,0:T(8,128)(2,1)} %bitcast.7, s32[256,128]{1,0:T(8,128)} %bitcast.11, bf16[8,64,128]{2,1,0:T(8,128)(2,1)} %w_ref.3), custom_call_target="tpu_custom_call" | custom-call | flops 536870912 | bytes 5373952 | tf_op jit(solution)/shard_map/pallas_call | solution.py:224
  39.2 0.0 collective-permute-done.3.refs_4_
  39.2 0.0 collective-permute-done.4.refs_5_
  39.2 0.0 copy-start.13
  39.2 0.0 collective-permute-done.5.refs_6_
  39.2 0.0 copy-start.14
  39.2 0.0 collective-permute-done.6.refs_7_
  39.2 0.0 copy-start.15
  39.2 1.6 %collective-permute-done.7.refs_8_ = bf16[512,128]{1,0:T(8,128)(2,1)S(1)} collective-permute-done((bf16[512,128]{1,0:T(8,128)(2,1)}, bf16[512,128]{1,0:T(8,128)(2,1)S(1)}, u32[]{:S(2)}, u32[]{:S(2)}) %collective-permute-start.7) | collective-permute-done | bytes 131104 | tf_op jit(solution)/shard_map/ppermute | solution.py:250
  40.8 0.0 copy-done.9
  40.8 0.0 copy-done.10
  40.9 0.0 copy-done.11
  40.9 0.0 copy-done.12
  40.9 0.0 copy-done.13
  40.9 0.0 copy-done.14
  40.9 0.0 copy-done.15
  40.9 0.6 copy-done.16
  41.5 5.3 %shard_map.75 = (bf16[128,4096]{1,0:T(8,128)(2,1)}, bf16[128,512]{1,0:T(8,128)(2,1)}, bf16[128,512]{1,0:T(8,128)(2,1)}, bf16[128,512]{1,0:T(8,128)(2,1)}, bf16[1...) custom-call(s32[64]{0:T(128)} %and_select_fusion.cw_ref, ...), custom_call_target="tpu_custom_call" | custom-call | flops 536870912 | bytes 4194304 | tf_op jit(solution)/shard_map/pallas_call | solution.py:273
  46.8 0.0 collective-permute-start.8
  46.8 3.9 %collective-permute-start.9 = (bf16[128,512]{1,0:T(8,128)(2,1)}, bf16[128,512]{1,0:T(8,128)(2,1)S(1)}, u32[]{:S(2)}, u32[]{:S(2)}) collective-permute-start(bf16[128,512]{1,0:T(8,128)(2,1)} %get-tuple-element.32), channel_id=1, source_target_pairs={{120,0},{121,1},{122,2},{123,3},{124,4},{125,5},{126,6},{127,7},{0... | collective-permute-start | bytes 393224 | tf_op jit(solution)/shard_map/ppermute | solution.py:276
  50.7 0.0 collective-permute-start.10
  50.7 0.1 collective-permute-start.11
  50.8 1.6 %collective-permute-start.12 = (bf16[128,512]{1,0:T(8,128)(2,1)}, bf16[128,512]{1,0:T(8,128)(2,1)S(1)}, u32[]{:S(2)}, u32[]{:S(2)}) collective-permute-start(bf16[128,512]{1,0:T(8,128)(2,1)} %get-tuple-element.35), channel_id=1, source_target_pairs={{1,0},{2,1},{3,2},{4,3},{5,4},{6,5},{7,6},{0,7},{9,8},{10,9},{11,1... | collective-permute-start | bytes 393224 | tf_op jit(solution)/shard_map/ppermute | solution.py:276
  52.4 4.6 %collective-permute-done.8.refs_1_ = bf16[128,512]{1,0:T(8,128)(2,1)S(1)} collective-permute-done((bf16[128,512]{1,0:T(8,128)(2,1)}, bf16[128,512]{1,0:T(8,128)(2,1)S(1)}, u32[]{:S(2)}, u32[]{:S(2)}) %collective-permute-start.8) | collective-permute-done | bytes 131104 | tf_op jit(solution)/shard_map/ppermute | solution.py:276
  57.1 1.0 %collective-permute-start.13 = (bf16[128,512]{1,0:T(8,128)(2,1)}, bf16[128,512]{1,0:T(8,128)(2,1)S(1)}, u32[]{:S(2)}, u32[]{:S(2)}) collective-permute-start(bf16[128,512]{1,0:T(8,128)(2,1)} %get-tuple-element.36), channel_id=1, source_target_pairs={{15,0},{8,1},{9,2},{10,3},{11,4},{12,5},{13,6},{14,7},{23,8},{16,9... | collective-permute-start | bytes 393224 | tf_op jit(solution)/shard_map/ppermute | solution.py:276
  58.1 0.6 collective-permute-done.9.refs_2_
  58.7 2.8 %collective-permute-start.14 = (bf16[128,512]{1,0:T(8,128)(2,1)}, bf16[128,512]{1,0:T(8,128)(2,1)S(1)}, u32[]{:S(2)}, u32[]{:S(2)}) collective-permute-start(bf16[128,512]{1,0:T(8,128)(2,1)} %get-tuple-element.37), channel_id=1, source_target_pairs={{8,0},{9,1},{10,2},{11,3},{12,4},{13,5},{14,6},{15,7},{16,8},{17,9... | collective-permute-start | bytes 393224 | tf_op jit(solution)/shard_map/ppermute | solution.py:276
  61.5 0.8 %collective-permute-done.10.refs_3_ = bf16[128,512]{1,0:T(8,128)(2,1)S(1)} collective-permute-done((bf16[128,512]{1,0:T(8,128)(2,1)}, bf16[128,512]{1,0:T(8,128)(2,1)S(1)}, u32[]{:S(2)}, u32[]{:S(2)}) %collective-permute-start.10) | collective-permute-done | bytes 131104 | tf_op jit(solution)/shard_map/ppermute | solution.py:276
  62.3 1.6 %collective-permute-start.15 = (bf16[128,512]{1,0:T(8,128)(2,1)}, bf16[128,512]{1,0:T(8,128)(2,1)S(1)}, u32[]{:S(2)}, u32[]{:S(2)}) collective-permute-start(bf16[128,512]{1,0:T(8,128)(2,1)} %get-tuple-element.38), channel_id=1, source_target_pairs={{9,0},{10,1},{11,2},{12,3},{13,4},{14,5},{15,6},{8,7},{17,8},{18,9... | collective-permute-start | bytes 393224 | tf_op jit(solution)/shard_map/ppermute | solution.py:276
  63.9 0.0 collective-permute-done.11.refs_4_
  63.9 0.0 collective-permute-done.12.refs_5_
  63.9 0.0 copy-start.4
  63.9 0.0 collective-permute-done.13.refs_6_
  63.9 0.0 copy-start.5
  63.9 1.8 %collective-permute-done.14.refs_7_ = bf16[128,512]{1,0:T(8,128)(2,1)S(1)} collective-permute-done((bf16[128,512]{1,0:T(8,128)(2,1)}, bf16[128,512]{1,0:T(8,128)(2,1)S(1)}, u32[]{:S(2)}, u32[]{:S(2)}) %collective-permute-start.14) | collective-permute-done | bytes 131104 | tf_op jit(solution)/shard_map/ppermute | solution.py:276
  65.8 3.8 %collective-permute-done.15.refs_8_ = bf16[128,512]{1,0:T(8,128)(2,1)S(1)} collective-permute-done((bf16[128,512]{1,0:T(8,128)(2,1)}, bf16[128,512]{1,0:T(8,128)(2,1)S(1)}, u32[]{:S(2)}, u32[]{:S(2)}) %collective-permute-start.15) | collective-permute-done | bytes 131104 | tf_op jit(solution)/shard_map/ppermute | solution.py:276
  69.5 0.0 copy-done
  69.5 0.0 copy-done.1
  69.6 0.6 copy-done.7
  70.2 10.4 %shard_map.76 = bf16[64,32768]{1,0:T(8,128)(2,1)} custom-call(s32[256]{0:T(256)} %get-tuple-element.40.win_ref, s32[256]{0:T(256)} %off_ref.5, bf16[64,32768]{1,0:T(8,128)(2,1)} %bitcast.8, s32[256,128]{1,0:T(8,128)} %bitcast.12, bf16[8,64,128]{2,1,0:T(8,128)(2,1)} %bitcast.13, bf16[128,4096]{1,0:T(8,128)(2,1)} %get-tuple-element.30.refs_0_, ...), custom_call_target="tpu_custom_call" | custom-call | flops 1610612736 | bytes 10616832 | tf_op jit(solution)/shard_map/pallas_call | solution.py:304
  (18 shorter events, 0.0 us)
Async XLA Ops:
  0.0 22.7 %copy-start.8 = (s32[1,8192]{1,0:T(1,128)S(1)}, s32[1,8192]{1,0:T(1,128)}, u32[]{:S(2)}) copy-start(s32[1,8192]{1,0:T(1,128)} %param.10) | copy-start | bytes 98308
  1.9 1.3 %copy-start.17 = (s32[4]{0:T(128)}, s32[4]{0:T(128)S(1)}, u32[]{:S(2)}) copy-start(s32[4]{0:T(128)S(1)} %get-tuple-element.42.count_ref) | copy-start | bytes 52
  13.1 11.1 %collective-permute-start = (bf16[512,128]{1,0:T(8,128)(2,1)}, bf16[512,128]{1,0:T(8,128)(2,1)S(1)}, u32[]{:S(2)}, u32[]{:S(2)}) collective-permute-start(bf16[512,128]{1,0:T(8,128)(2,1)} %get-tuple-element.22), channel_id=1, source_target_pairs={{0,127},{1,120},{2,121},{3,122},{4,123},{5,124},{6,125},{7,126},{8... | collective-permute-start | bytes 393224 | tf_op jit(solution)/shard_map/ppermute | solution.py:250
  20.2 6.8 %collective-permute-start.1 = (bf16[512,128]{1,0:T(8,128)(2,1)}, bf16[512,128]{1,0:T(8,128)(2,1)S(1)}, u32[]{:S(2)}, u32[]{:S(2)}) collective-permute-start(bf16[512,128]{1,0:T(8,128)(2,1)} %get-tuple-element.23), channel_id=1, source_target_pairs={{0,120},{1,121},{2,122},{3,123},{4,124},{5,125},{6,126},{7,127},{8... | collective-permute-start | bytes 393224 | tf_op jit(solution)/shard_map/ppermute | solution.py:250
  20.2 8.4 %collective-permute-start.2 = (bf16[512,128]{1,0:T(8,128)(2,1)}, bf16[512,128]{1,0:T(8,128)(2,1)S(1)}, u32[]{:S(2)}, u32[]{:S(2)}) collective-permute-start(bf16[512,128]{1,0:T(8,128)(2,1)} %get-tuple-element.24), channel_id=1, source_target_pairs={{0,121},{1,122},{2,123},{3,124},{4,125},{5,126},{6,127},{7,120},{8... | collective-permute-start | bytes 393224 | tf_op jit(solution)/shard_map/ppermute | solution.py:250
  21.2 18.0 %collective-permute-start.3 = (bf16[512,128]{1,0:T(8,128)(2,1)}, bf16[512,128]{1,0:T(8,128)(2,1)S(1)}, u32[]{:S(2)}, u32[]{:S(2)}) collective-permute-start(bf16[512,128]{1,0:T(8,128)(2,1)} %get-tuple-element.25), channel_id=1, source_target_pairs={{0,7},{1,0},{2,1},{3,2},{4,3},{5,4},{6,5},{7,6},{8,15},{9,8},{10,9... | collective-permute-start | bytes 393224 | tf_op jit(solution)/shard_map/ppermute | solution.py:250
  22.7 16.5 %collective-permute-start.4 = (bf16[512,128]{1,0:T(8,128)(2,1)}, bf16[512,128]{1,0:T(8,128)(2,1)S(1)}, u32[]{:S(2)}, u32[]{:S(2)}) collective-permute-start(bf16[512,128]{1,0:T(8,128)(2,1)} %get-tuple-element.26), channel_id=1, source_target_pairs={{0,1},{1,2},{2,3},{3,4},{4,5},{5,6},{6,7},{7,0},{8,9},{9,10},{10,1... | collective-permute-start | bytes 393224 | tf_op jit(solution)/shard_map/ppermute | solution.py:250
  24.2 16.7 %copy-start.9 = (bf16[512,128]{1,0:T(8,128)(2,1)}, bf16[512,128]{1,0:T(8,128)(2,1)S(1)}, u32[]{:S(2)}) copy-start(bf16[512,128]{1,0:T(8,128)(2,1)S(1)} %collective-permute-done.refs_1_) | copy-start | bytes 393220
  24.2 15.0 %collective-permute-start.5 = (bf16[512,128]{1,0:T(8,128)(2,1)}, bf16[512,128]{1,0:T(8,128)(2,1)S(1)}, u32[]{:S(2)}, u32[]{:S(2)}) collective-permute-start(bf16[512,128]{1,0:T(8,128)(2,1)} %get-tuple-element.27), channel_id=1, source_target_pairs={{0,15},{1,8},{2,9},{3,10},{4,11},{5,12},{6,13},{7,14},{8,23},{9,16... | collective-permute-start | bytes 393224 | tf_op jit(solution)/shard_map/ppermute | solution.py:250
  27.0 13.9 %copy-start.10 = (bf16[512,128]{1,0:T(8,128)(2,1)}, bf16[512,128]{1,0:T(8,128)(2,1)S(1)}, u32[]{:S(2)}) copy-start(bf16[512,128]{1,0:T(8,128)(2,1)S(1)} %collective-permute-done.1.refs_2_) | copy-start | bytes 393220
  27.0 12.2 %collective-permute-start.6 = (bf16[512,128]{1,0:T(8,128)(2,1)}, bf16[512,128]{1,0:T(8,128)(2,1)S(1)}, u32[]{:S(2)}, u32[]{:S(2)}) collective-permute-start(bf16[512,128]{1,0:T(8,128)(2,1)} %get-tuple-element.28), channel_id=1, source_target_pairs={{0,8},{1,9},{2,10},{3,11},{4,12},{5,13},{6,14},{7,15},{8,16},{9,17... | collective-permute-start | bytes 393224 | tf_op jit(solution)/shard_map/ppermute | solution.py:250
  28.6 12.2 %copy-start.11 = (bf16[512,128]{1,0:T(8,128)(2,1)}, bf16[512,128]{1,0:T(8,128)(2,1)S(1)}, u32[]{:S(2)}) copy-start(bf16[512,128]{1,0:T(8,128)(2,1)S(1)} %collective-permute-done.2.refs_3_) | copy-start | bytes 393220
  28.6 12.2 %collective-permute-start.7 = (bf16[512,128]{1,0:T(8,128)(2,1)}, bf16[512,128]{1,0:T(8,128)(2,1)S(1)}, u32[]{:S(2)}, u32[]{:S(2)}) collective-permute-start(bf16[512,128]{1,0:T(8,128)(2,1)} %get-tuple-element.29), channel_id=1, source_target_pairs={{0,9},{1,10},{2,11},{3,12},{4,13},{5,14},{6,15},{7,8},{8,17},{9,18... | collective-permute-start | bytes 393224 | tf_op jit(solution)/shard_map/ppermute | solution.py:250
  39.2 1.7 %copy-start.12 = (bf16[512,128]{1,0:T(8,128)(2,1)}, bf16[512,128]{1,0:T(8,128)(2,1)S(1)}, u32[]{:S(2)}) copy-start(bf16[512,128]{1,0:T(8,128)(2,1)S(1)} %collective-permute-done.3.refs_4_) | copy-start | bytes 393220
  39.2 1.7 %copy-start.13 = (bf16[512,128]{1,0:T(8,128)(2,1)}, bf16[512,128]{1,0:T(8,128)(2,1)S(1)}, u32[]{:S(2)}) copy-start(bf16[512,128]{1,0:T(8,128)(2,1)S(1)} %collective-permute-done.4.refs_5_) | copy-start | bytes 393220
  39.2 1.7 %copy-start.14 = (bf16[512,128]{1,0:T(8,128)(2,1)}, bf16[512,128]{1,0:T(8,128)(2,1)S(1)}, u32[]{:S(2)}) copy-start(bf16[512,128]{1,0:T(8,128)(2,1)S(1)} %collective-permute-done.5.refs_6_) | copy-start | bytes 393220
  39.2 1.7 %copy-start.15 = (bf16[512,128]{1,0:T(8,128)(2,1)}, bf16[512,128]{1,0:T(8,128)(2,1)S(1)}, u32[]{:S(2)}) copy-start(bf16[512,128]{1,0:T(8,128)(2,1)S(1)} %collective-permute-done.6.refs_7_) | copy-start | bytes 393220
  40.8 0.6 copy-start.16
  46.8 10.3 %collective-permute-start.8 = (bf16[128,512]{1,0:T(8,128)(2,1)}, bf16[128,512]{1,0:T(8,128)(2,1)S(1)}, u32[]{:S(2)}, u32[]{:S(2)}) collective-permute-start(bf16[128,512]{1,0:T(8,128)(2,1)} %get-tuple-element.31), channel_id=1, source_target_pairs={{127,0},{120,1},{121,2},{122,3},{123,4},{124,5},{125,6},{126,7},{7... | collective-permute-start | bytes 393224 | tf_op jit(solution)/shard_map/ppermute | solution.py:276
  46.8 11.9 %collective-permute-start.9 = (bf16[128,512]{1,0:T(8,128)(2,1)}, bf16[128,512]{1,0:T(8,128)(2,1)S(1)}, u32[]{:S(2)}, u32[]{:S(2)}) collective-permute-start(bf16[128,512]{1,0:T(8,128)(2,1)} %get-tuple-element.32), channel_id=1, source_target_pairs={{120,0},{121,1},{122,2},{123,3},{124,4},{125,5},{126,6},{127,7},{0... | collective-permute-start | bytes 393224 | tf_op jit(solution)/shard_map/ppermute | solution.py:276
  50.7 11.7 %collective-permute-start.10 = (bf16[128,512]{1,0:T(8,128)(2,1)}, bf16[128,512]{1,0:T(8,128)(2,1)S(1)}, u32[]{:S(2)}, u32[]{:S(2)}) collective-permute-start(bf16[128,512]{1,0:T(8,128)(2,1)} %get-tuple-element.33), channel_id=1, source_target_pairs={{121,0},{122,1},{123,2},{124,3},{125,4},{126,5},{127,6},{120,7},{1... | collective-permute-start | bytes 393224 | tf_op jit(solution)/shard_map/ppermute | solution.py:276
  50.7 13.2 %collective-permute-start.11 = (bf16[128,512]{1,0:T(8,128)(2,1)}, bf16[128,512]{1,0:T(8,128)(2,1)S(1)}, u32[]{:S(2)}, u32[]{:S(2)}) collective-permute-start(bf16[128,512]{1,0:T(8,128)(2,1)} %get-tuple-element.34), channel_id=1, source_target_pairs={{7,0},{0,1},{1,2},{2,3},{3,4},{4,5},{5,6},{6,7},{15,8},{8,9},{9,10... | collective-permute-start | bytes 393224 | tf_op jit(solution)/shard_map/ppermute | solution.py:276
  50.8 13.1 %collective-permute-start.12 = (bf16[128,512]{1,0:T(8,128)(2,1)}, bf16[128,512]{1,0:T(8,128)(2,1)S(1)}, u32[]{:S(2)}, u32[]{:S(2)}) collective-permute-start(bf16[128,512]{1,0:T(8,128)(2,1)} %get-tuple-element.35), channel_id=1, source_target_pairs={{1,0},{2,1},{3,2},{4,3},{5,4},{6,5},{7,6},{0,7},{9,8},{10,9},{11,1... | collective-permute-start | bytes 393224 | tf_op jit(solution)/shard_map/ppermute | solution.py:276
  57.1 12.4 %copy-start = (bf16[128,512]{1,0:T(8,128)(2,1)}, bf16[128,512]{1,0:T(8,128)(2,1)S(1)}, u32[]{:S(2)}) copy-start(bf16[128,512]{1,0:T(8,128)(2,1)S(1)} %collective-permute-done.8.refs_1_) | copy-start | bytes 393220
  57.1 6.8 %collective-permute-start.13 = (bf16[128,512]{1,0:T(8,128)(2,1)}, bf16[128,512]{1,0:T(8,128)(2,1)S(1)}, u32[]{:S(2)}, u32[]{:S(2)}) collective-permute-start(bf16[128,512]{1,0:T(8,128)(2,1)} %get-tuple-element.36), channel_id=1, source_target_pairs={{15,0},{8,1},{9,2},{10,3},{11,4},{12,5},{13,6},{14,7},{23,8},{16,9... | collective-permute-start | bytes 393224 | tf_op jit(solution)/shard_map/ppermute | solution.py:276
  58.7 10.8 %copy-start.1 = (bf16[128,512]{1,0:T(8,128)(2,1)}, bf16[128,512]{1,0:T(8,128)(2,1)S(1)}, u32[]{:S(2)}) copy-start(bf16[128,512]{1,0:T(8,128)(2,1)S(1)} %collective-permute-done.9.refs_2_) | copy-start | bytes 393220
  58.7 7.0 %collective-permute-start.14 = (bf16[128,512]{1,0:T(8,128)(2,1)}, bf16[128,512]{1,0:T(8,128)(2,1)S(1)}, u32[]{:S(2)}, u32[]{:S(2)}) collective-permute-start(bf16[128,512]{1,0:T(8,128)(2,1)} %get-tuple-element.37), channel_id=1, source_target_pairs={{8,0},{9,1},{10,2},{11,3},{12,4},{13,5},{14,6},{15,7},{16,8},{17,9... | collective-permute-start | bytes 393224 | tf_op jit(solution)/shard_map/ppermute | solution.py:276
  62.3 7.2 %copy-start.2 = (bf16[128,512]{1,0:T(8,128)(2,1)}, bf16[128,512]{1,0:T(8,128)(2,1)S(1)}, u32[]{:S(2)}) copy-start(bf16[128,512]{1,0:T(8,128)(2,1)S(1)} %collective-permute-done.10.refs_3_) | copy-start | bytes 393220
  62.3 7.2 %collective-permute-start.15 = (bf16[128,512]{1,0:T(8,128)(2,1)}, bf16[128,512]{1,0:T(8,128)(2,1)S(1)}, u32[]{:S(2)}, u32[]{:S(2)}) collective-permute-start(bf16[128,512]{1,0:T(8,128)(2,1)} %get-tuple-element.38), channel_id=1, source_target_pairs={{9,0},{10,1},{11,2},{12,3},{13,4},{14,5},{15,6},{8,7},{17,8},{18,9... | collective-permute-start | bytes 393224 | tf_op jit(solution)/shard_map/ppermute | solution.py:276
  63.9 5.6 %copy-start.3 = (bf16[128,512]{1,0:T(8,128)(2,1)}, bf16[128,512]{1,0:T(8,128)(2,1)S(1)}, u32[]{:S(2)}) copy-start(bf16[128,512]{1,0:T(8,128)(2,1)S(1)} %collective-permute-done.11.refs_4_) | copy-start | bytes 393220
  63.9 5.6 %copy-start.4 = (bf16[128,512]{1,0:T(8,128)(2,1)}, bf16[128,512]{1,0:T(8,128)(2,1)S(1)}, u32[]{:S(2)}) copy-start(bf16[128,512]{1,0:T(8,128)(2,1)S(1)} %collective-permute-done.12.refs_5_) | copy-start | bytes 393220
  63.9 5.6 %copy-start.5 = (bf16[128,512]{1,0:T(8,128)(2,1)}, bf16[128,512]{1,0:T(8,128)(2,1)S(1)}, u32[]{:S(2)}) copy-start(bf16[128,512]{1,0:T(8,128)(2,1)S(1)} %collective-permute-done.13.refs_6_) | copy-start | bytes 393220
  65.8 3.8 %copy-start.6 = (bf16[128,512]{1,0:T(8,128)(2,1)}, bf16[128,512]{1,0:T(8,128)(2,1)S(1)}, u32[]{:S(2)}) copy-start(bf16[128,512]{1,0:T(8,128)(2,1)S(1)} %collective-permute-done.14.refs_7_) | copy-start | bytes 393220
  69.5 0.7 copy-start.7
